TPU v7x, 256 devices: a whole 4x4x8 slice. The times are simulated.
256 devices in a mesh: tf: 4 (over x), gz: 8 (over z), sec: 8 (over y, core).
Axes of the slice: x: 4, y: 4, z: 8, core: 2. Of those that a mesh axis runs over, the one named last changes fastest.
Arguments:
- residuals: bfloat16 [3, 4, 8, 8, 4, 8192], P(None, 'tf', 'gz', 'sec'), may hold values from -6 to 6
- weights: bfloat16 [4, 8, 8, 4, 8192], P('tf', 'gz', 'sec'), may hold values from 0.5 to 2
- fraction: bfloat16 [4, 8, 8, 4, 8192], P('tf', 'gz', 'sec'), may hold values from 0 to 1
- voxels: int32 [3, 4, 8, 8, 4, 8192], P(None, 'tf', 'gz', 'sec'), may hold values from 0 to 255, as said below
- kernel_reach: int32 [152], P('sec'), may hold values from 1 to 4
Outputs:
- distortion: float32 [3, 256, 152, 180], P(None, ('tf', 'gz'), 'sec')
Inputs may be any that keep to these rules, and one draw needn't show every extreme that they name: `voxels`: component 0 is the pad row, 1 the pad bin, 2 the drift bin. A residual at sec index s has its row in s * 19 to s * 19 + 18; its pad bin is at most 178; a residual at gz index g in slot t of the fifth dimension has its drift bin in block t * (number of gz devices) + g, that is among the 8 bins from (t * (number of gz devices) + g) * 8 on.
All inputs are finite; a program needn't handle non-finite values.
Results may differ from a plain program's by a relative error of at most 0.0026.
Values may be sent and summed in bfloat16 or wider, within the bound.
No kernel may reach another device: no remote copies, remote signals or barrier semaphores. Data moves between devices by JAX's collectives and lax.ppermute only.
A program may use at most 64 MiB of HBM per device.

v0:
```python
import jax
import jax.numpy as jnp
from jax import lax
from jax.sharding import PartitionSpec as P

PAD = 180
DRIFT = 256


def entering(x, axis, combine, identity):
    devices, here = (lax.axis_size(axis), lax.axis_index(axis))
    everything = lax.all_gather(x, axis)
    start = jnp.broadcast_to(jnp.asarray(identity, x.dtype), x.shape)

    def hop(k, before):
        reached = k < here
        new = combine(before, everything[k])
        return jnp.where(reached, new, before)

    return lax.fori_loop(0, devices, hop, start)


def with_halo(block, sides, width):
    for axis, dim in sides:
        count = lax.axis_size(axis)
        forward = [(i, i + 1) for i in range(count - 1)]
        backward = [(target, source) for source, target in forward]
        low = lax.ppermute(
            lax.slice_in_dim(block, block.shape[dim] - width, None, axis=dim), axis, forward
        )
        high = lax.ppermute(lax.slice_in_dim(block, 0, width, axis=dim), axis, backward)
        block = jnp.concatenate([low, block, high], axis=dim)
    return block


def row_kernels(kernel_reach):
    spread = kernel_reach.astype(jnp.float32)[:, None, None]
    places = lax.broadcasted_iota(jnp.int32, (PAD, PAD), 0)
    others = lax.broadcasted_iota(jnp.int32, (PAD, PAD), 1)
    distance = jnp.abs(places - others).astype(jnp.float32)[None]
    return jnp.maximum(spread + 1.0 - distance, 0.0) / ((spread + 1.0) * (spread + 1.0))


def fill_slots(packed, floats, cell_count):
    blocks = packed.shape[0]
    slot_count = packed.shape[1]
    block_len = min(512, slot_count)
    pad_iota = lax.broadcasted_iota(jnp.int32, (1, 1, 1, PAD), 3)
    cell_iota = lax.broadcasted_iota(jnp.int32, (1, 1, cell_count), 2)
    nothing = jnp.zeros((), jnp.bfloat16)

    def advance(number, summed):
        index_part = lax.dynamic_slice_in_dim(packed, number * block_len, block_len, 1)
        value_part = lax.dynamic_slice_in_dim(floats, number * block_len, block_len, 2).astype(
            jnp.float32
        )
        cell_ids = index_part // PAD
        pad_ids = index_part - cell_ids * PAD
        weight_now = value_part[:, 3]
        left_share = weight_now * (1.0 - value_part[:, 4])
        right_share = weight_now * value_part[:, 4]
        left_chan = jnp.stack(
            [
                left_share,
                left_share * value_part[:, 0],
                left_share * value_part[:, 1],
                left_share * value_part[:, 2],
            ],
            2,
        ).astype(jnp.bfloat16)
        right_chan = jnp.stack(
            [
                right_share,
                right_share * value_part[:, 0],
                right_share * value_part[:, 1],
                right_share * value_part[:, 2],
            ],
            2,
        ).astype(jnp.bfloat16)
        at_left = pad_iota == pad_ids[:, :, None, None]
        at_right = pad_iota == pad_ids[:, :, None, None] + 1
        deposit = jnp.where(at_left, left_chan[..., None], nothing) + jnp.where(
            at_right, right_chan[..., None], nothing
        )
        deposit = deposit.reshape(blocks, block_len, 4 * PAD)
        onehot = (cell_iota == cell_ids[:, :, None]).astype(jnp.bfloat16)
        return summed + jnp.einsum(
            "tnk,tnc->tkc", onehot, deposit, preferred_element_type=jnp.float32
        )

    initial = jnp.zeros((blocks, cell_count, 4 * PAD), jnp.float32)
    return lax.fori_loop(0, slot_count // block_len, advance, initial)


def add_terms(earlier, later):
    return earlier + later


def accumulate(field):
    totals = jnp.sum(field, axis=1)
    carried = entering(totals, ("tf", "gz"), add_terms, jnp.zeros_like(totals))
    return carried[:, None] + jnp.cumsum(field, axis=1)


def smooth(field, kernel_reach):
    across = jnp.einsum(
        "kzrq,rpq->kzrp", field, row_kernels(kernel_reach), precision=lax.Precision.HIGHEST
    )
    rimmed = with_halo(across, (("sec", 2),), 2)
    row_total = across.shape[2]
    return (
        rimmed[:, :, 0:row_total]
        + 2.0 * rimmed[:, :, 1 : row_total + 1]
        + 3.0 * rimmed[:, :, 2 : row_total + 2]
        + 2.0 * rimmed[:, :, 3 : row_total + 3]
        + rimmed[:, :, 4 : row_total + 4]
    ) / 9.0


def per_device(residuals, weights, fraction, voxels, kernel_reach):
    gz_count = lax.axis_size("gz")
    drift_dev = DRIFT // (lax.axis_size("tf") * gz_count)
    row_dev = kernel_reach.shape[0]
    cell_count = drift_dev * row_dev
    coords = voxels[:, 0, 0, 0]
    target = lax.broadcasted_iota(jnp.int32, coords.shape[1:], 0)
    local_row = coords[0] - lax.axis_index("sec") * row_dev
    local_drift = coords[2] - (target * gz_count + lax.axis_index("gz")) * drift_dev
    packed = (local_drift * row_dev + local_row) * PAD + coords[1]
    floats = jnp.concatenate(
        [residuals[:, 0, 0, 0], weights[0, 0, 0][None], fraction[0, 0, 0][None]], 0
    )
    floats = jnp.transpose(floats, (1, 0, 2))
    block_count = drift_dev * lax.axis_size("tf") // drift_dev
    partial_sum = fill_slots(packed, floats, cell_count)
    histogram = lax.psum_scatter(
        partial_sum.reshape(block_count * drift_dev, row_dev, 4 * PAD),
        "tf",
        scatter_dimension=0,
        tiled=True,
    )
    histogram = histogram.reshape(drift_dev, row_dev, 4, PAD)
    means = histogram[:, :, 1:4] / (histogram[:, :, 0:1] + 1.0)
    means = jnp.transpose(means, (2, 0, 1, 3))
    result = accumulate(smooth(means, kernel_reach))
    return result


def solution(mesh):
    placed = (
        P(None, "tf", "gz", "sec", None, None),
        P("tf", "gz", "sec", None, None),
        P("tf", "gz", "sec", None, None),
        P(None, "tf", "gz", "sec", None, None),
        P("sec"),
    )
    return jax.shard_map(
        per_device,
        mesh=mesh,
        in_specs=placed,
        out_specs=P(None, ("tf", "gz"), "sec", None),
        check_vma=False,
    )
```

profile of v0, /device:TPU:8, one launch (start us, length us, event | category | flops | bytes accessed | tf_op | source)
XLA Modules:
  0.0 318.1 jit_solution(12109582473676356937)
XLA Ops:
  11.1 136.2 %while.32 = (s32[]{:T(128)}, f32[4,152,720]{2,1,0:T(8,128)}, s32[4,8192]{1,0:T(4,128)S(1)}, bf16[4,5,8192]{2,1,0:T(8,128)(2,1)S(1)}, s32[]{:T(128)}, /*index=5*/s32[]{:T(128)}, s32[]{:T(128)}, s32[]{:T(128)}) while((s32[]{:T(128)}, f32[4,152,720]{2,1,0:T(8,128)}, s32[4,8192]{1,0:T(4,128)S(1)}, ...), condition=%wide.region_1.2_spmd.clone.clone, body=%wide.region_0.1_spmd.clone.clone.sunk | while | flops 454812672 | bytes 18145484 | solution.py:92
  12.7 2.3 add.232
  15.0 4.2 %select_add_fusion.5 = f32[4,152,720]{2,1,0:T(8,128)} fusion(f32[4,152,720]{2,1,0:T(8,128)} %get-tuple-element.431, bf16[4,512,720]{1,2,0:T(8,128)(2,1)} %add.232, pred[]{:T(512)S(6)} %compare.7, s32[4,512]{1,0:T(4,128)S(1)} %get-tuple-element.421), kind=kOutput, calls=%fused_computation.6.clone.1 | convolution fusion | flops 449453056 | bytes 6459393 | tf_op jit(solution)/shard_map/while/body/eval_jaxpr/tnk,tnc->tkc/dot_general | solution.py:87
  23.0 4.7 %select_add_fusion.5 = f32[4,152,720]{2,1,0:T(8,128)} fusion(f32[4,152,720]{2,1,0:T(8,128)} %get-tuple-element.431, bf16[4,512,720]{1,2,0:T(8,128)(2,1)} %add.232, pred[]{:T(512)S(6)} %compare.7, s32[4,512]{1,0:T(4,128)S(1)} %get-tuple-element.421), kind=kOutput, calls=%fused_computation.6.clone.1 | convolution fusion | flops 449453056 | bytes 6459393 | tf_op jit(solution)/shard_map/while/body/eval_jaxpr/tnk,tnc->tkc/dot_general | solution.py:87
  31.5 4.7 %select_add_fusion.5 = f32[4,152,720]{2,1,0:T(8,128)} fusion(f32[4,152,720]{2,1,0:T(8,128)} %get-tuple-element.431, bf16[4,512,720]{1,2,0:T(8,128)(2,1)} %add.232, pred[]{:T(512)S(6)} %compare.7, s32[4,512]{1,0:T(4,128)S(1)} %get-tuple-element.421), kind=kOutput, calls=%fused_computation.6.clone.1 | convolution fusion | flops 449453056 | bytes 6459393 | tf_op jit(solution)/shard_map/while/body/eval_jaxpr/tnk,tnc->tkc/dot_general | solution.py:87
  40.0 4.7 %select_add_fusion.5 = f32[4,152,720]{2,1,0:T(8,128)} fusion(f32[4,152,720]{2,1,0:T(8,128)} %get-tuple-element.431, bf16[4,512,720]{1,2,0:T(8,128)(2,1)} %add.232, pred[]{:T(512)S(6)} %compare.7, s32[4,512]{1,0:T(4,128)S(1)} %get-tuple-element.421), kind=kOutput, calls=%fused_computation.6.clone.1 | convolution fusion | flops 449453056 | bytes 6459393 | tf_op jit(solution)/shard_map/while/body/eval_jaxpr/tnk,tnc->tkc/dot_general | solution.py:87
  48.6 4.7 %select_add_fusion.5 = f32[4,152,720]{2,1,0:T(8,128)} fusion(f32[4,152,720]{2,1,0:T(8,128)} %get-tuple-element.431, bf16[4,512,720]{1,2,0:T(8,128)(2,1)} %add.232, pred[]{:T(512)S(6)} %compare.7, s32[4,512]{1,0:T(4,128)S(1)} %get-tuple-element.421), kind=kOutput, calls=%fused_computation.6.clone.1 | convolution fusion | flops 449453056 | bytes 6459393 | tf_op jit(solution)/shard_map/while/body/eval_jaxpr/tnk,tnc->tkc/dot_general | solution.py:87
  57.1 4.7 %select_add_fusion.5 = f32[4,152,720]{2,1,0:T(8,128)} fusion(f32[4,152,720]{2,1,0:T(8,128)} %get-tuple-element.431, bf16[4,512,720]{1,2,0:T(8,128)(2,1)} %add.232, pred[]{:T(512)S(6)} %compare.7, s32[4,512]{1,0:T(4,128)S(1)} %get-tuple-element.421), kind=kOutput, calls=%fused_computation.6.clone.1 | convolution fusion | flops 449453056 | bytes 6459393 | tf_op jit(solution)/shard_map/while/body/eval_jaxpr/tnk,tnc->tkc/dot_general | solution.py:87
  65.7 4.7 %select_add_fusion.5 = f32[4,152,720]{2,1,0:T(8,128)} fusion(f32[4,152,720]{2,1,0:T(8,128)} %get-tuple-element.431, bf16[4,512,720]{1,2,0:T(8,128)(2,1)} %add.232, pred[]{:T(512)S(6)} %compare.7, s32[4,512]{1,0:T(4,128)S(1)} %get-tuple-element.421), kind=kOutput, calls=%fused_computation.6.clone.1 | convolution fusion | flops 449453056 | bytes 6459393 | tf_op jit(solution)/shard_map/while/body/eval_jaxpr/tnk,tnc->tkc/dot_general | solution.py:87
  74.2 4.7 %select_add_fusion.5 = f32[4,152,720]{2,1,0:T(8,128)} fusion(f32[4,152,720]{2,1,0:T(8,128)} %get-tuple-element.431, bf16[4,512,720]{1,2,0:T(8,128)(2,1)} %add.232, pred[]{:T(512)S(6)} %compare.7, s32[4,512]{1,0:T(4,128)S(1)} %get-tuple-element.421), kind=kOutput, calls=%fused_computation.6.clone.1 | convolution fusion | flops 449453056 | bytes 6459393 | tf_op jit(solution)/shard_map/while/body/eval_jaxpr/tnk,tnc->tkc/dot_general | solution.py:87
  82.8 4.7 %select_add_fusion.5 = f32[4,152,720]{2,1,0:T(8,128)} fusion(f32[4,152,720]{2,1,0:T(8,128)} %get-tuple-element.431, bf16[4,512,720]{1,2,0:T(8,128)(2,1)} %add.232, pred[]{:T(512)S(6)} %compare.7, s32[4,512]{1,0:T(4,128)S(1)} %get-tuple-element.421), kind=kOutput, calls=%fused_computation.6.clone.1 | convolution fusion | flops 449453056 | bytes 6459393 | tf_op jit(solution)/shard_map/while/body/eval_jaxpr/tnk,tnc->tkc/dot_general | solution.py:87
  91.3 4.7 %select_add_fusion.5 = f32[4,152,720]{2,1,0:T(8,128)} fusion(f32[4,152,720]{2,1,0:T(8,128)} %get-tuple-element.431, bf16[4,512,720]{1,2,0:T(8,128)(2,1)} %add.232, pred[]{:T(512)S(6)} %compare.7, s32[4,512]{1,0:T(4,128)S(1)} %get-tuple-element.421), kind=kOutput, calls=%fused_computation.6.clone.1 | convolution fusion | flops 449453056 | bytes 6459393 | tf_op jit(solution)/shard_map/while/body/eval_jaxpr/tnk,tnc->tkc/dot_general | solution.py:87
  99.8 4.7 %select_add_fusion.5 = f32[4,152,720]{2,1,0:T(8,128)} fusion(f32[4,152,720]{2,1,0:T(8,128)} %get-tuple-element.431, bf16[4,512,720]{1,2,0:T(8,128)(2,1)} %add.232, pred[]{:T(512)S(6)} %compare.7, s32[4,512]{1,0:T(4,128)S(1)} %get-tuple-element.421), kind=kOutput, calls=%fused_computation.6.clone.1 | convolution fusion | flops 449453056 | bytes 6459393 | tf_op jit(solution)/shard_map/while/body/eval_jaxpr/tnk,tnc->tkc/dot_general | solution.py:87
  108.4 4.7 %select_add_fusion.5 = f32[4,152,720]{2,1,0:T(8,128)} fusion(f32[4,152,720]{2,1,0:T(8,128)} %get-tuple-element.431, bf16[4,512,720]{1,2,0:T(8,128)(2,1)} %add.232, pred[]{:T(512)S(6)} %compare.7, s32[4,512]{1,0:T(4,128)S(1)} %get-tuple-element.421), kind=kOutput, calls=%fused_computation.6.clone.1 | convolution fusion | flops 449453056 | bytes 6459393 | tf_op jit(solution)/shard_map/while/body/eval_jaxpr/tnk,tnc->tkc/dot_general | solution.py:87
  116.9 4.7 %select_add_fusion.5 = f32[4,152,720]{2,1,0:T(8,128)} fusion(f32[4,152,720]{2,1,0:T(8,128)} %get-tuple-element.431, bf16[4,512,720]{1,2,0:T(8,128)(2,1)} %add.232, pred[]{:T(512)S(6)} %compare.7, s32[4,512]{1,0:T(4,128)S(1)} %get-tuple-element.421), kind=kOutput, calls=%fused_computation.6.clone.1 | convolution fusion | flops 449453056 | bytes 6459393 | tf_op jit(solution)/shard_map/while/body/eval_jaxpr/tnk,tnc->tkc/dot_general | solution.py:87
  125.5 4.7 %select_add_fusion.5 = f32[4,152,720]{2,1,0:T(8,128)} fusion(f32[4,152,720]{2,1,0:T(8,128)} %get-tuple-element.431, bf16[4,512,720]{1,2,0:T(8,128)(2,1)} %add.232, pred[]{:T(512)S(6)} %compare.7, s32[4,512]{1,0:T(4,128)S(1)} %get-tuple-element.421), kind=kOutput, calls=%fused_computation.6.clone.1 | convolution fusion | flops 449453056 | bytes 6459393 | tf_op jit(solution)/shard_map/while/body/eval_jaxpr/tnk,tnc->tkc/dot_general | solution.py:87
  134.0 4.7 %select_add_fusion.5 = f32[4,152,720]{2,1,0:T(8,128)} fusion(f32[4,152,720]{2,1,0:T(8,128)} %get-tuple-element.431, bf16[4,512,720]{1,2,0:T(8,128)(2,1)} %add.232, pred[]{:T(512)S(6)} %compare.7, s32[4,512]{1,0:T(4,128)S(1)} %get-tuple-element.421), kind=kOutput, calls=%fused_computation.6.clone.1 | convolution fusion | flops 449453056 | bytes 6459393 | tf_op jit(solution)/shard_map/while/body/eval_jaxpr/tnk,tnc->tkc/dot_general | solution.py:87
  142.6 4.7 %select_add_fusion.5 = f32[4,152,720]{2,1,0:T(8,128)} fusion(f32[4,152,720]{2,1,0:T(8,128)} %get-tuple-element.431, bf16[4,512,720]{1,2,0:T(8,128)(2,1)} %add.232, pred[]{:T(512)S(6)} %compare.7, s32[4,512]{1,0:T(4,128)S(1)} %get-tuple-element.421), kind=kOutput, calls=%fused_computation.6.clone.1 | convolution fusion | flops 449453056 | bytes 6459393 | tf_op jit(solution)/shard_map/while/body/eval_jaxpr/tnk,tnc->tkc/dot_general | solution.py:87
  147.3 2.7 reshape.444
  150.2 37.3 %reduce-scatter.2.cloned.1.call-done = f32[8,19,720]{2,1,0:T(8,128)} async-done(((f32[32,19,720]{2,1,0:T(8,128)}), f32[8,19,720]{2,1,0:T(8,128)}) %reduce-scatter.2.cloned.1.call-update) | async-done | bytes 437776 | tf_op jit(solution)/shard_map/reduce_scatter | solution.py:136
  189.6 3.6 %fusion.12 = f32[3,8,19,180]{3,1,0,2:T(8,128)S(1)} fusion(f32[19]{0:T(128)S(1)} %get-tuple-element.337, f32[180,180]{1,0:T(8,128)S(1)} %abs_convert_fusion, f32[19]{0:T(128)S(1)} %get-tuple-element.336, f32[3,8,19,180]{3,0,1,2:T(4,128)S(1)} %fusion.13), kind=kOutput, calls=%fused_computation.37 | convolution fusion | flops 179139600 | bytes 786392
  195.2 3.6 %collective-permute-start.1 = (f32[3,8,2,180]{3,1,0,2:T(8,128)S(1)}, f32[3,8,2,180]{3,1,0,2:T(8,128)S(1)}, u32[]{:S(2)}, u32[]{:S(2)}) collective-permute-start(f32[3,8,2,180]{3,1,0,2:T(8,128)S(1)} %get-tuple-element.335), channel_id=1, source_target_pairs={{1,0},{2,1},{3,2},{4,3},{5,4},{6,5},{7,6},{9,8},{10,9},{11,10},{12... | collective-permute-start | bytes 103688 | tf_op jit(solution)/shard_map/ppermute | solution.py:31
  201.9 78.6 %all-gather.3.cloned.1.call-done = f32[96,19,180]{2,1,0:T(8,128)} async-done(((f32[3,19,180]{2,1,0:T(8,128)}), f32[96,19,180]{2,1,0:T(8,128)}) %all-gather.3.cloned.1.call-update) | async-done | bytes 1313296 | tf_op jit(solution)/shard_map/all_gather | solution.py:12
  280.5 29.8 %while.31 = (s32[]{:T(128)}, f32[3,19,180]{2,1,0:T(8,128)S(1)}, s32[]{:T(128)}, f32[32,3,19,180]{3,2,1,0:T(8,128)}, s32[]{:T(128)}, /*index=5*/s32[]{:T(128)}) while((s32[]{:T(128)}, f32[3,19,180]{2,1,0:T(8,128)S(1)}, s32[]{:T(128)}, f32[32,3,19,180]{3,2,1,0:T(8,128)}, s32[]{:T(128)}, /*index=5*/s32[]{:T(128)}) %tuple.108), condition=%wide.region_5.6_spmd.clone, body=%wide.region_4.5_spmd.clone.sunk | while | flops 30784 | bytes 123213 | solution.py:20
  (254 shorter events, 99.8 us)
Async XLA Ops:
  6.5 180.9 %reduce-scatter.2.cloned.1.call-start = ((), (), s32[]{:S(2)}) async-start(), calls=%async_computation.1 | async-start | bytes 2949120 | tf_op jit(solution)/shard_map/reduce_scatter | solution.py:136
  11.1 0.7 copy-start
  15.0 4.2 %copy-start.1 = (s32[4,8192]{1,0:T(4,128)S(1)}, s32[4,8192]{1,0:T(4,128)}, u32[]{:S(2)}) copy-start(s32[4,8192]{1,0:T(4,128)} %copy-done) | copy-start | bytes 393220 | tf_op jit(solution)/shard_map/while
  23.0 4.7 %copy-start.1 = (s32[4,8192]{1,0:T(4,128)S(1)}, s32[4,8192]{1,0:T(4,128)}, u32[]{:S(2)}) copy-start(s32[4,8192]{1,0:T(4,128)} %copy-done) | copy-start | bytes 393220 | tf_op jit(solution)/shard_map/while
  31.5 4.7 %copy-start.1 = (s32[4,8192]{1,0:T(4,128)S(1)}, s32[4,8192]{1,0:T(4,128)}, u32[]{:S(2)}) copy-start(s32[4,8192]{1,0:T(4,128)} %copy-done) | copy-start | bytes 393220 | tf_op jit(solution)/shard_map/while
  36.2 0.7 copy-start
  40.0 4.7 %copy-start.1 = (s32[4,8192]{1,0:T(4,128)S(1)}, s32[4,8192]{1,0:T(4,128)}, u32[]{:S(2)}) copy-start(s32[4,8192]{1,0:T(4,128)} %copy-done) | copy-start | bytes 393220 | tf_op jit(solution)/shard_map/while
  48.6 4.7 %copy-start.1 = (s32[4,8192]{1,0:T(4,128)S(1)}, s32[4,8192]{1,0:T(4,128)}, u32[]{:S(2)}) copy-start(s32[4,8192]{1,0:T(4,128)} %copy-done) | copy-start | bytes 393220 | tf_op jit(solution)/shard_map/while
  57.1 4.7 %copy-start.1 = (s32[4,8192]{1,0:T(4,128)S(1)}, s32[4,8192]{1,0:T(4,128)}, u32[]{:S(2)}) copy-start(s32[4,8192]{1,0:T(4,128)} %copy-done) | copy-start | bytes 393220 | tf_op jit(solution)/shard_map/while
  65.7 4.7 %copy-start.1 = (s32[4,8192]{1,0:T(4,128)S(1)}, s32[4,8192]{1,0:T(4,128)}, u32[]{:S(2)}) copy-start(s32[4,8192]{1,0:T(4,128)} %copy-done) | copy-start | bytes 393220 | tf_op jit(solution)/shard_map/while
  74.2 4.7 %copy-start.1 = (s32[4,8192]{1,0:T(4,128)S(1)}, s32[4,8192]{1,0:T(4,128)}, u32[]{:S(2)}) copy-start(s32[4,8192]{1,0:T(4,128)} %copy-done) | copy-start | bytes 393220 | tf_op jit(solution)/shard_map/while
  82.8 4.7 %copy-start.1 = (s32[4,8192]{1,0:T(4,128)S(1)}, s32[4,8192]{1,0:T(4,128)}, u32[]{:S(2)}) copy-start(s32[4,8192]{1,0:T(4,128)} %copy-done) | copy-start | bytes 393220 | tf_op jit(solution)/shard_map/while
  91.3 4.7 %copy-start.1 = (s32[4,8192]{1,0:T(4,128)S(1)}, s32[4,8192]{1,0:T(4,128)}, u32[]{:S(2)}) copy-start(s32[4,8192]{1,0:T(4,128)} %copy-done) | copy-start | bytes 393220 | tf_op jit(solution)/shard_map/while
  99.8 4.7 %copy-start.1 = (s32[4,8192]{1,0:T(4,128)S(1)}, s32[4,8192]{1,0:T(4,128)}, u32[]{:S(2)}) copy-start(s32[4,8192]{1,0:T(4,128)} %copy-done) | copy-start | bytes 393220 | tf_op jit(solution)/shard_map/while
  108.4 4.7 %copy-start.1 = (s32[4,8192]{1,0:T(4,128)S(1)}, s32[4,8192]{1,0:T(4,128)}, u32[]{:S(2)}) copy-start(s32[4,8192]{1,0:T(4,128)} %copy-done) | copy-start | bytes 393220 | tf_op jit(solution)/shard_map/while
  113.1 0.7 copy-start
  116.9 4.7 %copy-start.1 = (s32[4,8192]{1,0:T(4,128)S(1)}, s32[4,8192]{1,0:T(4,128)}, u32[]{:S(2)}) copy-start(s32[4,8192]{1,0:T(4,128)} %copy-done) | copy-start | bytes 393220 | tf_op jit(solution)/shard_map/while
  125.5 4.7 %copy-start.1 = (s32[4,8192]{1,0:T(4,128)S(1)}, s32[4,8192]{1,0:T(4,128)}, u32[]{:S(2)}) copy-start(s32[4,8192]{1,0:T(4,128)} %copy-done) | copy-start | bytes 393220 | tf_op jit(solution)/shard_map/while
  134.0 4.7 %copy-start.1 = (s32[4,8192]{1,0:T(4,128)S(1)}, s32[4,8192]{1,0:T(4,128)}, u32[]{:S(2)}) copy-start(s32[4,8192]{1,0:T(4,128)} %copy-done) | copy-start | bytes 393220 | tf_op jit(solution)/shard_map/while
  142.6 4.7 %copy-start.1 = (s32[4,8192]{1,0:T(4,128)S(1)}, s32[4,8192]{1,0:T(4,128)}, u32[]{:S(2)}) copy-start(s32[4,8192]{1,0:T(4,128)} %copy-done) | copy-start | bytes 393220 | tf_op jit(solution)/shard_map/while
  147.3 2.9 copy-start.2
  150.1 130.4 %all-gather.3.cloned.1.call-start = ((), (), s32[]{:S(2)}) async-start(), calls=%async_computation.2 | async-start | bytes 2433024 | tf_op jit(solution)/shard_map/all_gather | solution.py:12
  193.2 5.6 %collective-permute-start = (f32[3,8,2,180]{3,1,0,2:T(8,128)S(1)}, f32[3,8,2,180]{3,1,0,2:T(8,128)S(1)}, u32[]{:S(2)}, u32[]{:S(2)}) collective-permute-start(f32[3,8,2,180]{3,1,0,2:T(8,128)S(1)} %get-tuple-element.334), channel_id=1, source_target_pairs={{0,1},{1,2},{2,3},{3,4},{4,5},{5,6},{6,7},{8,9},{9,10},{10,11},{11... | collective-permute-start | bytes 103688 | tf_op jit(solution)/shard_map/ppermute | solution.py:28
  195.2 5.4 %collective-permute-start.1 = (f32[3,8,2,180]{3,1,0,2:T(8,128)S(1)}, f32[3,8,2,180]{3,1,0,2:T(8,128)S(1)}, u32[]{:S(2)}, u32[]{:S(2)}) collective-permute-start(f32[3,8,2,180]{3,1,0,2:T(8,128)S(1)} %get-tuple-element.335), channel_id=1, source_target_pairs={{1,0},{2,1},{3,2},{4,3},{5,4},{6,5},{7,6},{9,8},{10,9},{11,10},{12... | collective-permute-start | bytes 103688 | tf_op jit(solution)/shard_map/ppermute | solution.py:31
  (13 other events, 8.5 us)
Sparse Core Ops, SparseCore 0:
  150.2 37.2 reduce-scatter.1
  201.6 78.8 all-gather.2
where the time goes:
time: 320 us; the launch traced here: 318 us
  waiting for transfers between devices  118 us (37%)
  matrix products  78.7 us (25%)
  other arithmetic  55.1 us (17%)
  local copies, waits for them, and re-layouts  46 us (14%)
  between operations  13.6 us (4%)
  starting transfers between devices  5.61 us (2%)
    all_gather x1, waiting for transfers between devices, entering(): everything = lax.all_gather(x, axis)  78.6 us
    dot_general x16, matrix products, advance(): jnp.einsum('tnk,tnc->tkc', onehot, deposit, preferred_element_type=jnp.fl...  75.1 us
    reduce_scatter x1, waiting for transfers between devices, per_device(): lax.psum_scatter(partial_sum.reshape(block_count * drift_dev, row_dev, 4...  37.3 us
    add x16, local copies, waits for them, and re-layouts, advance(): jnp.where(at_left, left_chan[..., None], nothing)  36.7 us
    select_n x32, other arithmetic, hop(): return jnp.where(reached, new, before)  29.1 us
    add x16, other arithmetic, advance(): jnp.where(at_left, left_chan[..., None], nothing)  13.7 us
    eq x16, other arithmetic, advance(): at_right = pad_iota == pad_ids[:, :, None, None] + 1  6.41 us
  transfers between devices with their start and end apart: 4, of which 3 were waited for; matrix products, arithmetic and copies ran while one was open for 0% of the time, Pallas kernels for 0%

commit v1 on v0

v1 whole, which is shorter than its diff:
```python
import functools

import jax
import jax.numpy as jnp
from jax import lax
from jax.experimental import pallas as pl
from jax.experimental.pallas import tpu as pltpu
from jax.sharding import PartitionSpec as P

PAD = 180
DRIFT = 256
PAD_SLOT = 192
CHUNK = 512


def with_halo(block, sides, width):
    for axis, dim in sides:
        count = lax.axis_size(axis)
        forward = [(i, i + 1) for i in range(count - 1)]
        backward = [(target, source) for source, target in forward]
        low = lax.ppermute(
            lax.slice_in_dim(block, block.shape[dim] - width, None, axis=dim), axis, forward
        )
        high = lax.ppermute(lax.slice_in_dim(block, 0, width, axis=dim), axis, backward)
        block = jnp.concatenate([low, block, high], axis=dim)
    return block


def row_kernels(kernel_reach):
    spread = kernel_reach.astype(jnp.float32)[:, None, None]
    places = lax.broadcasted_iota(jnp.int32, (PAD, PAD), 0)
    others = lax.broadcasted_iota(jnp.int32, (PAD, PAD), 1)
    distance = jnp.abs(places - others).astype(jnp.float32)[None]
    return jnp.maximum(spread + 1.0 - distance, 0.0) / ((spread + 1.0) * (spread + 1.0))


def hist_kernel(cell_rows, idx_ref, dep_ref, out_ref):
    source = pl.program_id(0)

    @pl.when(source == 0)
    def _():
        out_ref[...] = jnp.zeros_like(out_ref)

    length = idx_ref.shape[2]

    def body(step, carry):
        off = pl.multiple_of(step * CHUNK, CHUNK)
        cell = idx_ref[0, 0:1, pl.ds(off, CHUNK)]
        pad = idx_ref[0, 1:2, pl.ds(off, CHUNK)]
        dep = dep_ref[0, :, pl.ds(off, CHUNK)]
        c_iota = lax.broadcasted_iota(jnp.int32, (cell_rows, CHUNK), 0)
        onehot = jnp.where(c_iota == cell, 1.0, 0.0).astype(jnp.bfloat16)
        p_iota = lax.broadcasted_iota(jnp.int32, (PAD_SLOT, CHUNK), 0)
        at_left = p_iota == pad
        at_right = p_iota == pad + 1
        parts = []
        for k in range(4):
            parts.append(
                jnp.where(at_left, dep[k : k + 1], jnp.where(at_right, dep[4 + k : 5 + k], 0.0))
            )
        spread = jnp.concatenate(parts, 0).astype(jnp.bfloat16)
        out_ref[...] += lax.dot_general(
            onehot, spread, (((1,), (1,)), ((), ())), preferred_element_type=jnp.float32
        )
        return carry

    lax.fori_loop(0, length // CHUNK, body, 0)


def build_histogram(idx, dep, cell_rows):
    sources, _, length = idx.shape
    flops = 2 * cell_rows * 4 * PAD_SLOT * sources * length
    return pl.pallas_call(
        functools.partial(hist_kernel, cell_rows),
        out_shape=jax.ShapeDtypeStruct((cell_rows, 4 * PAD_SLOT), jnp.float32),
        grid=(sources,),
        in_specs=[
            pl.BlockSpec((1, 2, length), lambda s: (s, 0, 0)),
            pl.BlockSpec((1, 8, length), lambda s: (s, 0, 0)),
        ],
        out_specs=pl.BlockSpec((cell_rows, 4 * PAD_SLOT), lambda s: (0, 0)),
        compiler_params=pltpu.CompilerParams(dimension_semantics=("arbitrary",)),
        cost_estimate=pl.CostEstimate(
            flops=flops,
            transcendentals=0,
            bytes_accessed=sources * length * 40 + cell_rows * 4 * PAD_SLOT * 4,
        ),
    )(idx, dep)


def exclusive_prefix(totals):
    gz_count = lax.axis_size("gz")
    tf_count = lax.axis_size("tf")
    g = lax.axis_index("gz")
    before = jnp.zeros_like(totals)
    row_sum = totals
    for shift in range(1, gz_count):
        pairs = [(i, (i + shift) % gz_count) for i in range(gz_count)]
        got = lax.ppermute(totals, "gz", pairs)
        row_sum = row_sum + got
        before = before + jnp.where(shift <= g, got, 0.0)
    for shift in range(1, tf_count):
        pairs = [(i, i + shift) for i in range(tf_count - shift)]
        before = before + lax.ppermute(row_sum, "tf", pairs)
    return before


def smooth(field, kernel_reach):
    across = jnp.einsum(
        "kzrq,rpq->kzrp", field, row_kernels(kernel_reach), precision=lax.Precision.HIGHEST
    )
    rimmed = with_halo(across, (("sec", 2),), 2)
    row_total = across.shape[2]
    return (
        rimmed[:, :, 0:row_total]
        + 2.0 * rimmed[:, :, 1 : row_total + 1]
        + 3.0 * rimmed[:, :, 2 : row_total + 2]
        + 2.0 * rimmed[:, :, 3 : row_total + 3]
        + rimmed[:, :, 4 : row_total + 4]
    ) / 9.0


def per_device(residuals, weights, fraction, voxels, kernel_reach):
    gz_count = lax.axis_size("gz")
    drift_dev = DRIFT // (lax.axis_size("tf") * gz_count)
    row_dev = kernel_reach.shape[0]
    cell_count = drift_dev * row_dev
    cell_rows = -(-cell_count // 16) * 16
    coords = voxels[:, 0, 0, 0]
    target = lax.broadcasted_iota(jnp.int32, coords.shape[1:], 0)
    local_row = coords[0] - lax.axis_index("sec") * row_dev
    local_drift = coords[2] - (target * gz_count + lax.axis_index("gz")) * drift_dev
    cell = local_drift * row_dev + local_row
    outgoing = jnp.concatenate(
        [
            cell[:, None].astype(jnp.bfloat16),
            coords[1][:, None].astype(jnp.bfloat16),
            jnp.transpose(residuals[:, 0, 0, 0], (1, 0, 2)),
            weights[0, 0, 0][:, None],
            fraction[0, 0, 0][:, None],
        ],
        1,
    )
    incoming = lax.all_to_all(outgoing, "tf", 0, 0, tiled=True)
    idx = incoming[:, 0:2].astype(jnp.int32)
    values = incoming[:, 2:].astype(jnp.float32)
    weight_now = values[:, 3]
    share = values[:, 4]
    left_share = weight_now * (1.0 - share)
    right_share = weight_now * share
    dep = jnp.stack(
        [
            left_share,
            left_share * values[:, 0],
            left_share * values[:, 1],
            left_share * values[:, 2],
            right_share,
            right_share * values[:, 0],
            right_share * values[:, 1],
            right_share * values[:, 2],
        ],
        1,
    ).astype(jnp.bfloat16).astype(jnp.float32)
    raw = build_histogram(idx, dep, cell_rows)
    histogram = raw.reshape(cell_rows, 4, PAD_SLOT)[:cell_count, :, :PAD]
    histogram = histogram.reshape(drift_dev, row_dev, 4, PAD)
    means = histogram[:, :, 1:4] / (histogram[:, :, 0:1] + 1.0)
    means = jnp.transpose(means, (2, 0, 1, 3))
    field = smooth(means, kernel_reach)
    carried = exclusive_prefix(jnp.sum(field, axis=1))
    return carried[:, None] + jnp.cumsum(field, axis=1)


def solution(mesh):
    placed = (
        P(None, "tf", "gz", "sec", None, None),
        P("tf", "gz", "sec", None, None),
        P("tf", "gz", "sec", None, None),
        P(None, "tf", "gz", "sec", None, None),
        P("sec"),
    )
    return jax.shard_map(
        per_device,
        mesh=mesh,
        in_specs=placed,
        out_specs=P(None, ("tf", "gz"), "sec", None),
        check_vma=False,
    )
```

time: 320 us -> 109 us (0.34)
  waiting for transfers between devices: 118 us -> 23 us
  matrix products: 78.7 us -> 3.6 us
  other arithmetic: 55.1 us -> 5.85 us
  local copies, waits for them, and re-layouts: 46 us -> 6.69 us
  Pallas kernels: 0 us -> 35.3 us
  starting transfers between devices: 5.61 us -> 33 us
  between operations: 13.6 us -> 0.29 us
    all_gather x1 -> x0, waiting for transfers between devices: 78.6 us -> none  [entering(): everything = lax.all_gather(x, axis)]
    dot_general x16 -> x0, matrix products: 75.1 us -> none  [advance(): jnp.einsum('tnk,tnc->tkc', onehot, deposit, preferred_element_type=jnp.fl...]
    reduce_scatter x1 -> x0, waiting for transfers between devices: 37.3 us -> none  [per_device(): lax.psum_scatter(partial_sum.reshape(block_count * drift_dev, row_dev, 4...]
    add x17 -> x1, local copies, waits for them, and re-layouts: 37.5 us -> 0.8 us  [per_device(): return carried[:, None] + jnp.cumsum(field, axis=1)]
    pallas_call x0 -> x1, Pallas kernels: none -> 35.3 us  [build_histogram(): pl.pallas_call(functools.partial(hist_kernel, cell_rows), out_shape=jax.S...]
    select_n x32 -> x0, other arithmetic: 29.1 us -> none  [hop(): return jnp.where(reached, new, before)]
    ppermute x0 -> x10, starting transfers between devices: none -> 24.4 us  [the longest x7 17.3 us: exclusive_prefix(): got = lax.ppermute(totals, 'gz', pairs)]
    add x35 -> x3, other arithmetic: 15.6 us -> 0.3 us  [the longest x1 0.13 us: exclusive_prefix(): before = before + lax.ppermute(row_sum, 'tf', pairs)]
  transfers between devices with their start and end apart: 4 -> 13, of which waited for: 3 -> 6; matrix products, arithmetic and copies ran while one was open for 0% -> 0% of each run, Pallas kernels for 0% -> 0%
where the time goes in v1:
time: 109 us; the launch traced here: 108 us
  Pallas kernels  35.3 us (32%)
  starting transfers between devices  33 us (30%)
  waiting for transfers between devices  23 us (21%)
  local copies, waits for them, and re-layouts  6.69 us (6%)
  other arithmetic  5.85 us (5%)
  matrix products  3.6 us (3%)
    pallas_call x1, Pallas kernels, build_histogram(): pl.pallas_call(functools.partial(hist_kernel, cell_rows), out_shape=jax.S...  35.3 us
    ppermute x7, starting transfers between devices, exclusive_prefix(): got = lax.ppermute(totals, 'gz', pairs)  17.3 us
    all_to_all x1, waiting for transfers between devices, per_device(): incoming = lax.all_to_all(outgoing, 'tf', 0, 0, tiled=True)  9.42 us
    ppermute x7, waiting for transfers between devices, exclusive_prefix(): got = lax.ppermute(totals, 'gz', pairs)  9.07 us
    ppermute x3, starting transfers between devices, exclusive_prefix(): before = before + lax.ppermute(row_sum, 'tf', pairs)  7.13 us
    all_to_all x1, starting transfers between devices, per_device(): incoming = lax.all_to_all(outgoing, 'tf', 0, 0, tiled=True)  4.29 us
    unnamed x1, matrix products  3.6 us
    ppermute x1, waiting for transfers between devices, with_halo(): lax.ppermute(lax.slice_in_dim(block, block.shape[dim] - width, None, axis...  2.98 us
  transfers between devices with their start and end apart: 13, of which 6 were waited for; matrix products, arithmetic and copies ran while one was open for 0% of the time, Pallas kernels for 0%

profile of v1, /device:TPU:8, one launch (start us, length us, event | category | flops | bytes accessed | tf_op | source)
XLA Modules:
  0.0 107.8 jit_solution(14027349997394610885)
XLA Ops:
  0.0 1.1 %fusion.23 = (bf16[4,1,8192]{2,0,1:T(4,128)(2,1)S(1)}, s32[1,1,1,1,4,8192]{5,4,3,2,1,0:T(4,128)S(1)}, s32[1,1,1,1,4,8192]{5,4,3,2,1,0:T(4,128)S(1)}) fusion(s32[3,1,1,1,4,8192]{5,4,3,2,1,0:T(4,128)} %param.8, s32[]{:T(128)S(6)} %mul.84), kind=kLoop, calls=%fused_computation.51 | loop fusion | flops 65536 | bytes 720900 | tf_op jit(solution)/shard_map/convert_element_type | solution.py:137
  2.0 2.0 %concatenate.12 = bf16[4,7,8192]{2,1,0:T(8,128)(2,1)} concatenate(bf16[4,1,8192]{2,1,0:T(2,128)(2,1)S(1)} %fusion.20, bf16[4,1,8192]{2,1,0:T(2,128)(2,1)S(1)} %copy.31, bf16[4,3,8192]{2,1,0:T(4,128)(2,1)S(1)} %bitcast.39, bf16[4,1,8192]{2,1,0:T(2,128)(2,1)S(1)} %copy.32, bf16[4,1,8192]{2,1,0:T(2,128)(2,1)S(1)} %copy.33), dimensions={1} | concatenate | bytes 917504 | tf_op jit(solution)/shard_map/concatenate | solution.py:134
  4.0 4.3 %all-to-all-start = ((bf16[4,7,8192]{2,1,0:T(8,128)(2,1)}), bf16[4,7,8192]{2,1,0:T(8,128)(2,1)S(1)}, u32[]{:S(2)}, u32[]{:S(2)}) async-start(bf16[4,7,8192]{2,1,0:T(8,128)(2,1)} %concatenate.12), calls=%async_computation | async-start | bytes 1048576 | tf_op jit(solution)/shard_map/all_to_all | solution.py:144
  8.4 9.4 %all-to-all-done = bf16[4,7,8192]{2,1,0:T(8,128)(2,1)S(1)} async-done(((bf16[4,7,8192]{2,1,0:T(8,128)(2,1)}), bf16[4,7,8192]{2,1,0:T(8,128)(2,1)S(1)}, u32[]{:S(2)}, u32[]{:S(2)}) %all-to-all-start) | async-done | bytes 458784 | tf_op jit(solution)/shard_map/all_to_all | solution.py:144
  19.1 1.6 %stack.3 = bf16[4,8,8192]{2,1,0:T(8,128)(2,1)S(1)} concatenate(bf16[4,1,8192]{2,1,0:T(2,128)(2,1)S(1)} %get-tuple-element.23, bf16[4,1,8192]{2,1,0:T(2,128)(2,1)S(1)} %get-tuple-element.14, bf16[4,1,8192]{2,1,0:T(2,128)(2,1)S(1)} %get-tuple-element.13, bf16[4,1,8192]{2,1,0:T(2,128)(2,1)S(1)} %get-tuple-element.15, bf16[4,1,8192]{2,1,0:T(2,128)(2,1)S(1)} %get-tuple-element.22, ...), dimensions={1} | concatenate | bytes 1048576 | tf_op jit(solution)/shard_map/stack | solution.py:151
  20.7 1.0 convert_element_type.49.dep_ref
  22.6 35.3 %shard_map.55 = f32[160,768]{1,0:T(8,128)} custom-call(s32[4,2,8192]{2,1,0:T(2,128)} %slice_convert_fusion.1.idx_ref, f32[4,8,8192]{2,1,0:T(8,128)} %convert_element_type.49.dep_ref), custom_call_target="tpu_custom_call" | custom-call | flops 8053063680 | bytes 1802240 | tf_op jit(solution)/shard_map/pallas_call | solution.py:73
  57.9 1.5 %reshape.87 = f32[160,4,192]{2,1,0:T(4,128)S(1)} reshape(f32[160,768]{1,0:T(8,128)} %shard_map.55) | data formatting | bytes 983040 | tf_op jit(solution)/shard_map/reshape | solution.py:165
  59.9 3.6 %fusion.5 = f32[3,8,19,180]{3,1,0,2:T(8,128)S(1)} fusion(f32[19]{0:T(128)S(1)} %get-tuple-element.25, f32[180,180]{1,0:T(8,128)S(1)} %abs_convert_fusion, f32[19]{0:T(128)S(1)} %get-tuple-element.24, f32[3,8,19,180]{3,0,2,1:T(4,128)S(1)} %fusion.6), kind=kOutput, calls=%fused_computation.6 | convolution fusion | flops 179139600 | bytes 786392
  63.6 1.9 %collective-permute-start.1 = (f32[3,8,2,180]{3,1,0,2:T(8,128)S(1)}, f32[3,8,2,180]{3,1,0,2:T(8,128)S(1)}, u32[]{:S(2)}, u32[]{:S(2)}) collective-permute-start(f32[3,8,2,180]{3,1,0,2:T(8,128)S(1)} %get-tuple-element.18), channel_id=1, source_target_pairs={{1,0},{2,1},{3,2},{4,3},{5,4},{6,5},{7,6},{9,8},{10,9},{11,10},{12... | collective-permute-start | bytes 103688 | tf_op jit(solution)/shard_map/ppermute | solution.py:24
  65.5 2.4 %collective-permute-start = (f32[3,8,2,180]{3,1,0,2:T(8,128)S(1)}, f32[3,8,2,180]{3,1,0,2:T(8,128)S(1)}, u32[]{:S(2)}, u32[]{:S(2)}) collective-permute-start(f32[3,8,2,180]{3,1,0,2:T(8,128)S(1)} %get-tuple-element.17), channel_id=1, source_target_pairs={{0,1},{1,2},{2,3},{3,4},{4,5},{5,6},{6,7},{8,9},{9,10},{10,11},{11... | collective-permute-start | bytes 103688 | tf_op jit(solution)/shard_map/ppermute | solution.py:21
  67.9 3.0 %collective-permute-done = f32[3,8,2,180]{3,1,0,2:T(8,128)S(1)} collective-permute-done((f32[3,8,2,180]{3,1,0,2:T(8,128)S(1)}, f32[3,8,2,180]{3,1,0,2:T(8,128)S(1)}, u32[]{:S(2)}, u32[]{:S(2)}) %collective-permute-start) | collective-permute-done | bytes 34592 | tf_op jit(solution)/shard_map/ppermute | solution.py:21
  71.2 5.9 %collective-permute-start.8 = (f32[3,19,180]{2,0,1:T(4,128)S(1)}, f32[3,19,180]{2,0,1:T(4,128)S(1)}, u32[]{:S(2)}, u32[]{:S(2)}) collective-permute-start(f32[3,19,180]{2,0,1:T(4,128)S(1)} %get-tuple-element.5), channel_id=1, source_target_pairs={{0,56},{8,0},{16,8},{24,16},{32,24},{40,32},{48,40},{56,48},{1,57}... | collective-permute-start | bytes 123128 | tf_op jit(solution)/shard_map/ppermute | solution.py:99
  77.1 1.5 %collective-permute-start.7 = (f32[3,19,180]{2,0,1:T(4,128)S(1)}, f32[3,19,180]{2,0,1:T(4,128)S(1)}, u32[]{:S(2)}, u32[]{:S(2)}) collective-permute-start(f32[3,19,180]{2,0,1:T(4,128)S(1)} %get-tuple-element.5), channel_id=1, source_target_pairs={{0,48},{8,56},{16,0},{24,8},{32,16},{40,24},{48,32},{56,40},{1,49}... | collective-permute-start | bytes 123128 | tf_op jit(solution)/shard_map/ppermute | solution.py:99
  79.0 5.0 %collective-permute-start.5 = (f32[3,19,180]{2,0,1:T(4,128)S(1)}, f32[3,19,180]{2,0,1:T(4,128)S(1)}, u32[]{:S(2)}, u32[]{:S(2)}) collective-permute-start(f32[3,19,180]{2,0,1:T(4,128)S(1)} %get-tuple-element.5), channel_id=1, source_target_pairs={{0,32},{8,40},{16,48},{24,56},{32,0},{40,8},{48,16},{56,24},{1,33}... | collective-permute-start | bytes 123128 | tf_op jit(solution)/shard_map/ppermute | solution.py:99
  84.1 2.5 %collective-permute-start.3 = (f32[3,19,180]{2,0,1:T(4,128)S(1)}, f32[3,19,180]{2,0,1:T(4,128)S(1)}, u32[]{:S(2)}, u32[]{:S(2)}) collective-permute-start(f32[3,19,180]{2,0,1:T(4,128)S(1)} %get-tuple-element.5), channel_id=1, source_target_pairs={{0,16},{8,24},{16,32},{24,40},{32,48},{40,56},{48,0},{56,8},{1,17}... | collective-permute-start | bytes 123128 | tf_op jit(solution)/shard_map/ppermute | solution.py:99
  86.5 1.9 %collective-permute-start.2 = (f32[3,19,180]{2,0,1:T(4,128)S(1)}, f32[3,19,180]{2,0,1:T(4,128)S(1)}, u32[]{:S(2)}, u32[]{:S(2)}) collective-permute-start(f32[3,19,180]{2,0,1:T(4,128)S(1)} %get-tuple-element.5), channel_id=1, source_target_pairs={{0,8},{8,16},{16,24},{24,32},{32,40},{40,48},{48,56},{56,0},{1,9},... | collective-permute-start | bytes 123128 | tf_op jit(solution)/shard_map/ppermute | solution.py:99
  88.4 1.8 %collective-permute-done.6 = f32[3,19,180]{2,0,1:T(4,128)S(1)} collective-permute-done((f32[3,19,180]{2,0,1:T(4,128)S(1)}, f32[3,19,180]{2,0,1:T(4,128)S(1)}, u32[]{:S(2)}, u32[]{:S(2)}) %collective-permute-start.6) | collective-permute-done | bytes 41072 | tf_op jit(solution)/shard_map/ppermute | solution.py:99
  90.3 4.7 %collective-permute-done.4 = f32[3,19,180]{2,0,1:T(4,128)S(1)} collective-permute-done((f32[3,19,180]{2,0,1:T(4,128)S(1)}, f32[3,19,180]{2,0,1:T(4,128)S(1)}, u32[]{:S(2)}, u32[]{:S(2)}) %collective-permute-start.4) | collective-permute-done | bytes 41072 | tf_op jit(solution)/shard_map/ppermute | solution.py:99
  95.0 2.5 %collective-permute-done.3 = f32[3,19,180]{2,0,1:T(4,128)S(1)} collective-permute-done((f32[3,19,180]{2,0,1:T(4,128)S(1)}, f32[3,19,180]{2,0,1:T(4,128)S(1)}, u32[]{:S(2)}, u32[]{:S(2)}) %collective-permute-start.3) | collective-permute-done | bytes 41072 | tf_op jit(solution)/shard_map/ppermute | solution.py:99
  97.6 3.1 %collective-permute-start.11 = (f32[3,19,180]{2,0,1:T(4,128)S(1)}, f32[3,19,180]{2,0,1:T(4,128)S(1)}, u32[]{:S(2)}, u32[]{:S(2)}) collective-permute-start(f32[3,19,180]{2,0,1:T(4,128)S(1)} %add_add_fusion.1), channel_id=1, source_target_pairs={{0,192},{1,193},{2,194},{3,195},{4,196},{5,197},{6,198},{7,199},{8... | collective-permute-start | bytes 123128 | tf_op jit(solution)/shard_map/ppermute | solution.py:104
  100.7 1.3 %collective-permute-start.10 = (f32[3,19,180]{2,0,1:T(4,128)S(1)}, f32[3,19,180]{2,0,1:T(4,128)S(1)}, u32[]{:S(2)}, u32[]{:S(2)}) collective-permute-start(f32[3,19,180]{2,0,1:T(4,128)S(1)} %add_add_fusion.1), channel_id=1, source_target_pairs={{0,128},{64,192},{1,129},{65,193},{2,130},{66,194},{3,131},{67,195... | collective-permute-start | bytes 123128 | tf_op jit(solution)/shard_map/ppermute | solution.py:104
  102.0 2.8 %collective-permute-start.9 = (f32[3,19,180]{2,0,1:T(4,128)S(1)}, f32[3,19,180]{2,0,1:T(4,128)S(1)}, u32[]{:S(2)}, u32[]{:S(2)}) collective-permute-start(f32[3,19,180]{2,0,1:T(4,128)S(1)} %add_add_fusion.1), channel_id=1, source_target_pairs={{0,64},{64,128},{128,192},{1,65},{65,129},{129,193},{2,66},{66,130... | collective-permute-start | bytes 123128 | tf_op jit(solution)/shard_map/ppermute | solution.py:104
  105.2 1.5 %collective-permute-done.9 = f32[3,19,180]{2,0,1:T(4,128)S(1)} collective-permute-done((f32[3,19,180]{2,0,1:T(4,128)S(1)}, f32[3,19,180]{2,0,1:T(4,128)S(1)}, u32[]{:S(2)}, u32[]{:S(2)}) %collective-permute-start.9) | collective-permute-done | bytes 41072 | tf_op jit(solution)/shard_map/ppermute | solution.py:104
  (42 shorter events, 5.7 us)
Async XLA Ops:
  0.0 1.3 %copy-start = (bf16[3,1,1,1,4,8192]{5,4,3,2,1,0:T(4,128)(2,1)S(1)}, bf16[3,1,1,1,4,8192]{5,4,3,2,1,0:T(4,128)(2,1)}, u32[]{:S(2)}) copy-start(bf16[3,1,1,1,4,8192]{5,4,3,2,1,0:T(4,128)(2,1)} %param.5) | copy-start | bytes 589828
  0.0 1.5 %copy-start.1 = (bf16[1,1,1,4,8192]{4,3,2,1,0:T(4,128)(2,1)S(1)}, bf16[1,1,1,4,8192]{4,3,2,1,0:T(4,128)(2,1)}, u32[]{:S(2)}) copy-start(bf16[1,1,1,4,8192]{4,3,2,1,0:T(4,128)(2,1)} %param.6) | copy-start | bytes 196612
  0.0 1.6 %copy-start.2 = (bf16[1,1,1,4,8192]{4,3,2,1,0:T(4,128)(2,1)S(1)}, bf16[1,1,1,4,8192]{4,3,2,1,0:T(4,128)(2,1)}, u32[]{:S(2)}) copy-start(bf16[1,1,1,4,8192]{4,3,2,1,0:T(4,128)(2,1)} %param.7) | copy-start | bytes 196612
  2.0 6.4 %copy-start.3 = (s32[19]{0:T(128)S(1)}, s32[19]{0:T(128)}, u32[]{:S(2)}) copy-start(s32[19]{0:T(128)} %param.9) | copy-start | bytes 232
  4.0 13.8 %all-to-all-start = ((bf16[4,7,8192]{2,1,0:T(8,128)(2,1)}), bf16[4,7,8192]{2,1,0:T(8,128)(2,1)S(1)}, u32[]{:S(2)}, u32[]{:S(2)}) async-start(bf16[4,7,8192]{2,1,0:T(8,128)(2,1)} %concatenate.12), calls=%async_computation | async-start | bytes 1048576 | tf_op jit(solution)/shard_map/all_to_all | solution.py:144
  63.6 4.3 %collective-permute-start.1 = (f32[3,8,2,180]{3,1,0,2:T(8,128)S(1)}, f32[3,8,2,180]{3,1,0,2:T(8,128)S(1)}, u32[]{:S(2)}, u32[]{:S(2)}) collective-permute-start(f32[3,8,2,180]{3,1,0,2:T(8,128)S(1)} %get-tuple-element.18), channel_id=1, source_target_pairs={{1,0},{2,1},{3,2},{4,3},{5,4},{6,5},{7,6},{9,8},{10,9},{11,10},{12... | collective-permute-start | bytes 103688 | tf_op jit(solution)/shard_map/ppermute | solution.py:24
  65.5 5.4 %collective-permute-start = (f32[3,8,2,180]{3,1,0,2:T(8,128)S(1)}, f32[3,8,2,180]{3,1,0,2:T(8,128)S(1)}, u32[]{:S(2)}, u32[]{:S(2)}) collective-permute-start(f32[3,8,2,180]{3,1,0,2:T(8,128)S(1)} %get-tuple-element.17), channel_id=1, source_target_pairs={{0,1},{1,2},{2,3},{3,4},{4,5},{5,6},{6,7},{8,9},{9,10},{10,11},{11... | collective-permute-start | bytes 103688 | tf_op jit(solution)/shard_map/ppermute | solution.py:21
  71.2 12.9 %collective-permute-start.8 = (f32[3,19,180]{2,0,1:T(4,128)S(1)}, f32[3,19,180]{2,0,1:T(4,128)S(1)}, u32[]{:S(2)}, u32[]{:S(2)}) collective-permute-start(f32[3,19,180]{2,0,1:T(4,128)S(1)} %get-tuple-element.5), channel_id=1, source_target_pairs={{0,56},{8,0},{16,8},{24,16},{32,24},{40,32},{48,40},{56,48},{1,57}... | collective-permute-start | bytes 123128 | tf_op jit(solution)/shard_map/ppermute | solution.py:99
  77.1 9.4 %collective-permute-start.7 = (f32[3,19,180]{2,0,1:T(4,128)S(1)}, f32[3,19,180]{2,0,1:T(4,128)S(1)}, u32[]{:S(2)}, u32[]{:S(2)}) collective-permute-start(f32[3,19,180]{2,0,1:T(4,128)S(1)} %get-tuple-element.5), channel_id=1, source_target_pairs={{0,48},{8,56},{16,0},{24,8},{32,16},{40,24},{48,32},{56,40},{1,49}... | collective-permute-start | bytes 123128 | tf_op jit(solution)/shard_map/ppermute | solution.py:99
  78.6 11.7 %collective-permute-start.6 = (f32[3,19,180]{2,0,1:T(4,128)S(1)}, f32[3,19,180]{2,0,1:T(4,128)S(1)}, u32[]{:S(2)}, u32[]{:S(2)}) collective-permute-start(f32[3,19,180]{2,0,1:T(4,128)S(1)} %get-tuple-element.5), channel_id=1, source_target_pairs={{0,40},{8,48},{16,56},{24,0},{32,8},{40,16},{48,24},{56,32},{1,41}... | collective-permute-start | bytes 123128 | tf_op jit(solution)/shard_map/ppermute | solution.py:99
  79.0 11.3 %collective-permute-start.5 = (f32[3,19,180]{2,0,1:T(4,128)S(1)}, f32[3,19,180]{2,0,1:T(4,128)S(1)}, u32[]{:S(2)}, u32[]{:S(2)}) collective-permute-start(f32[3,19,180]{2,0,1:T(4,128)S(1)} %get-tuple-element.5), channel_id=1, source_target_pairs={{0,32},{8,40},{16,48},{24,56},{32,0},{40,8},{48,16},{56,24},{1,33}... | collective-permute-start | bytes 123128 | tf_op jit(solution)/shard_map/ppermute | solution.py:99
  84.0 10.9 %collective-permute-start.4 = (f32[3,19,180]{2,0,1:T(4,128)S(1)}, f32[3,19,180]{2,0,1:T(4,128)S(1)}, u32[]{:S(2)}, u32[]{:S(2)}) collective-permute-start(f32[3,19,180]{2,0,1:T(4,128)S(1)} %get-tuple-element.5), channel_id=1, source_target_pairs={{0,24},{8,32},{16,40},{24,48},{32,56},{40,0},{48,8},{56,16},{1,25}... | collective-permute-start | bytes 123128 | tf_op jit(solution)/shard_map/ppermute | solution.py:99
  84.1 13.4 %collective-permute-start.3 = (f32[3,19,180]{2,0,1:T(4,128)S(1)}, f32[3,19,180]{2,0,1:T(4,128)S(1)}, u32[]{:S(2)}, u32[]{:S(2)}) collective-permute-start(f32[3,19,180]{2,0,1:T(4,128)S(1)} %get-tuple-element.5), channel_id=1, source_target_pairs={{0,16},{8,24},{16,32},{24,40},{32,48},{40,56},{48,0},{56,8},{1,17}... | collective-permute-start | bytes 123128 | tf_op jit(solution)/shard_map/ppermute | solution.py:99
  86.5 11.0 %collective-permute-start.2 = (f32[3,19,180]{2,0,1:T(4,128)S(1)}, f32[3,19,180]{2,0,1:T(4,128)S(1)}, u32[]{:S(2)}, u32[]{:S(2)}) collective-permute-start(f32[3,19,180]{2,0,1:T(4,128)S(1)} %get-tuple-element.5), channel_id=1, source_target_pairs={{0,8},{8,16},{16,24},{24,32},{32,40},{40,48},{48,56},{56,0},{1,9},... | collective-permute-start | bytes 123128 | tf_op jit(solution)/shard_map/ppermute | solution.py:99
  97.6 7.6 %collective-permute-start.11 = (f32[3,19,180]{2,0,1:T(4,128)S(1)}, f32[3,19,180]{2,0,1:T(4,128)S(1)}, u32[]{:S(2)}, u32[]{:S(2)}) collective-permute-start(f32[3,19,180]{2,0,1:T(4,128)S(1)} %add_add_fusion.1), channel_id=1, source_target_pairs={{0,192},{1,193},{2,194},{3,195},{4,196},{5,197},{6,198},{7,199},{8... | collective-permute-start | bytes 123128 | tf_op jit(solution)/shard_map/ppermute | solution.py:104
  100.7 4.5 %collective-permute-start.10 = (f32[3,19,180]{2,0,1:T(4,128)S(1)}, f32[3,19,180]{2,0,1:T(4,128)S(1)}, u32[]{:S(2)}, u32[]{:S(2)}) collective-permute-start(f32[3,19,180]{2,0,1:T(4,128)S(1)} %add_add_fusion.1), channel_id=1, source_target_pairs={{0,128},{64,192},{1,129},{65,193},{2,130},{66,194},{3,131},{67,195... | collective-permute-start | bytes 123128 | tf_op jit(solution)/shard_map/ppermute | solution.py:104
  102.0 4.8 %collective-permute-start.9 = (f32[3,19,180]{2,0,1:T(4,128)S(1)}, f32[3,19,180]{2,0,1:T(4,128)S(1)}, u32[]{:S(2)}, u32[]{:S(2)}) collective-permute-start(f32[3,19,180]{2,0,1:T(4,128)S(1)} %add_add_fusion.1), channel_id=1, source_target_pairs={{0,64},{64,128},{128,192},{1,65},{65,129},{129,193},{2,66},{66,130... | collective-permute-start | bytes 123128 | tf_op jit(solution)/shard_map/ppermute | solution.py:104

commit v2 on v1

--- a/solution.py
+++ b/solution.py
@@ -10,7 +10,7 @@
 PAD = 180
 DRIFT = 256
 PAD_SLOT = 192
-CHUNK = 512
+CHUNK = 4096
 
 
 def with_halo(block, sides, width):
@@ -42,25 +42,27 @@
         out_ref[...] = jnp.zeros_like(out_ref)
 
     length = idx_ref.shape[2]
+    zero = jnp.zeros((), jnp.bfloat16)
+    one = jnp.ones((), jnp.bfloat16)
 
     def body(step, carry):
         off = pl.multiple_of(step * CHUNK, CHUNK)
-        cell = idx_ref[0, 0:1, pl.ds(off, CHUNK)]
-        pad = idx_ref[0, 1:2, pl.ds(off, CHUNK)]
-        dep = dep_ref[0, :, pl.ds(off, CHUNK)]
-        c_iota = lax.broadcasted_iota(jnp.int32, (cell_rows, CHUNK), 0)
-        onehot = jnp.where(c_iota == cell, 1.0, 0.0).astype(jnp.bfloat16)
-        p_iota = lax.broadcasted_iota(jnp.int32, (PAD_SLOT, CHUNK), 0)
+        cell = idx_ref[0, 0:1, pl.ds(off, CHUNK)].astype(jnp.bfloat16)
+        pad = idx_ref[0, 1:2, pl.ds(off, CHUNK)].astype(jnp.bfloat16)
+        dep = dep_ref[0, :, pl.ds(off, CHUNK)].astype(jnp.bfloat16)
+        c_iota = lax.broadcasted_iota(jnp.int32, (cell_rows, CHUNK), 0).astype(jnp.bfloat16)
+        onehot = jnp.where(c_iota == cell, one, zero)
+        p_iota = lax.broadcasted_iota(jnp.int32, (PAD_SLOT, CHUNK), 0).astype(jnp.bfloat16)
         at_left = p_iota == pad
-        at_right = p_iota == pad + 1
+        at_right = p_iota == pad + one
         parts = []
         for k in range(4):
             parts.append(
-                jnp.where(at_left, dep[k : k + 1], jnp.where(at_right, dep[4 + k : 5 + k], 0.0))
+                jnp.where(at_left, dep[k : k + 1], jnp.where(at_right, dep[4 + k : 5 + k], zero))
             )
-        spread = jnp.concatenate(parts, 0).astype(jnp.bfloat16)
+        spread = jnp.concatenate(parts, 0)
         out_ref[...] += lax.dot_general(
-            onehot, spread, (((1,), (1,)), ((), ())), preferred_element_type=jnp.float32
+            spread, onehot, (((1,), (1,)), ((), ())), preferred_element_type=jnp.float32
         )
         return carry
 
@@ -72,13 +74,13 @@
     flops = 2 * cell_rows * 4 * PAD_SLOT * sources * length
     return pl.pallas_call(
         functools.partial(hist_kernel, cell_rows),
-        out_shape=jax.ShapeDtypeStruct((cell_rows, 4 * PAD_SLOT), jnp.float32),
+        out_shape=jax.ShapeDtypeStruct((4 * PAD_SLOT, cell_rows), jnp.float32),
         grid=(sources,),
         in_specs=[
             pl.BlockSpec((1, 2, length), lambda s: (s, 0, 0)),
             pl.BlockSpec((1, 8, length), lambda s: (s, 0, 0)),
         ],
-        out_specs=pl.BlockSpec((cell_rows, 4 * PAD_SLOT), lambda s: (0, 0)),
+        out_specs=pl.BlockSpec((4 * PAD_SLOT, cell_rows), lambda s: (0, 0)),
         compiler_params=pltpu.CompilerParams(dimension_semantics=("arbitrary",)),
         cost_estimate=pl.CostEstimate(
             flops=flops,
@@ -162,7 +164,7 @@
         1,
     ).astype(jnp.bfloat16).astype(jnp.float32)
     raw = build_histogram(idx, dep, cell_rows)
-    histogram = raw.reshape(cell_rows, 4, PAD_SLOT)[:cell_count, :, :PAD]
+    histogram = raw.T.reshape(cell_rows, 4, PAD_SLOT)[:cell_count, :, :PAD]
     histogram = histogram.reshape(drift_dev, row_dev, 4, PAD)
     means = histogram[:, :, 1:4] / (histogram[:, :, 0:1] + 1.0)
     means = jnp.transpose(means, (2, 0, 1, 3))

time: 109 us -> 90.3 us (0.83)
  Pallas kernels: 35.3 us -> 16.4 us
    pallas_call x1, Pallas kernels: 35.3 us -> 16.4 us  [build_histogram(): pl.pallas_call(functools.partial(hist_kernel, cell_rows), out_shape=jax.S...]
    reshape x1 -> x0, local copies, waits for them, and re-layouts: 1.5 us -> none  [per_device(): histogram = raw.reshape(cell_rows, 4, PAD_SLOT)[:cell_count, :, :PAD]]
where the time goes in v2:
time: 90.3 us; the launch traced here: 88.9 us
  starting transfers between devices  33 us (37%)
  waiting for transfers between devices  23 us (25%)
  Pallas kernels  16.4 us (18%)
  local copies, waits for them, and re-layouts  6.6 us (7%)
  other arithmetic  5.96 us (7%)
  matrix products  3.59 us (4%)
    ppermute x7, starting transfers between devices, exclusive_prefix(): got = lax.ppermute(totals, 'gz', pairs)  17.3 us
    pallas_call x1, Pallas kernels, build_histogram(): pl.pallas_call(functools.partial(hist_kernel, cell_rows), out_shape=jax.S...  16.4 us
    all_to_all x1, waiting for transfers between devices, per_device(): incoming = lax.all_to_all(outgoing, 'tf', 0, 0, tiled=True)  9.42 us
    ppermute x7, waiting for transfers between devices, exclusive_prefix(): got = lax.ppermute(totals, 'gz', pairs)  9.07 us
    ppermute x3, starting transfers between devices, exclusive_prefix(): before = before + lax.ppermute(row_sum, 'tf', pairs)  7.13 us
    all_to_all x1, starting transfers between devices, per_device(): incoming = lax.all_to_all(outgoing, 'tf', 0, 0, tiled=True)  4.29 us
    unnamed x1, matrix products  3.59 us
    ppermute x1, waiting for transfers between devices, with_halo(): lax.ppermute(lax.slice_in_dim(block, block.shape[dim] - width, None, axis...  2.98 us
  transfers between devices with their start and end apart: 13, of which 6 were waited for; matrix products, arithmetic and copies ran while one was open for 0% of the time, Pallas kernels for 0%

profile of v2, /device:TPU:8, one launch (start us, length us, event | category | flops | bytes accessed | tf_op | source)
XLA Modules:
  0.0 88.9 jit_solution(15839521759284989057)
XLA Ops:
  0.0 1.1 %fusion.23 = (bf16[4,1,8192]{2,0,1:T(4,128)(2,1)S(1)}, s32[1,1,1,1,4,8192]{5,4,3,2,1,0:T(4,128)S(1)}, s32[1,1,1,1,4,8192]{5,4,3,2,1,0:T(4,128)S(1)}) fusion(s32[3,1,1,1,4,8192]{5,4,3,2,1,0:T(4,128)} %param.8, s32[]{:T(128)S(6)} %mul.84), kind=kLoop, calls=%fused_computation.51 | loop fusion | flops 65536 | bytes 720900 | tf_op jit(solution)/shard_map/convert_element_type | solution.py:139
  2.0 2.0 %concatenate.12 = bf16[4,7,8192]{2,1,0:T(8,128)(2,1)} concatenate(bf16[4,1,8192]{2,1,0:T(2,128)(2,1)S(1)} %fusion.20, bf16[4,1,8192]{2,1,0:T(2,128)(2,1)S(1)} %copy.33, bf16[4,3,8192]{2,1,0:T(4,128)(2,1)S(1)} %bitcast.42, bf16[4,1,8192]{2,1,0:T(2,128)(2,1)S(1)} %copy.34, bf16[4,1,8192]{2,1,0:T(2,128)(2,1)S(1)} %copy.35), dimensions={1} | concatenate | bytes 917504 | tf_op jit(solution)/shard_map/concatenate | solution.py:136
  4.0 4.3 %all-to-all-start = ((bf16[4,7,8192]{2,1,0:T(8,128)(2,1)}), bf16[4,7,8192]{2,1,0:T(8,128)(2,1)S(1)}, u32[]{:S(2)}, u32[]{:S(2)}) async-start(bf16[4,7,8192]{2,1,0:T(8,128)(2,1)} %concatenate.12), calls=%async_computation | async-start | bytes 1048576 | tf_op jit(solution)/shard_map/all_to_all | solution.py:146
  8.4 9.4 %all-to-all-done = bf16[4,7,8192]{2,1,0:T(8,128)(2,1)S(1)} async-done(((bf16[4,7,8192]{2,1,0:T(8,128)(2,1)}), bf16[4,7,8192]{2,1,0:T(8,128)(2,1)S(1)}, u32[]{:S(2)}, u32[]{:S(2)}) %all-to-all-start) | async-done | bytes 458784 | tf_op jit(solution)/shard_map/all_to_all | solution.py:146
  19.3 1.6 %stack.3 = bf16[4,8,8192]{2,1,0:T(8,128)(2,1)S(1)} concatenate(bf16[4,1,8192]{2,1,0:T(2,128)(2,1)S(1)} %get-tuple-element.23, bf16[4,1,8192]{2,1,0:T(2,128)(2,1)S(1)} %get-tuple-element.14, bf16[4,1,8192]{2,1,0:T(2,128)(2,1)S(1)} %get-tuple-element.13, bf16[4,1,8192]{2,1,0:T(2,128)(2,1)S(1)} %get-tuple-element.15, bf16[4,1,8192]{2,1,0:T(2,128)(2,1)S(1)} %get-tuple-element.22, ...), dimensions={1} | concatenate | bytes 1048576 | tf_op jit(solution)/shard_map/stack | solution.py:153
  20.9 1.0 %convert_element_type.49.dep_ref = f32[4,8,8192]{2,1,0:T(8,128)} convert(bf16[4,8,8192]{2,1,0:T(8,128)(2,1)S(1)} %stack.3) | non-fusion elementwise | flops 262144 | bytes 1572864 | tf_op jit(solution)/shard_map/convert_element_type | solution.py:165
  22.7 16.4 %shard_map.55 = f32[768,160]{1,0:T(8,128)} custom-call(s32[4,2,8192]{2,1,0:T(2,128)} %slice_convert_fusion.1.idx_ref, f32[4,8,8192]{2,1,0:T(8,128)} %convert_element_type.49.dep_ref), custom_call_target="tpu_custom_call" | custom-call | flops 8053063680 | bytes 1802240 | tf_op jit(solution)/shard_map/pallas_call | solution.py:75
  39.2 1.2 %slice.95 = f32[152,4,180]{0,2,1:T(8,128)S(1)} slice(f32[160,4,192]{0,2,1:T(8,128)} %bitcast.43), slice={[0:152], [0:4], [0:180]} | slice | bytes 875520 | tf_op jit(solution)/shard_map/slice | solution.py:167
  41.1 3.6 %fusion.5 = f32[3,8,19,180]{3,1,0,2:T(8,128)S(1)} fusion(f32[19]{0:T(128)S(1)} %get-tuple-element.25, f32[180,180]{1,0:T(8,128)S(1)} %abs_convert_fusion, f32[19]{0:T(128)S(1)} %get-tuple-element.24, f32[3,8,19,180]{3,0,2,1:T(4,128)S(1)} %fusion.6), kind=kOutput, calls=%fused_computation.6 | convolution fusion | flops 179139600 | bytes 786392
  44.8 1.9 %collective-permute-start.1 = (f32[3,8,2,180]{3,1,0,2:T(8,128)S(1)}, f32[3,8,2,180]{3,1,0,2:T(8,128)S(1)}, u32[]{:S(2)}, u32[]{:S(2)}) collective-permute-start(f32[3,8,2,180]{3,1,0,2:T(8,128)S(1)} %get-tuple-element.18), channel_id=1, source_target_pairs={{1,0},{2,1},{3,2},{4,3},{5,4},{6,5},{7,6},{9,8},{10,9},{11,10},{12... | collective-permute-start | bytes 103688 | tf_op jit(solution)/shard_map/ppermute | solution.py:24
  46.7 2.4 %collective-permute-start = (f32[3,8,2,180]{3,1,0,2:T(8,128)S(1)}, f32[3,8,2,180]{3,1,0,2:T(8,128)S(1)}, u32[]{:S(2)}, u32[]{:S(2)}) collective-permute-start(f32[3,8,2,180]{3,1,0,2:T(8,128)S(1)} %get-tuple-element.17), channel_id=1, source_target_pairs={{0,1},{1,2},{2,3},{3,4},{4,5},{5,6},{6,7},{8,9},{9,10},{10,11},{11... | collective-permute-start | bytes 103688 | tf_op jit(solution)/shard_map/ppermute | solution.py:21
  49.1 3.0 %collective-permute-done = f32[3,8,2,180]{3,1,0,2:T(8,128)S(1)} collective-permute-done((f32[3,8,2,180]{3,1,0,2:T(8,128)S(1)}, f32[3,8,2,180]{3,1,0,2:T(8,128)S(1)}, u32[]{:S(2)}, u32[]{:S(2)}) %collective-permute-start) | collective-permute-done | bytes 34592 | tf_op jit(solution)/shard_map/ppermute | solution.py:21
  52.4 5.9 %collective-permute-start.8 = (f32[3,19,180]{2,0,1:T(4,128)S(1)}, f32[3,19,180]{2,0,1:T(4,128)S(1)}, u32[]{:S(2)}, u32[]{:S(2)}) collective-permute-start(f32[3,19,180]{2,0,1:T(4,128)S(1)} %get-tuple-element.5), channel_id=1, source_target_pairs={{0,56},{8,0},{16,8},{24,16},{32,24},{40,32},{48,40},{56,48},{1,57}... | collective-permute-start | bytes 123128 | tf_op jit(solution)/shard_map/ppermute | solution.py:101
  58.3 1.5 %collective-permute-start.7 = (f32[3,19,180]{2,0,1:T(4,128)S(1)}, f32[3,19,180]{2,0,1:T(4,128)S(1)}, u32[]{:S(2)}, u32[]{:S(2)}) collective-permute-start(f32[3,19,180]{2,0,1:T(4,128)S(1)} %get-tuple-element.5), channel_id=1, source_target_pairs={{0,48},{8,56},{16,0},{24,8},{32,16},{40,24},{48,32},{56,40},{1,49}... | collective-permute-start | bytes 123128 | tf_op jit(solution)/shard_map/ppermute | solution.py:101
  60.2 5.0 %collective-permute-start.5 = (f32[3,19,180]{2,0,1:T(4,128)S(1)}, f32[3,19,180]{2,0,1:T(4,128)S(1)}, u32[]{:S(2)}, u32[]{:S(2)}) collective-permute-start(f32[3,19,180]{2,0,1:T(4,128)S(1)} %get-tuple-element.5), channel_id=1, source_target_pairs={{0,32},{8,40},{16,48},{24,56},{32,0},{40,8},{48,16},{56,24},{1,33}... | collective-permute-start | bytes 123128 | tf_op jit(solution)/shard_map/ppermute | solution.py:101
  65.2 2.5 %collective-permute-start.3 = (f32[3,19,180]{2,0,1:T(4,128)S(1)}, f32[3,19,180]{2,0,1:T(4,128)S(1)}, u32[]{:S(2)}, u32[]{:S(2)}) collective-permute-start(f32[3,19,180]{2,0,1:T(4,128)S(1)} %get-tuple-element.5), channel_id=1, source_target_pairs={{0,16},{8,24},{16,32},{24,40},{32,48},{40,56},{48,0},{56,8},{1,17}... | collective-permute-start | bytes 123128 | tf_op jit(solution)/shard_map/ppermute | solution.py:101
  67.7 1.9 %collective-permute-start.2 = (f32[3,19,180]{2,0,1:T(4,128)S(1)}, f32[3,19,180]{2,0,1:T(4,128)S(1)}, u32[]{:S(2)}, u32[]{:S(2)}) collective-permute-start(f32[3,19,180]{2,0,1:T(4,128)S(1)} %get-tuple-element.5), channel_id=1, source_target_pairs={{0,8},{8,16},{16,24},{24,32},{32,40},{40,48},{48,56},{56,0},{1,9},... | collective-permute-start | bytes 123128 | tf_op jit(solution)/shard_map/ppermute | solution.py:101
  69.6 1.8 %collective-permute-done.6 = f32[3,19,180]{2,0,1:T(4,128)S(1)} collective-permute-done((f32[3,19,180]{2,0,1:T(4,128)S(1)}, f32[3,19,180]{2,0,1:T(4,128)S(1)}, u32[]{:S(2)}, u32[]{:S(2)}) %collective-permute-start.6) | collective-permute-done | bytes 41072 | tf_op jit(solution)/shard_map/ppermute | solution.py:101
  71.5 4.7 %collective-permute-done.4 = f32[3,19,180]{2,0,1:T(4,128)S(1)} collective-permute-done((f32[3,19,180]{2,0,1:T(4,128)S(1)}, f32[3,19,180]{2,0,1:T(4,128)S(1)}, u32[]{:S(2)}, u32[]{:S(2)}) %collective-permute-start.4) | collective-permute-done | bytes 41072 | tf_op jit(solution)/shard_map/ppermute | solution.py:101
  76.2 2.5 %collective-permute-done.3 = f32[3,19,180]{2,0,1:T(4,128)S(1)} collective-permute-done((f32[3,19,180]{2,0,1:T(4,128)S(1)}, f32[3,19,180]{2,0,1:T(4,128)S(1)}, u32[]{:S(2)}, u32[]{:S(2)}) %collective-permute-start.3) | collective-permute-done | bytes 41072 | tf_op jit(solution)/shard_map/ppermute | solution.py:101
  78.8 3.1 %collective-permute-start.11 = (f32[3,19,180]{2,0,1:T(4,128)S(1)}, f32[3,19,180]{2,0,1:T(4,128)S(1)}, u32[]{:S(2)}, u32[]{:S(2)}) collective-permute-start(f32[3,19,180]{2,0,1:T(4,128)S(1)} %add_add_fusion.1), channel_id=1, source_target_pairs={{0,192},{1,193},{2,194},{3,195},{4,196},{5,197},{6,198},{7,199},{8... | collective-permute-start | bytes 123128 | tf_op jit(solution)/shard_map/ppermute | solution.py:106
  81.8 1.3 %collective-permute-start.10 = (f32[3,19,180]{2,0,1:T(4,128)S(1)}, f32[3,19,180]{2,0,1:T(4,128)S(1)}, u32[]{:S(2)}, u32[]{:S(2)}) collective-permute-start(f32[3,19,180]{2,0,1:T(4,128)S(1)} %add_add_fusion.1), channel_id=1, source_target_pairs={{0,128},{64,192},{1,129},{65,193},{2,130},{66,194},{3,131},{67,195... | collective-permute-start | bytes 123128 | tf_op jit(solution)/shard_map/ppermute | solution.py:106
  83.2 2.8 %collective-permute-start.9 = (f32[3,19,180]{2,0,1:T(4,128)S(1)}, f32[3,19,180]{2,0,1:T(4,128)S(1)}, u32[]{:S(2)}, u32[]{:S(2)}) collective-permute-start(f32[3,19,180]{2,0,1:T(4,128)S(1)} %add_add_fusion.1), channel_id=1, source_target_pairs={{0,64},{64,128},{128,192},{1,65},{65,129},{129,193},{2,66},{66,130... | collective-permute-start | bytes 123128 | tf_op jit(solution)/shard_map/ppermute | solution.py:106
  86.4 1.5 %collective-permute-done.9 = f32[3,19,180]{2,0,1:T(4,128)S(1)} collective-permute-done((f32[3,19,180]{2,0,1:T(4,128)S(1)}, f32[3,19,180]{2,0,1:T(4,128)S(1)}, u32[]{:S(2)}, u32[]{:S(2)}) %collective-permute-start.9) | collective-permute-done | bytes 41072 | tf_op jit(solution)/shard_map/ppermute | solution.py:106
  (42 shorter events, 6.1 us)
Async XLA Ops:
  0.0 1.3 %copy-start = (bf16[3,1,1,1,4,8192]{5,4,3,2,1,0:T(4,128)(2,1)S(1)}, bf16[3,1,1,1,4,8192]{5,4,3,2,1,0:T(4,128)(2,1)}, u32[]{:S(2)}) copy-start(bf16[3,1,1,1,4,8192]{5,4,3,2,1,0:T(4,128)(2,1)} %param.5) | copy-start | bytes 589828
  0.0 1.5 %copy-start.1 = (bf16[1,1,1,4,8192]{4,3,2,1,0:T(4,128)(2,1)S(1)}, bf16[1,1,1,4,8192]{4,3,2,1,0:T(4,128)(2,1)}, u32[]{:S(2)}) copy-start(bf16[1,1,1,4,8192]{4,3,2,1,0:T(4,128)(2,1)} %param.6) | copy-start | bytes 196612
  0.0 1.6 %copy-start.2 = (bf16[1,1,1,4,8192]{4,3,2,1,0:T(4,128)(2,1)S(1)}, bf16[1,1,1,4,8192]{4,3,2,1,0:T(4,128)(2,1)}, u32[]{:S(2)}) copy-start(bf16[1,1,1,4,8192]{4,3,2,1,0:T(4,128)(2,1)} %param.7) | copy-start | bytes 196612
  2.0 6.4 %copy-start.3 = (s32[19]{0:T(128)S(1)}, s32[19]{0:T(128)}, u32[]{:S(2)}) copy-start(s32[19]{0:T(128)} %param.9) | copy-start | bytes 232
  4.0 13.8 %all-to-all-start = ((bf16[4,7,8192]{2,1,0:T(8,128)(2,1)}), bf16[4,7,8192]{2,1,0:T(8,128)(2,1)S(1)}, u32[]{:S(2)}, u32[]{:S(2)}) async-start(bf16[4,7,8192]{2,1,0:T(8,128)(2,1)} %concatenate.12), calls=%async_computation | async-start | bytes 1048576 | tf_op jit(solution)/shard_map/all_to_all | solution.py:146
  44.8 4.3 %collective-permute-start.1 = (f32[3,8,2,180]{3,1,0,2:T(8,128)S(1)}, f32[3,8,2,180]{3,1,0,2:T(8,128)S(1)}, u32[]{:S(2)}, u32[]{:S(2)}) collective-permute-start(f32[3,8,2,180]{3,1,0,2:T(8,128)S(1)} %get-tuple-element.18), channel_id=1, source_target_pairs={{1,0},{2,1},{3,2},{4,3},{5,4},{6,5},{7,6},{9,8},{10,9},{11,10},{12... | collective-permute-start | bytes 103688 | tf_op jit(solution)/shard_map/ppermute | solution.py:24
  46.7 5.4 %collective-permute-start = (f32[3,8,2,180]{3,1,0,2:T(8,128)S(1)}, f32[3,8,2,180]{3,1,0,2:T(8,128)S(1)}, u32[]{:S(2)}, u32[]{:S(2)}) collective-permute-start(f32[3,8,2,180]{3,1,0,2:T(8,128)S(1)} %get-tuple-element.17), channel_id=1, source_target_pairs={{0,1},{1,2},{2,3},{3,4},{4,5},{5,6},{6,7},{8,9},{9,10},{10,11},{11... | collective-permute-start | bytes 103688 | tf_op jit(solution)/shard_map/ppermute | solution.py:21
  52.4 12.9 %collective-permute-start.8 = (f32[3,19,180]{2,0,1:T(4,128)S(1)}, f32[3,19,180]{2,0,1:T(4,128)S(1)}, u32[]{:S(2)}, u32[]{:S(2)}) collective-permute-start(f32[3,19,180]{2,0,1:T(4,128)S(1)} %get-tuple-element.5), channel_id=1, source_target_pairs={{0,56},{8,0},{16,8},{24,16},{32,24},{40,32},{48,40},{56,48},{1,57}... | collective-permute-start | bytes 123128 | tf_op jit(solution)/shard_map/ppermute | solution.py:101
  58.3 9.4 %collective-permute-start.7 = (f32[3,19,180]{2,0,1:T(4,128)S(1)}, f32[3,19,180]{2,0,1:T(4,128)S(1)}, u32[]{:S(2)}, u32[]{:S(2)}) collective-permute-start(f32[3,19,180]{2,0,1:T(4,128)S(1)} %get-tuple-element.5), channel_id=1, source_target_pairs={{0,48},{8,56},{16,0},{24,8},{32,16},{40,24},{48,32},{56,40},{1,49}... | collective-permute-start | bytes 123128 | tf_op jit(solution)/shard_map/ppermute | solution.py:101
  59.7 11.7 %collective-permute-start.6 = (f32[3,19,180]{2,0,1:T(4,128)S(1)}, f32[3,19,180]{2,0,1:T(4,128)S(1)}, u32[]{:S(2)}, u32[]{:S(2)}) collective-permute-start(f32[3,19,180]{2,0,1:T(4,128)S(1)} %get-tuple-element.5), channel_id=1, source_target_pairs={{0,40},{8,48},{16,56},{24,0},{32,8},{40,16},{48,24},{56,32},{1,41}... | collective-permute-start | bytes 123128 | tf_op jit(solution)/shard_map/ppermute | solution.py:101
  60.2 11.3 %collective-permute-start.5 = (f32[3,19,180]{2,0,1:T(4,128)S(1)}, f32[3,19,180]{2,0,1:T(4,128)S(1)}, u32[]{:S(2)}, u32[]{:S(2)}) collective-permute-start(f32[3,19,180]{2,0,1:T(4,128)S(1)} %get-tuple-element.5), channel_id=1, source_target_pairs={{0,32},{8,40},{16,48},{24,56},{32,0},{40,8},{48,16},{56,24},{1,33}... | collective-permute-start | bytes 123128 | tf_op jit(solution)/shard_map/ppermute | solution.py:101
  65.2 10.9 %collective-permute-start.4 = (f32[3,19,180]{2,0,1:T(4,128)S(1)}, f32[3,19,180]{2,0,1:T(4,128)S(1)}, u32[]{:S(2)}, u32[]{:S(2)}) collective-permute-start(f32[3,19,180]{2,0,1:T(4,128)S(1)} %get-tuple-element.5), channel_id=1, source_target_pairs={{0,24},{8,32},{16,40},{24,48},{32,56},{40,0},{48,8},{56,16},{1,25}... | collective-permute-start | bytes 123128 | tf_op jit(solution)/shard_map/ppermute | solution.py:101
  65.2 13.4 %collective-permute-start.3 = (f32[3,19,180]{2,0,1:T(4,128)S(1)}, f32[3,19,180]{2,0,1:T(4,128)S(1)}, u32[]{:S(2)}, u32[]{:S(2)}) collective-permute-start(f32[3,19,180]{2,0,1:T(4,128)S(1)} %get-tuple-element.5), channel_id=1, source_target_pairs={{0,16},{8,24},{16,32},{24,40},{32,48},{40,56},{48,0},{56,8},{1,17}... | collective-permute-start | bytes 123128 | tf_op jit(solution)/shard_map/ppermute | solution.py:101
  67.7 11.0 %collective-permute-start.2 = (f32[3,19,180]{2,0,1:T(4,128)S(1)}, f32[3,19,180]{2,0,1:T(4,128)S(1)}, u32[]{:S(2)}, u32[]{:S(2)}) collective-permute-start(f32[3,19,180]{2,0,1:T(4,128)S(1)} %get-tuple-element.5), channel_id=1, source_target_pairs={{0,8},{8,16},{16,24},{24,32},{32,40},{40,48},{48,56},{56,0},{1,9},... | collective-permute-start | bytes 123128 | tf_op jit(solution)/shard_map/ppermute | solution.py:101
  78.8 7.6 %collective-permute-start.11 = (f32[3,19,180]{2,0,1:T(4,128)S(1)}, f32[3,19,180]{2,0,1:T(4,128)S(1)}, u32[]{:S(2)}, u32[]{:S(2)}) collective-permute-start(f32[3,19,180]{2,0,1:T(4,128)S(1)} %add_add_fusion.1), channel_id=1, source_target_pairs={{0,192},{1,193},{2,194},{3,195},{4,196},{5,197},{6,198},{7,199},{8... | collective-permute-start | bytes 123128 | tf_op jit(solution)/shard_map/ppermute | solution.py:106
  81.8 4.5 %collective-permute-start.10 = (f32[3,19,180]{2,0,1:T(4,128)S(1)}, f32[3,19,180]{2,0,1:T(4,128)S(1)}, u32[]{:S(2)}, u32[]{:S(2)}) collective-permute-start(f32[3,19,180]{2,0,1:T(4,128)S(1)} %add_add_fusion.1), channel_id=1, source_target_pairs={{0,128},{64,192},{1,129},{65,193},{2,130},{66,194},{3,131},{67,195... | collective-permute-start | bytes 123128 | tf_op jit(solution)/shard_map/ppermute | solution.py:106
  83.2 4.8 %collective-permute-start.9 = (f32[3,19,180]{2,0,1:T(4,128)S(1)}, f32[3,19,180]{2,0,1:T(4,128)S(1)}, u32[]{:S(2)}, u32[]{:S(2)}) collective-permute-start(f32[3,19,180]{2,0,1:T(4,128)S(1)} %add_add_fusion.1), channel_id=1, source_target_pairs={{0,64},{64,128},{128,192},{1,65},{65,129},{129,193},{2,66},{66,130... | collective-permute-start | bytes 123128 | tf_op jit(solution)/shard_map/ppermute | solution.py:106

commit v3 on v2

--- a/solution.py
+++ b/solution.py
@@ -34,22 +34,29 @@
     return jnp.maximum(spread + 1.0 - distance, 0.0) / ((spread + 1.0) * (spread + 1.0))
 
 
-def hist_kernel(cell_rows, idx_ref, dep_ref, out_ref):
-    source = pl.program_id(0)
+def hist_kernel(cell_rows, first, order_ref, rows_ref, *rest):
+    out_ref = rest[-1]
 
-    @pl.when(source == 0)
+    @pl.when(pl.program_id(0) == 0)
     def _():
-        out_ref[...] = jnp.zeros_like(out_ref)
+        if first:
+            out_ref[...] = jnp.zeros_like(out_ref)
+        else:
+            out_ref[...] = rest[0][...]
 
-    length = idx_ref.shape[2]
+    length = rows_ref.shape[2]
     zero = jnp.zeros((), jnp.bfloat16)
     one = jnp.ones((), jnp.bfloat16)
 
     def body(step, carry):
         off = pl.multiple_of(step * CHUNK, CHUNK)
-        cell = idx_ref[0, 0:1, pl.ds(off, CHUNK)].astype(jnp.bfloat16)
-        pad = idx_ref[0, 1:2, pl.ds(off, CHUNK)].astype(jnp.bfloat16)
-        dep = dep_ref[0, :, pl.ds(off, CHUNK)].astype(jnp.bfloat16)
+        rows = rows_ref[0, :, pl.ds(off, CHUNK)].astype(jnp.float32)
+        cell = rows[0:1].astype(jnp.bfloat16)
+        pad = rows[1:2].astype(jnp.bfloat16)
+        weight_now = rows[5:6]
+        share = rows[6:7]
+        left_share = weight_now * (1.0 - share)
+        right_share = weight_now * share
         c_iota = lax.broadcasted_iota(jnp.int32, (cell_rows, CHUNK), 0).astype(jnp.bfloat16)
         onehot = jnp.where(c_iota == cell, one, zero)
         p_iota = lax.broadcasted_iota(jnp.int32, (PAD_SLOT, CHUNK), 0).astype(jnp.bfloat16)
@@ -57,9 +64,13 @@
         at_right = p_iota == pad + one
         parts = []
         for k in range(4):
-            parts.append(
-                jnp.where(at_left, dep[k : k + 1], jnp.where(at_right, dep[4 + k : 5 + k], zero))
-            )
+            if k == 0:
+                left, right = left_share, right_share
+            else:
+                left, right = left_share * rows[k + 1 : k + 2], right_share * rows[k + 1 : k + 2]
+            left = left.astype(jnp.bfloat16)
+            right = right.astype(jnp.bfloat16)
+            parts.append(jnp.where(at_left, left, jnp.where(at_right, right, zero)))
         spread = jnp.concatenate(parts, 0)
         out_ref[...] += lax.dot_general(
             spread, onehot, (((1,), (1,)), ((), ())), preferred_element_type=jnp.float32
@@ -69,25 +80,34 @@
     lax.fori_loop(0, length // CHUNK, body, 0)
 
 
-def build_histogram(idx, dep, cell_rows):
-    sources, _, length = idx.shape
-    flops = 2 * cell_rows * 4 * PAD_SLOT * sources * length
+def build_histogram(order, rows, steps, cell_rows, partial=None):
+    sources, features, length = rows.shape
+    first = partial is None
+    flops = 2 * cell_rows * 4 * PAD_SLOT * steps * length
+    in_specs = [pl.BlockSpec((1, features, length), lambda s, o: (o[s], 0, 0))]
+    operands = [order, rows]
+    aliases = {}
+    if not first:
+        in_specs.append(pl.BlockSpec((4 * PAD_SLOT, cell_rows), lambda s, o: (0, 0)))
+        operands.append(partial)
+        aliases = {2: 0}
     return pl.pallas_call(
-        functools.partial(hist_kernel, cell_rows),
+        functools.partial(hist_kernel, cell_rows, first),
         out_shape=jax.ShapeDtypeStruct((4 * PAD_SLOT, cell_rows), jnp.float32),
-        grid=(sources,),
-        in_specs=[
-            pl.BlockSpec((1, 2, length), lambda s: (s, 0, 0)),
-            pl.BlockSpec((1, 8, length), lambda s: (s, 0, 0)),
-        ],
-        out_specs=pl.BlockSpec((4 * PAD_SLOT, cell_rows), lambda s: (0, 0)),
+        grid_spec=pltpu.PrefetchScalarGridSpec(
+            num_scalar_prefetch=1,
+            grid=(steps,),
+            in_specs=in_specs,
+            out_specs=pl.BlockSpec((4 * PAD_SLOT, cell_rows), lambda s, o: (0, 0)),
+        ),
+        input_output_aliases=aliases,
         compiler_params=pltpu.CompilerParams(dimension_semantics=("arbitrary",)),
         cost_estimate=pl.CostEstimate(
             flops=flops,
             transcendentals=0,
-            bytes_accessed=sources * length * 40 + cell_rows * 4 * PAD_SLOT * 4,
+            bytes_accessed=steps * length * features * 2 + cell_rows * 4 * PAD_SLOT * 8,
         ),
-    )(idx, dep)
+    )(*operands)
 
 
 def exclusive_prefix(totals):
@@ -144,26 +164,11 @@
         1,
     )
     incoming = lax.all_to_all(outgoing, "tf", 0, 0, tiled=True)
-    idx = incoming[:, 0:2].astype(jnp.int32)
-    values = incoming[:, 2:].astype(jnp.float32)
-    weight_now = values[:, 3]
-    share = values[:, 4]
-    left_share = weight_now * (1.0 - share)
-    right_share = weight_now * share
-    dep = jnp.stack(
-        [
-            left_share,
-            left_share * values[:, 0],
-            left_share * values[:, 1],
-            left_share * values[:, 2],
-            right_share,
-            right_share * values[:, 0],
-            right_share * values[:, 1],
-            right_share * values[:, 2],
-        ],
-        1,
-    ).astype(jnp.bfloat16).astype(jnp.float32)
-    raw = build_histogram(idx, dep, cell_rows)
+    tf_count = lax.axis_size("tf")
+    here = lax.axis_index("tf")
+    local = build_histogram(here[None], outgoing, 1, cell_rows)
+    others = (here + lax.broadcasted_iota(jnp.int32, (tf_count - 1,), 0) + 1) % tf_count
+    raw = build_histogram(others, incoming, tf_count - 1, cell_rows, local)
     histogram = raw.T.reshape(cell_rows, 4, PAD_SLOT)[:cell_count, :, :PAD]
     histogram = histogram.reshape(drift_dev, row_dev, 4, PAD)
     means = histogram[:, :, 1:4] / (histogram[:, :, 0:1] + 1.0)

time: 90.3 us -> 84.5 us (0.936)
  waiting for transfers between devices: 23 us -> 16.1 us
  Pallas kernels: 16.4 us -> 19.2 us
  other arithmetic: 5.96 us -> 3.18 us
  starting transfers between devices: 33 us -> 34.8 us
    all_to_all x1, waiting for transfers between devices: 9.42 us -> 3.4 us  [per_device(): incoming = lax.all_to_all(outgoing, 'tf', 0, 0, tiled=True)]
    ppermute x1, waiting for transfers between devices: 2.98 us -> 0.01 us  [with_halo(): lax.ppermute(lax.slice_in_dim(block, block.shape[dim] - width, None, axis...]
    pallas_call x1 -> x2, Pallas kernels: 16.4 us -> 19.2 us  [build_histogram(): pl.pallas_call(functools.partial(hist_kernel, cell_rows, first), out_shap...]
    convert_element_type x3 -> x0, other arithmetic: 1.96 us -> none  [the longest x1 1.05 us: per_device(): dep = jnp.stack([left_share, left_share * values[:, 0], left_share * valu...]
    ppermute x1, starting transfers between devices: 1.92 us -> 3.64 us  [with_halo(): lax.ppermute(lax.slice_in_dim(block, 0, width, axis=dim), axis, backward)]
    ppermute x1, waiting for transfers between devices: 0.01 us -> 1.72 us  [with_halo(): lax.ppermute(lax.slice_in_dim(block, 0, width, axis=dim), axis, backward)]
    another operation x1 -> x0, local copies, waits for them, and re-layouts: 1.6 us -> none  [per_device(): jnp.stack([left_share, left_share * values[:, 0], left_share * values[:,...]
    another operation x3 -> x0, other arithmetic: 1.37 us -> none
  transfers between devices with their start and end apart: 13 -> 13, of which waited for: 6 -> 8; matrix products, arithmetic and copies ran while one was open for 0% -> 1% of each run, Pallas kernels for 0% -> 7%
where the time goes in v3:
time: 84.5 us; the launch traced here: 82.9 us
  starting transfers between devices  34.8 us (41%)
  Pallas kernels  19.2 us (23%)
  waiting for transfers between devices  16.1 us (19%)
  local copies, waits for them, and re-layouts  5.81 us (7%)
  matrix products  3.59 us (4%)
  other arithmetic  3.18 us (4%)
    pallas_call x2, Pallas kernels, build_histogram(): pl.pallas_call(functools.partial(hist_kernel, cell_rows, first), out_shap...  19.2 us
    ppermute x7, starting transfers between devices, exclusive_prefix(): got = lax.ppermute(totals, 'gz', pairs)  18.5 us
    ppermute x7, waiting for transfers between devices, exclusive_prefix(): got = lax.ppermute(totals, 'gz', pairs)  9.42 us
    ppermute x3, starting transfers between devices, exclusive_prefix(): before = before + lax.ppermute(row_sum, 'tf', pairs)  6.51 us
    all_to_all x1, starting transfers between devices, per_device(): incoming = lax.all_to_all(outgoing, 'tf', 0, 0, tiled=True)  4.29 us
    ppermute x1, starting transfers between devices, with_halo(): lax.ppermute(lax.slice_in_dim(block, 0, width, axis=dim), axis, backward)  3.64 us
    unnamed x1, matrix products  3.59 us
    all_to_all x1, waiting for transfers between devices, per_device(): incoming = lax.all_to_all(outgoing, 'tf', 0, 0, tiled=True)  3.4 us
  transfers between devices with their start and end apart: 13, of which 8 were waited for; matrix products, arithmetic and copies ran while one was open for 1% of the time, Pallas kernels for 7%

profile of v3, /device:TPU:8, one launch (start us, length us, event | category | flops | bytes accessed | tf_op | source)
XLA Modules:
  0.0 82.9 jit_solution(6945475008488142836)
XLA Ops:
  0.0 1.1 %fusion.23 = (bf16[4,1,8192]{2,0,1:T(4,128)(2,1)S(1)}, s32[1,1,1,1,4,8192]{5,4,3,2,1,0:T(4,128)S(1)}, s32[1,1,1,1,4,8192]{5,4,3,2,1,0:T(4,128)S(1)}) fusion(s32[3,1,1,1,4,8192]{5,4,3,2,1,0:T(4,128)} %param.8, s32[]{:T(128)S(6)} %mul.46), kind=kLoop, calls=%fused_computation.41 | loop fusion | flops 65536 | bytes 720900 | tf_op jit(solution)/shard_map/convert_element_type | solution.py:159
  2.0 2.0 %concatenate.12.rows_ref = bf16[4,7,8192]{2,1,0:T(8,128)(2,1)} concatenate(bf16[4,1,8192]{2,1,0:T(2,128)(2,1)S(1)} %fusion.20, bf16[4,1,8192]{2,1,0:T(2,128)(2,1)S(1)} %copy.34, bf16[4,3,8192]{2,1,0:T(4,128)(2,1)S(1)} %bitcast.43, bf16[4,1,8192]{2,1,0:T(2,128)(2,1)S(1)} %copy.35, bf16[4,1,8192]{2,1,0:T(2,128)(2,1)S(1)} %copy.36), dimensions={1} | concatenate | bytes 917504 | tf_op jit(solution)/shard_map/concatenate | solution.py:156
  4.0 4.3 %all-to-all-start = ((bf16[4,7,8192]{2,1,0:T(8,128)(2,1)}), bf16[4,7,8192]{2,1,0:T(8,128)(2,1)S(1)}, u32[]{:S(2)}, u32[]{:S(2)}) async-start(bf16[4,7,8192]{2,1,0:T(8,128)(2,1)} %concatenate.12.rows_ref), calls=%async_computation | async-start | bytes 1048576 | tf_op jit(solution)/shard_map/all_to_all | solution.py:166
  8.3 5.5 %shard_map.55.rest_0_ = f32[768,160]{1,0:T(8,128)} custom-call(s32[1]{0:T(128)} %bitcast.7.order_ref, bf16[4,7,8192]{2,1,0:T(8,128)(2,1)} %concatenate.12.rows_ref), custom_call_target="tpu_custom_call" | custom-call | flops 2013265920 | bytes 1097728 | tf_op jit(solution)/shard_map/pallas_call | solution.py:94
  14.4 3.4 %all-to-all-done.rows_ref = bf16[4,7,8192]{2,1,0:T(8,128)(2,1)S(1)} async-done(((bf16[4,7,8192]{2,1,0:T(8,128)(2,1)}), bf16[4,7,8192]{2,1,0:T(8,128)(2,1)S(1)}, u32[]{:S(2)}, u32[]{:S(2)}) %all-to-all-start) | async-done | bytes 458784 | tf_op jit(solution)/shard_map/all_to_all | solution.py:166
  18.6 13.7 %shard_map.56 = f32[768,160]{1,0:T(8,128)} custom-call(s32[3]{0:T(128)} %and_select_fusion.order_ref, bf16[4,7,8192]{2,1,0:T(8,128)(2,1)} %copy-done, f32[768,160]{1,0:T(8,128)} %shard_map.55.rest_0_), custom_call_target="tpu_custom_call", output_to_operand_aliasing={{}: (2, {})} | custom-call | flops 6039797760 | bytes 1327104 | tf_op jit(solution)/shard_map/pallas_call | solution.py:94
  32.3 1.2 %slice.57 = f32[152,4,180]{0,2,1:T(8,128)S(1)} slice(f32[160,4,192]{0,2,1:T(8,128)} %bitcast.44), slice={[0:152], [0:4], [0:180]} | slice | bytes 875520 | tf_op jit(solution)/shard_map/slice | solution.py:172
  34.2 3.6 %fusion.5 = f32[3,8,19,180]{3,1,0,2:T(8,128)S(1)} fusion(f32[19]{0:T(128)S(1)} %get-tuple-element.13, f32[180,180]{1,0:T(8,128)S(1)} %abs_convert_fusion, f32[19]{0:T(128)S(1)} %get-tuple-element.12, f32[3,8,19,180]{3,0,2,1:T(4,128)S(1)} %fusion.6), kind=kOutput, calls=%fused_computation.6 | convolution fusion | flops 179139600 | bytes 786392
  37.9 1.9 %collective-permute-start = (f32[3,8,2,180]{3,1,0,2:T(8,128)S(1)}, f32[3,8,2,180]{3,1,0,2:T(8,128)S(1)}, u32[]{:S(2)}, u32[]{:S(2)}) collective-permute-start(f32[3,8,2,180]{3,1,0,2:T(8,128)S(1)} %get-tuple-element.7), channel_id=1, source_target_pairs={{0,1},{1,2},{2,3},{3,4},{4,5},{5,6},{6,7},{8,9},{9,10},{10,11},{11... | collective-permute-start | bytes 103688 | tf_op jit(solution)/shard_map/ppermute | solution.py:21
  39.8 3.6 %collective-permute-start.1 = (f32[3,8,2,180]{3,1,0,2:T(8,128)S(1)}, f32[3,8,2,180]{3,1,0,2:T(8,128)S(1)}, u32[]{:S(2)}, u32[]{:S(2)}) collective-permute-start(f32[3,8,2,180]{3,1,0,2:T(8,128)S(1)} %get-tuple-element.8), channel_id=1, source_target_pairs={{1,0},{2,1},{3,2},{4,3},{5,4},{6,5},{7,6},{9,8},{10,9},{11,10},{12... | collective-permute-start | bytes 103688 | tf_op jit(solution)/shard_map/ppermute | solution.py:24
  43.4 1.7 %collective-permute-done.1 = f32[3,8,2,180]{3,1,0,2:T(8,128)S(1)} collective-permute-done((f32[3,8,2,180]{3,1,0,2:T(8,128)S(1)}, f32[3,8,2,180]{3,1,0,2:T(8,128)S(1)}, u32[]{:S(2)}, u32[]{:S(2)}) %collective-permute-start.1) | collective-permute-done | bytes 34592 | tf_op jit(solution)/shard_map/ppermute | solution.py:24
  45.4 2.0 %collective-permute-start.2 = (f32[3,19,180]{2,0,1:T(4,128)S(1)}, f32[3,19,180]{2,0,1:T(4,128)S(1)}, u32[]{:S(2)}, u32[]{:S(2)}) collective-permute-start(f32[3,19,180]{2,0,1:T(4,128)S(1)} %get-tuple-element.5), channel_id=1, source_target_pairs={{0,8},{8,16},{16,24},{24,32},{32,40},{40,48},{48,56},{56,0},{1,9},... | collective-permute-start | bytes 123128 | tf_op jit(solution)/shard_map/ppermute | solution.py:121
  47.4 3.3 %collective-permute-start.3 = (f32[3,19,180]{2,0,1:T(4,128)S(1)}, f32[3,19,180]{2,0,1:T(4,128)S(1)}, u32[]{:S(2)}, u32[]{:S(2)}) collective-permute-start(f32[3,19,180]{2,0,1:T(4,128)S(1)} %get-tuple-element.5), channel_id=1, source_target_pairs={{0,16},{8,24},{16,32},{24,40},{32,48},{40,56},{48,0},{56,8},{1,17}... | collective-permute-start | bytes 123128 | tf_op jit(solution)/shard_map/ppermute | solution.py:121
  50.7 4.0 %collective-permute-start.4 = (f32[3,19,180]{2,0,1:T(4,128)S(1)}, f32[3,19,180]{2,0,1:T(4,128)S(1)}, u32[]{:S(2)}, u32[]{:S(2)}) collective-permute-start(f32[3,19,180]{2,0,1:T(4,128)S(1)} %get-tuple-element.5), channel_id=1, source_target_pairs={{0,24},{8,32},{16,40},{24,48},{32,56},{40,0},{48,8},{56,16},{1,25}... | collective-permute-start | bytes 123128 | tf_op jit(solution)/shard_map/ppermute | solution.py:121
  55.3 5.0 %collective-permute-start.6 = (f32[3,19,180]{2,0,1:T(4,128)S(1)}, f32[3,19,180]{2,0,1:T(4,128)S(1)}, u32[]{:S(2)}, u32[]{:S(2)}) collective-permute-start(f32[3,19,180]{2,0,1:T(4,128)S(1)} %get-tuple-element.5), channel_id=1, source_target_pairs={{0,40},{8,48},{16,56},{24,0},{32,8},{40,16},{48,24},{56,32},{1,41}... | collective-permute-start | bytes 123128 | tf_op jit(solution)/shard_map/ppermute | solution.py:121
  60.2 2.7 %collective-permute-start.7 = (f32[3,19,180]{2,0,1:T(4,128)S(1)}, f32[3,19,180]{2,0,1:T(4,128)S(1)}, u32[]{:S(2)}, u32[]{:S(2)}) collective-permute-start(f32[3,19,180]{2,0,1:T(4,128)S(1)} %get-tuple-element.5), channel_id=1, source_target_pairs={{0,48},{8,56},{16,0},{24,8},{32,16},{40,24},{48,32},{56,40},{1,49}... | collective-permute-start | bytes 123128 | tf_op jit(solution)/shard_map/ppermute | solution.py:121
  62.9 1.0 %collective-permute-start.8 = (f32[3,19,180]{2,0,1:T(4,128)S(1)}, f32[3,19,180]{2,0,1:T(4,128)S(1)}, u32[]{:S(2)}, u32[]{:S(2)}) collective-permute-start(f32[3,19,180]{2,0,1:T(4,128)S(1)} %get-tuple-element.5), channel_id=1, source_target_pairs={{0,56},{8,0},{16,8},{24,16},{32,24},{40,32},{48,40},{56,48},{1,57}... | collective-permute-start | bytes 123128 | tf_op jit(solution)/shard_map/ppermute | solution.py:121
  64.9 1.2 %collective-permute-done.5 = f32[3,19,180]{2,0,1:T(4,128)S(1)} collective-permute-done((f32[3,19,180]{2,0,1:T(4,128)S(1)}, f32[3,19,180]{2,0,1:T(4,128)S(1)}, u32[]{:S(2)}, u32[]{:S(2)}) %collective-permute-start.5) | collective-permute-done | bytes 41072 | tf_op jit(solution)/shard_map/ppermute | solution.py:121
  66.1 3.5 %collective-permute-done.6 = f32[3,19,180]{2,0,1:T(4,128)S(1)} collective-permute-done((f32[3,19,180]{2,0,1:T(4,128)S(1)}, f32[3,19,180]{2,0,1:T(4,128)S(1)}, u32[]{:S(2)}, u32[]{:S(2)}) %collective-permute-start.6) | collective-permute-done | bytes 41072 | tf_op jit(solution)/shard_map/ppermute | solution.py:121
  69.6 3.3 %collective-permute-done.7 = f32[3,19,180]{2,0,1:T(4,128)S(1)} collective-permute-done((f32[3,19,180]{2,0,1:T(4,128)S(1)}, f32[3,19,180]{2,0,1:T(4,128)S(1)}, u32[]{:S(2)}, u32[]{:S(2)}) %collective-permute-start.7) | collective-permute-done | bytes 41072 | tf_op jit(solution)/shard_map/ppermute | solution.py:121
  73.4 2.5 %collective-permute-start.10 = (f32[3,19,180]{2,0,1:T(4,128)S(1)}, f32[3,19,180]{2,0,1:T(4,128)S(1)}, u32[]{:S(2)}, u32[]{:S(2)}) collective-permute-start(f32[3,19,180]{2,0,1:T(4,128)S(1)} %add_add_fusion.1), channel_id=1, source_target_pairs={{0,128},{64,192},{1,129},{65,193},{2,130},{66,194},{3,131},{67,195... | collective-permute-start | bytes 123128 | tf_op jit(solution)/shard_map/ppermute | solution.py:126
  75.9 1.9 %collective-permute-start.11 = (f32[3,19,180]{2,0,1:T(4,128)S(1)}, f32[3,19,180]{2,0,1:T(4,128)S(1)}, u32[]{:S(2)}, u32[]{:S(2)}) collective-permute-start(f32[3,19,180]{2,0,1:T(4,128)S(1)} %add_add_fusion.1), channel_id=1, source_target_pairs={{0,192},{1,193},{2,194},{3,195},{4,196},{5,197},{6,198},{7,199},{8... | collective-permute-start | bytes 123128 | tf_op jit(solution)/shard_map/ppermute | solution.py:126
  77.8 2.1 %collective-permute-start.9 = (f32[3,19,180]{2,0,1:T(4,128)S(1)}, f32[3,19,180]{2,0,1:T(4,128)S(1)}, u32[]{:S(2)}, u32[]{:S(2)}) collective-permute-start(f32[3,19,180]{2,0,1:T(4,128)S(1)} %add_add_fusion.1), channel_id=1, source_target_pairs={{0,64},{64,128},{128,192},{1,65},{65,129},{129,193},{2,66},{66,130... | collective-permute-start | bytes 123128 | tf_op jit(solution)/shard_map/ppermute | solution.py:126
  80.4 1.5 %collective-permute-done.9 = f32[3,19,180]{2,0,1:T(4,128)S(1)} collective-permute-done((f32[3,19,180]{2,0,1:T(4,128)S(1)}, f32[3,19,180]{2,0,1:T(4,128)S(1)}, u32[]{:S(2)}, u32[]{:S(2)}) %collective-permute-start.9) | collective-permute-done | bytes 41072 | tf_op jit(solution)/shard_map/ppermute | solution.py:126
  (39 shorter events, 6.7 us)
Async XLA Ops:
  0.0 1.3 %copy-start.1 = (bf16[3,1,1,1,4,8192]{5,4,3,2,1,0:T(4,128)(2,1)S(1)}, bf16[3,1,1,1,4,8192]{5,4,3,2,1,0:T(4,128)(2,1)}, u32[]{:S(2)}) copy-start(bf16[3,1,1,1,4,8192]{5,4,3,2,1,0:T(4,128)(2,1)} %param.5) | copy-start | bytes 589828
  0.0 1.5 %copy-start.2 = (bf16[1,1,1,4,8192]{4,3,2,1,0:T(4,128)(2,1)S(1)}, bf16[1,1,1,4,8192]{4,3,2,1,0:T(4,128)(2,1)}, u32[]{:S(2)}) copy-start(bf16[1,1,1,4,8192]{4,3,2,1,0:T(4,128)(2,1)} %param.6) | copy-start | bytes 196612
  0.0 1.6 %copy-start.3 = (bf16[1,1,1,4,8192]{4,3,2,1,0:T(4,128)(2,1)S(1)}, bf16[1,1,1,4,8192]{4,3,2,1,0:T(4,128)(2,1)}, u32[]{:S(2)}) copy-start(bf16[1,1,1,4,8192]{4,3,2,1,0:T(4,128)(2,1)} %param.7) | copy-start | bytes 196612
  4.0 13.8 %all-to-all-start = ((bf16[4,7,8192]{2,1,0:T(8,128)(2,1)}), bf16[4,7,8192]{2,1,0:T(8,128)(2,1)S(1)}, u32[]{:S(2)}, u32[]{:S(2)}) async-start(bf16[4,7,8192]{2,1,0:T(8,128)(2,1)} %concatenate.12.rows_ref), calls=%async_computation | async-start | bytes 1048576 | tf_op jit(solution)/shard_map/all_to_all | solution.py:166
  8.3 6.1 %copy-start.4 = (s32[19]{0:T(128)S(1)}, s32[19]{0:T(128)}, u32[]{:S(2)}) copy-start(s32[19]{0:T(128)} %param.9) | copy-start | bytes 232
  17.8 0.8 copy-start
  37.9 5.6 %collective-permute-start = (f32[3,8,2,180]{3,1,0,2:T(8,128)S(1)}, f32[3,8,2,180]{3,1,0,2:T(8,128)S(1)}, u32[]{:S(2)}, u32[]{:S(2)}) collective-permute-start(f32[3,8,2,180]{3,1,0,2:T(8,128)S(1)} %get-tuple-element.7), channel_id=1, source_target_pairs={{0,1},{1,2},{2,3},{3,4},{4,5},{5,6},{6,7},{8,9},{9,10},{10,11},{11... | collective-permute-start | bytes 103688 | tf_op jit(solution)/shard_map/ppermute | solution.py:21
  39.8 5.4 %collective-permute-start.1 = (f32[3,8,2,180]{3,1,0,2:T(8,128)S(1)}, f32[3,8,2,180]{3,1,0,2:T(8,128)S(1)}, u32[]{:S(2)}, u32[]{:S(2)}) collective-permute-start(f32[3,8,2,180]{3,1,0,2:T(8,128)S(1)} %get-tuple-element.8), channel_id=1, source_target_pairs={{1,0},{2,1},{3,2},{4,3},{5,4},{6,5},{7,6},{9,8},{10,9},{11,10},{12... | collective-permute-start | bytes 103688 | tf_op jit(solution)/shard_map/ppermute | solution.py:24
  45.4 14.8 %collective-permute-start.2 = (f32[3,19,180]{2,0,1:T(4,128)S(1)}, f32[3,19,180]{2,0,1:T(4,128)S(1)}, u32[]{:S(2)}, u32[]{:S(2)}) collective-permute-start(f32[3,19,180]{2,0,1:T(4,128)S(1)} %get-tuple-element.5), channel_id=1, source_target_pairs={{0,8},{8,16},{16,24},{24,32},{32,40},{40,48},{48,56},{56,0},{1,9},... | collective-permute-start | bytes 123128 | tf_op jit(solution)/shard_map/ppermute | solution.py:121
  47.4 15.5 %collective-permute-start.3 = (f32[3,19,180]{2,0,1:T(4,128)S(1)}, f32[3,19,180]{2,0,1:T(4,128)S(1)}, u32[]{:S(2)}, u32[]{:S(2)}) collective-permute-start(f32[3,19,180]{2,0,1:T(4,128)S(1)} %get-tuple-element.5), channel_id=1, source_target_pairs={{0,16},{8,24},{16,32},{24,40},{32,48},{40,56},{48,0},{56,8},{1,17}... | collective-permute-start | bytes 123128 | tf_op jit(solution)/shard_map/ppermute | solution.py:121
  50.7 14.2 %collective-permute-start.4 = (f32[3,19,180]{2,0,1:T(4,128)S(1)}, f32[3,19,180]{2,0,1:T(4,128)S(1)}, u32[]{:S(2)}, u32[]{:S(2)}) collective-permute-start(f32[3,19,180]{2,0,1:T(4,128)S(1)} %get-tuple-element.5), channel_id=1, source_target_pairs={{0,24},{8,32},{16,40},{24,48},{32,56},{40,0},{48,8},{56,16},{1,25}... | collective-permute-start | bytes 123128 | tf_op jit(solution)/shard_map/ppermute | solution.py:121
  54.7 11.4 %collective-permute-start.5 = (f32[3,19,180]{2,0,1:T(4,128)S(1)}, f32[3,19,180]{2,0,1:T(4,128)S(1)}, u32[]{:S(2)}, u32[]{:S(2)}) collective-permute-start(f32[3,19,180]{2,0,1:T(4,128)S(1)} %get-tuple-element.5), channel_id=1, source_target_pairs={{0,32},{8,40},{16,48},{24,56},{32,0},{40,8},{48,16},{56,24},{1,33}... | collective-permute-start | bytes 123128 | tf_op jit(solution)/shard_map/ppermute | solution.py:121
  55.3 14.3 %collective-permute-start.6 = (f32[3,19,180]{2,0,1:T(4,128)S(1)}, f32[3,19,180]{2,0,1:T(4,128)S(1)}, u32[]{:S(2)}, u32[]{:S(2)}) collective-permute-start(f32[3,19,180]{2,0,1:T(4,128)S(1)} %get-tuple-element.5), channel_id=1, source_target_pairs={{0,40},{8,48},{16,56},{24,0},{32,8},{40,16},{48,24},{56,32},{1,41}... | collective-permute-start | bytes 123128 | tf_op jit(solution)/shard_map/ppermute | solution.py:121
  60.2 12.7 %collective-permute-start.7 = (f32[3,19,180]{2,0,1:T(4,128)S(1)}, f32[3,19,180]{2,0,1:T(4,128)S(1)}, u32[]{:S(2)}, u32[]{:S(2)}) collective-permute-start(f32[3,19,180]{2,0,1:T(4,128)S(1)} %get-tuple-element.5), channel_id=1, source_target_pairs={{0,48},{8,56},{16,0},{24,8},{32,16},{40,24},{48,32},{56,40},{1,49}... | collective-permute-start | bytes 123128 | tf_op jit(solution)/shard_map/ppermute | solution.py:121
  62.9 10.4 %collective-permute-start.8 = (f32[3,19,180]{2,0,1:T(4,128)S(1)}, f32[3,19,180]{2,0,1:T(4,128)S(1)}, u32[]{:S(2)}, u32[]{:S(2)}) collective-permute-start(f32[3,19,180]{2,0,1:T(4,128)S(1)} %get-tuple-element.5), channel_id=1, source_target_pairs={{0,56},{8,0},{16,8},{24,16},{32,24},{40,32},{48,40},{56,48},{1,57}... | collective-permute-start | bytes 123128 | tf_op jit(solution)/shard_map/ppermute | solution.py:121
  73.4 7.0 %collective-permute-start.10 = (f32[3,19,180]{2,0,1:T(4,128)S(1)}, f32[3,19,180]{2,0,1:T(4,128)S(1)}, u32[]{:S(2)}, u32[]{:S(2)}) collective-permute-start(f32[3,19,180]{2,0,1:T(4,128)S(1)} %add_add_fusion.1), channel_id=1, source_target_pairs={{0,128},{64,192},{1,129},{65,193},{2,130},{66,194},{3,131},{67,195... | collective-permute-start | bytes 123128 | tf_op jit(solution)/shard_map/ppermute | solution.py:126
  75.9 4.5 %collective-permute-start.11 = (f32[3,19,180]{2,0,1:T(4,128)S(1)}, f32[3,19,180]{2,0,1:T(4,128)S(1)}, u32[]{:S(2)}, u32[]{:S(2)}) collective-permute-start(f32[3,19,180]{2,0,1:T(4,128)S(1)} %add_add_fusion.1), channel_id=1, source_target_pairs={{0,192},{1,193},{2,194},{3,195},{4,196},{5,197},{6,198},{7,199},{8... | collective-permute-start | bytes 123128 | tf_op jit(solution)/shard_map/ppermute | solution.py:126
  77.8 4.1 %collective-permute-start.9 = (f32[3,19,180]{2,0,1:T(4,128)S(1)}, f32[3,19,180]{2,0,1:T(4,128)S(1)}, u32[]{:S(2)}, u32[]{:S(2)}) collective-permute-start(f32[3,19,180]{2,0,1:T(4,128)S(1)} %add_add_fusion.1), channel_id=1, source_target_pairs={{0,64},{64,128},{128,192},{1,65},{65,129},{129,193},{2,66},{66,130... | collective-permute-start | bytes 123128 | tf_op jit(solution)/shard_map/ppermute | solution.py:126

commit v4 on v3

--- a/solution.py
+++ b/solution.py
@@ -11,19 +11,6 @@
 DRIFT = 256
 PAD_SLOT = 192
 CHUNK = 4096
-
-
-def with_halo(block, sides, width):
-    for axis, dim in sides:
-        count = lax.axis_size(axis)
-        forward = [(i, i + 1) for i in range(count - 1)]
-        backward = [(target, source) for source, target in forward]
-        low = lax.ppermute(
-            lax.slice_in_dim(block, block.shape[dim] - width, None, axis=dim), axis, forward
-        )
-        high = lax.ppermute(lax.slice_in_dim(block, 0, width, axis=dim), axis, backward)
-        block = jnp.concatenate([low, block, high], axis=dim)
-    return block
 
 
 def row_kernels(kernel_reach):
@@ -111,35 +98,21 @@
 
 
 def exclusive_prefix(totals):
-    gz_count = lax.axis_size("gz")
-    tf_count = lax.axis_size("tf")
-    g = lax.axis_index("gz")
     before = jnp.zeros_like(totals)
-    row_sum = totals
-    for shift in range(1, gz_count):
-        pairs = [(i, (i + shift) % gz_count) for i in range(gz_count)]
-        got = lax.ppermute(totals, "gz", pairs)
-        row_sum = row_sum + got
-        before = before + jnp.where(shift <= g, got, 0.0)
-    for shift in range(1, tf_count):
-        pairs = [(i, i + shift) for i in range(tf_count - shift)]
-        before = before + lax.ppermute(row_sum, "tf", pairs)
-    return before
-
-
-def smooth(field, kernel_reach):
-    across = jnp.einsum(
-        "kzrq,rpq->kzrp", field, row_kernels(kernel_reach), precision=lax.Precision.HIGHEST
-    )
-    rimmed = with_halo(across, (("sec", 2),), 2)
-    row_total = across.shape[2]
-    return (
-        rimmed[:, :, 0:row_total]
-        + 2.0 * rimmed[:, :, 1 : row_total + 1]
-        + 3.0 * rimmed[:, :, 2 : row_total + 2]
-        + 2.0 * rimmed[:, :, 3 : row_total + 3]
-        + rimmed[:, :, 4 : row_total + 4]
-    ) / 9.0
+    group = totals
+    for axis in ("gz", "tf"):
+        count = lax.axis_size(axis)
+        me = lax.axis_index(axis)
+        mask = 1
+        while mask < count:
+            pairs = [(i, i ^ mask) for i in range(count)]
+            got = lax.ppermute(group, axis, pairs)
+            before = before + jnp.where((me & mask) != 0, got, 0.0)
+            group = group + got
+            mask *= 2
+        if axis == "gz":
+            before_row, before, group = before, jnp.zeros_like(totals), group
+    return before_row + before
 
 
 def per_device(residuals, weights, fraction, voxels, kernel_reach):
@@ -173,8 +146,33 @@
     histogram = histogram.reshape(drift_dev, row_dev, 4, PAD)
     means = histogram[:, :, 1:4] / (histogram[:, :, 0:1] + 1.0)
     means = jnp.transpose(means, (2, 0, 1, 3))
-    field = smooth(means, kernel_reach)
-    carried = exclusive_prefix(jnp.sum(field, axis=1))
+    return finish(means, kernel_reach)
+
+
+def pad_smooth(field, kernels):
+    return jnp.einsum("...rq,rpq->...rp", field, kernels, precision=lax.Precision.HIGHEST)
+
+
+def row_smooth(rimmed, row_total, axis):
+    part = lambda start: lax.slice_in_dim(rimmed, start, start + row_total, axis=axis)
+    return (part(0) + 2.0 * part(1) + 3.0 * part(2) + 2.0 * part(3) + part(4)) / 9.0
+
+
+def finish(means, kernel_reach):
+    count = lax.axis_size("sec")
+    forward = [(i, i + 1) for i in range(count - 1)]
+    backward = [(target, source) for source, target in forward]
+    kernels = row_kernels(kernel_reach)
+    row_total = kernels.shape[0]
+    top = pad_smooth(means[:, :, row_total - 2 :], kernels[row_total - 2 :])
+    bottom = pad_smooth(means[:, :, :2], kernels[:2])
+    low = lax.ppermute(top, "sec", forward)
+    high = lax.ppermute(bottom, "sec", backward)
+    summed = pad_smooth(jnp.sum(means, axis=1), kernels)
+    rim_sum = jnp.concatenate([jnp.sum(low, axis=1), summed, jnp.sum(high, axis=1)], axis=1)
+    carried = exclusive_prefix(row_smooth(rim_sum, row_total, 1))
+    across = pad_smooth(means, kernels)
+    field = row_smooth(jnp.concatenate([low, across, high], axis=2), row_total, 2)
     return carried[:, None] + jnp.cumsum(field, axis=1)
 
 

time: 84.5 us -> 77.9 us (0.922); the launches traced: 82.9 us -> 77.6 us
  starting transfers between devices: 34.8 us -> 25.5 us
  matrix products: 3.59 us -> 8.21 us
    ppermute x12 -> x7, starting transfers between devices: 30.5 us -> 21.2 us  [the longest x5 15.6 us: exclusive_prefix(): got = lax.ppermute(group, axis, pairs)]
    dot_general x0 -> x1, matrix products: none -> 3.51 us  [pad_smooth(): jnp.einsum('...rq,rpq->...rp', field, kernels, precision=lax.Precision.HI...]
    unnamed x1 -> x3, matrix products: 3.59 us -> 4.7 us
    ppermute x12 -> x7, waiting for transfers between devices: 12.7 us -> 12.1 us  [the longest x5 12.1 us: exclusive_prefix(): got = lax.ppermute(group, axis, pairs)]
  transfers between devices with their start and end apart: 13 -> 8, of which waited for: 8 -> 6; matrix products, arithmetic and copies ran while one was open for 1% -> 11% of each run, Pallas kernels for 7% -> 7%
where the time goes in v4:
time: 77.9 us; the launch traced here: 77.6 us
  starting transfers between devices  25.5 us (33%)
  Pallas kernels  19.2 us (25%)
  waiting for transfers between devices  15.5 us (20%)
  matrix products  8.21 us (11%)
  local copies, waits for them, and re-layouts  5.89 us (8%)
  other arithmetic  3.08 us (4%)
    pallas_call x2, Pallas kernels, build_histogram(): pl.pallas_call(functools.partial(hist_kernel, cell_rows, first), out_shap...  19.2 us
    ppermute x5, starting transfers between devices, exclusive_prefix(): got = lax.ppermute(group, axis, pairs)  15.6 us
    ppermute x5, waiting for transfers between devices, exclusive_prefix(): got = lax.ppermute(group, axis, pairs)  12.1 us
    unnamed x3, matrix products  4.7 us
    all_to_all x1, starting transfers between devices, per_device(): incoming = lax.all_to_all(outgoing, 'tf', 0, 0, tiled=True)  4.29 us
    ppermute x1, starting transfers between devices, finish(): high = lax.ppermute(bottom, 'sec', backward)  3.64 us
    dot_general x1, matrix products, pad_smooth(): jnp.einsum('...rq,rpq->...rp', field, kernels, precision=lax.Precision.HI...  3.51 us
    all_to_all x1, waiting for transfers between devices, per_device(): incoming = lax.all_to_all(outgoing, 'tf', 0, 0, tiled=True)  3.45 us
  transfers between devices with their start and end apart: 8, of which 6 were waited for; matrix products, arithmetic and copies ran while one was open for 11% of the time, Pallas kernels for 7%

profile of v4, /device:TPU:8, one launch (start us, length us, event | category | flops | bytes accessed | tf_op | source)
XLA Modules:
  0.0 77.6 jit_solution(11165633406656802048)
XLA Ops:
  0.0 1.1 %fusion.32 = (bf16[4,1,8192]{2,0,1:T(4,128)(2,1)S(1)}, s32[1,1,1,1,4,8192]{5,4,3,2,1,0:T(4,128)S(1)}, s32[1,1,1,1,4,8192]{5,4,3,2,1,0:T(4,128)S(1)}) fusion(s32[3,1,1,1,4,8192]{5,4,3,2,1,0:T(4,128)} %param.8, s32[]{:T(128)S(6)} %mul.58), kind=kLoop, calls=%fused_computation.55 | loop fusion | flops 65536 | bytes 720900 | tf_op jit(solution)/shard_map/convert_element_type | solution.py:132
  2.0 2.0 %concatenate.21.rows_ref = bf16[4,7,8192]{2,1,0:T(8,128)(2,1)} concatenate(bf16[4,1,8192]{2,1,0:T(2,128)(2,1)S(1)} %fusion.20, bf16[4,1,8192]{2,1,0:T(2,128)(2,1)S(1)} %copy.34, bf16[4,3,8192]{2,1,0:T(4,128)(2,1)S(1)} %bitcast.66, bf16[4,1,8192]{2,1,0:T(2,128)(2,1)S(1)} %copy.35, bf16[4,1,8192]{2,1,0:T(2,128)(2,1)S(1)} %copy.36), dimensions={1} | concatenate | bytes 917504 | tf_op jit(solution)/shard_map/concatenate | solution.py:129
  4.0 4.3 %all-to-all-start = ((bf16[4,7,8192]{2,1,0:T(8,128)(2,1)}), bf16[4,7,8192]{2,1,0:T(8,128)(2,1)S(1)}, u32[]{:S(2)}, u32[]{:S(2)}) async-start(bf16[4,7,8192]{2,1,0:T(8,128)(2,1)} %concatenate.21.rows_ref), calls=%async_computation | async-start | bytes 1048576 | tf_op jit(solution)/shard_map/all_to_all | solution.py:139
  8.3 5.5 %shard_map.55.rest_0_ = f32[768,160]{1,0:T(8,128)} custom-call(s32[1]{0:T(128)} %bitcast.7.order_ref, bf16[4,7,8192]{2,1,0:T(8,128)(2,1)} %concatenate.21.rows_ref), custom_call_target="tpu_custom_call" | custom-call | flops 2013265920 | bytes 1097728 | tf_op jit(solution)/shard_map/pallas_call | solution.py:81
  14.3 3.5 %all-to-all-done.rows_ref = bf16[4,7,8192]{2,1,0:T(8,128)(2,1)S(1)} async-done(((bf16[4,7,8192]{2,1,0:T(8,128)(2,1)}), bf16[4,7,8192]{2,1,0:T(8,128)(2,1)S(1)}, u32[]{:S(2)}, u32[]{:S(2)}) %all-to-all-start) | async-done | bytes 458784 | tf_op jit(solution)/shard_map/all_to_all | solution.py:139
  17.8 0.8 %copy-done = bf16[4,7,8192]{2,1,0:T(8,128)(2,1)} copy-done((bf16[4,7,8192]{2,1,0:T(8,128)(2,1)}, bf16[4,7,8192]{2,1,0:T(8,128)(2,1)S(1)}, u32[]{:S(2)}) %copy-start) | copy-done | bytes 458776
  18.6 13.7 %shard_map.56 = f32[768,160]{1,0:T(8,128)} custom-call(s32[3]{0:T(128)} %and_select_fusion.order_ref, bf16[4,7,8192]{2,1,0:T(8,128)(2,1)} %copy-done, f32[768,160]{1,0:T(8,128)} %shard_map.55.rest_0_), custom_call_target="tpu_custom_call", output_to_operand_aliasing={{}: (2, {})} | custom-call | flops 6039797760 | bytes 1327104 | tf_op jit(solution)/shard_map/pallas_call | solution.py:81
  32.2 1.2 %slice.85 = f32[152,4,180]{0,2,1:T(8,128)S(1)} slice(f32[160,4,192]{0,2,1:T(8,128)} %bitcast.67), slice={[0:152], [0:4], [0:180]} | slice | bytes 875520 | tf_op jit(solution)/shard_map/slice | solution.py:145
  34.3 0.5 fusion.6
  34.9 0.5 fusion.7
  35.4 1.9 %collective-permute-start = (f32[3,8,2,180]{3,1,0,2:T(8,128)S(1)}, f32[3,8,2,180]{3,1,0,2:T(8,128)S(1)}, u32[]{:S(2)}, u32[]{:S(2)}) collective-permute-start(f32[3,8,2,180]{3,1,0,2:T(8,128)S(1)} %fusion.6), channel_id=1, source_target_pairs={{0,1},{1,2},{2,3},{3,4},{4,5},{5,6},{6,7},{8,9},{9,10},{10,11},{11... | collective-permute-start | bytes 103688 | tf_op jit(solution)/shard_map/ppermute | solution.py:169
  37.3 3.6 %collective-permute-start.1 = (f32[3,8,2,180]{3,1,0,2:T(8,128)S(1)}, f32[3,8,2,180]{3,1,0,2:T(8,128)S(1)}, u32[]{:S(2)}, u32[]{:S(2)}) collective-permute-start(f32[3,8,2,180]{3,1,0,2:T(8,128)S(1)} %fusion.7), channel_id=1, source_target_pairs={{1,0},{2,1},{3,2},{4,3},{5,4},{6,5},{7,6},{9,8},{10,9},{11,10},{12... | collective-permute-start | bytes 103688 | tf_op jit(solution)/shard_map/ppermute | solution.py:170
  41.0 3.5 %fusion.5 = f32[3,19,180]{2,0,1:T(4,128)S(1)} fusion(f32[3,19,180]{2,0,1:T(4,128)S(1)} %get-tuple-element.5, f32[19]{0:T(128)S(1)} %get-tuple-element.11, f32[180,180]{1,0:T(8,128)S(1)} %abs_convert_fusion, f32[19]{0:T(128)S(1)} %get-tuple-element.10), kind=kOutput, calls=%fused_computation.6 | convolution fusion | flops 24008400 | bytes 211832 | tf_op jit(solution)/shard_map/...rq,rpq->...rp/dot_general | solution.py:153
  44.7 2.0 %collective-permute-start.2 = (f32[3,19,180]{2,0,1:T(4,128)S(1)}, f32[3,19,180]{2,0,1:T(4,128)S(1)}, u32[]{:S(2)}, u32[]{:S(2)}) collective-permute-start(f32[3,19,180]{2,0,1:T(4,128)S(1)} %fusion.27), channel_id=1, source_target_pairs={{0,8},{8,0},{16,24},{24,16},{32,40},{40,32},{48,56},{56,48},{1,9},... | collective-permute-start | bytes 123128 | tf_op jit(solution)/shard_map/ppermute | solution.py:109
  46.7 2.5 %collective-permute-done.2 = f32[3,19,180]{2,0,1:T(4,128)S(1)} collective-permute-done((f32[3,19,180]{2,0,1:T(4,128)S(1)}, f32[3,19,180]{2,0,1:T(4,128)S(1)}, u32[]{:S(2)}, u32[]{:S(2)}) %collective-permute-start.2) | collective-permute-done | bytes 41072 | tf_op jit(solution)/shard_map/ppermute | solution.py:109
  49.2 3.4 %collective-permute-start.3 = (f32[3,19,180]{2,0,1:T(4,128)S(1)}, f32[3,19,180]{2,0,1:T(4,128)S(1)}, u32[]{:S(2)}, u32[]{:S(2)}) collective-permute-start(f32[3,19,180]{2,0,1:T(4,128)S(1)} %add.115), channel_id=1, source_target_pairs={{0,16},{8,24},{16,0},{24,8},{32,48},{40,56},{48,32},{56,40},{1,17}... | collective-permute-start | bytes 123128 | tf_op jit(solution)/shard_map/ppermute | solution.py:109
  52.5 2.7 %collective-permute-done.3 = f32[3,19,180]{2,0,1:T(4,128)S(1)} collective-permute-done((f32[3,19,180]{2,0,1:T(4,128)S(1)}, f32[3,19,180]{2,0,1:T(4,128)S(1)}, u32[]{:S(2)}, u32[]{:S(2)}) %collective-permute-start.3) | collective-permute-done | bytes 41072 | tf_op jit(solution)/shard_map/ppermute | solution.py:109
  55.2 7.5 %collective-permute-start.4 = (f32[3,19,180]{2,0,1:T(4,128)S(1)}, f32[3,19,180]{2,0,1:T(4,128)S(1)}, u32[]{:S(2)}, u32[]{:S(2)}) collective-permute-start(f32[3,19,180]{2,0,1:T(4,128)S(1)} %add.117), channel_id=1, source_target_pairs={{0,32},{8,40},{16,48},{24,56},{32,0},{40,8},{48,16},{56,24},{1,33}... | collective-permute-start | bytes 123128 | tf_op jit(solution)/shard_map/ppermute | solution.py:109
  62.7 3.2 %collective-permute-done.4 = f32[3,19,180]{2,0,1:T(4,128)S(1)} collective-permute-done((f32[3,19,180]{2,0,1:T(4,128)S(1)}, f32[3,19,180]{2,0,1:T(4,128)S(1)}, u32[]{:S(2)}, u32[]{:S(2)}) %collective-permute-start.4) | collective-permute-done | bytes 41072 | tf_op jit(solution)/shard_map/ppermute | solution.py:109
  66.0 0.8 %collective-permute-start.5 = (f32[3,19,180]{2,0,1:T(4,128)S(1)}, f32[3,19,180]{2,0,1:T(4,128)S(1)}, u32[]{:S(2)}, u32[]{:S(2)}) collective-permute-start(f32[3,19,180]{2,0,1:T(4,128)S(1)} %add.119), channel_id=1, source_target_pairs={{0,64},{64,0},{128,192},{192,128},{1,65},{65,1},{129,193},{193,129... | collective-permute-start | bytes 123128 | tf_op jit(solution)/shard_map/ppermute | solution.py:109
  66.8 3.6 %fusion.4 = f32[3,8,19,180]{3,1,0,2:T(8,128)S(1)} fusion(f32[19]{0:T(128)S(1)} %get-tuple-element.11, f32[180,180]{1,0:T(8,128)S(1)} %abs_convert_fusion, f32[19]{0:T(128)S(1)} %get-tuple-element.10, f32[8,19,3,180]{3,2,1,0:T(4,128)S(1)} %slice.86, f32[8,19,180]{2,0,1:T(8,128)S(1)} %fusion.18), kind=kOutput, calls=%fused_computation.5 | convolution fusion | flops 179221680 | bytes 895832
  70.6 2.0 %collective-permute-start.6 = (f32[3,19,180]{2,0,1:T(4,128)S(1)}, f32[3,19,180]{2,0,1:T(4,128)S(1)}, u32[]{:S(2)}, u32[]{:S(2)}) collective-permute-start(f32[3,19,180]{2,0,1:T(4,128)S(1)} %add.120), channel_id=1, source_target_pairs={{0,128},{64,192},{128,0},{192,64},{1,129},{65,193},{129,1},{193,65... | collective-permute-start | bytes 123128 | tf_op jit(solution)/shard_map/ppermute | solution.py:109
  73.1 3.5 %collective-permute-done.6 = f32[3,19,180]{2,0,1:T(4,128)S(1)} collective-permute-done((f32[3,19,180]{2,0,1:T(4,128)S(1)}, f32[3,19,180]{2,0,1:T(4,128)S(1)}, u32[]{:S(2)}, u32[]{:S(2)}) %collective-permute-start.6) | collective-permute-done | bytes 41072 | tf_op jit(solution)/shard_map/ppermute | solution.py:109
  76.8 0.8 %copy.40 = f32[3,8,19,180]{3,1,2,0:T(8,128)} copy(f32[3,8,19,180]{3,1,0,2:T(8,128)S(1)} %broadcast_add_fusion) | data formatting | bytes 656640 | tf_op jit(solution)/shard_map/add | solution.py:176
  (37 shorter events, 3.3 us)
Async XLA Ops:
  0.0 1.3 %copy-start.1 = (bf16[3,1,1,1,4,8192]{5,4,3,2,1,0:T(4,128)(2,1)S(1)}, bf16[3,1,1,1,4,8192]{5,4,3,2,1,0:T(4,128)(2,1)}, u32[]{:S(2)}) copy-start(bf16[3,1,1,1,4,8192]{5,4,3,2,1,0:T(4,128)(2,1)} %param.5) | copy-start | bytes 589828
  0.0 1.5 %copy-start.2 = (bf16[1,1,1,4,8192]{4,3,2,1,0:T(4,128)(2,1)S(1)}, bf16[1,1,1,4,8192]{4,3,2,1,0:T(4,128)(2,1)}, u32[]{:S(2)}) copy-start(bf16[1,1,1,4,8192]{4,3,2,1,0:T(4,128)(2,1)} %param.6) | copy-start | bytes 196612
  0.0 1.6 %copy-start.3 = (bf16[1,1,1,4,8192]{4,3,2,1,0:T(4,128)(2,1)S(1)}, bf16[1,1,1,4,8192]{4,3,2,1,0:T(4,128)(2,1)}, u32[]{:S(2)}) copy-start(bf16[1,1,1,4,8192]{4,3,2,1,0:T(4,128)(2,1)} %param.7) | copy-start | bytes 196612
  4.0 13.8 %all-to-all-start = ((bf16[4,7,8192]{2,1,0:T(8,128)(2,1)}), bf16[4,7,8192]{2,1,0:T(8,128)(2,1)S(1)}, u32[]{:S(2)}, u32[]{:S(2)}) async-start(bf16[4,7,8192]{2,1,0:T(8,128)(2,1)} %concatenate.21.rows_ref), calls=%async_computation | async-start | bytes 1048576 | tf_op jit(solution)/shard_map/all_to_all | solution.py:139
  8.3 6.0 %copy-start.4 = (s32[19]{0:T(128)S(1)}, s32[19]{0:T(128)}, u32[]{:S(2)}) copy-start(s32[19]{0:T(128)} %param.9) | copy-start | bytes 232
  17.8 0.8 %copy-start = (bf16[4,7,8192]{2,1,0:T(8,128)(2,1)}, bf16[4,7,8192]{2,1,0:T(8,128)(2,1)S(1)}, u32[]{:S(2)}) copy-start(bf16[4,7,8192]{2,1,0:T(8,128)(2,1)S(1)} %all-to-all-done.rows_ref) | copy-start | bytes 1376260
  35.4 9.1 %collective-permute-start = (f32[3,8,2,180]{3,1,0,2:T(8,128)S(1)}, f32[3,8,2,180]{3,1,0,2:T(8,128)S(1)}, u32[]{:S(2)}, u32[]{:S(2)}) collective-permute-start(f32[3,8,2,180]{3,1,0,2:T(8,128)S(1)} %fusion.6), channel_id=1, source_target_pairs={{0,1},{1,2},{2,3},{3,4},{4,5},{5,6},{6,7},{8,9},{9,10},{10,11},{11... | collective-permute-start | bytes 103688 | tf_op jit(solution)/shard_map/ppermute | solution.py:169
  37.3 7.2 %collective-permute-start.1 = (f32[3,8,2,180]{3,1,0,2:T(8,128)S(1)}, f32[3,8,2,180]{3,1,0,2:T(8,128)S(1)}, u32[]{:S(2)}, u32[]{:S(2)}) collective-permute-start(f32[3,8,2,180]{3,1,0,2:T(8,128)S(1)} %fusion.7), channel_id=1, source_target_pairs={{1,0},{2,1},{3,2},{4,3},{5,4},{6,5},{7,6},{9,8},{10,9},{11,10},{12... | collective-permute-start | bytes 103688 | tf_op jit(solution)/shard_map/ppermute | solution.py:170
  44.7 4.5 %collective-permute-start.2 = (f32[3,19,180]{2,0,1:T(4,128)S(1)}, f32[3,19,180]{2,0,1:T(4,128)S(1)}, u32[]{:S(2)}, u32[]{:S(2)}) collective-permute-start(f32[3,19,180]{2,0,1:T(4,128)S(1)} %fusion.27), channel_id=1, source_target_pairs={{0,8},{8,0},{16,24},{24,16},{32,40},{40,32},{48,56},{56,48},{1,9},... | collective-permute-start | bytes 123128 | tf_op jit(solution)/shard_map/ppermute | solution.py:109
  49.2 6.0 %collective-permute-start.3 = (f32[3,19,180]{2,0,1:T(4,128)S(1)}, f32[3,19,180]{2,0,1:T(4,128)S(1)}, u32[]{:S(2)}, u32[]{:S(2)}) collective-permute-start(f32[3,19,180]{2,0,1:T(4,128)S(1)} %add.115), channel_id=1, source_target_pairs={{0,16},{8,24},{16,0},{24,8},{32,48},{40,56},{48,32},{56,40},{1,17}... | collective-permute-start | bytes 123128 | tf_op jit(solution)/shard_map/ppermute | solution.py:109
  55.2 10.7 %collective-permute-start.4 = (f32[3,19,180]{2,0,1:T(4,128)S(1)}, f32[3,19,180]{2,0,1:T(4,128)S(1)}, u32[]{:S(2)}, u32[]{:S(2)}) collective-permute-start(f32[3,19,180]{2,0,1:T(4,128)S(1)} %add.117), channel_id=1, source_target_pairs={{0,32},{8,40},{16,48},{24,56},{32,0},{40,8},{48,16},{56,24},{1,33}... | collective-permute-start | bytes 123128 | tf_op jit(solution)/shard_map/ppermute | solution.py:109
  66.0 4.7 %collective-permute-start.5 = (f32[3,19,180]{2,0,1:T(4,128)S(1)}, f32[3,19,180]{2,0,1:T(4,128)S(1)}, u32[]{:S(2)}, u32[]{:S(2)}) collective-permute-start(f32[3,19,180]{2,0,1:T(4,128)S(1)} %add.119), channel_id=1, source_target_pairs={{0,64},{64,0},{128,192},{192,128},{1,65},{65,1},{129,193},{193,129... | collective-permute-start | bytes 123128 | tf_op jit(solution)/shard_map/ppermute | solution.py:109
  70.6 6.0 %collective-permute-start.6 = (f32[3,19,180]{2,0,1:T(4,128)S(1)}, f32[3,19,180]{2,0,1:T(4,128)S(1)}, u32[]{:S(2)}, u32[]{:S(2)}) collective-permute-start(f32[3,19,180]{2,0,1:T(4,128)S(1)} %add.120), channel_id=1, source_target_pairs={{0,128},{64,192},{128,0},{192,64},{1,129},{65,193},{129,1},{193,65... | collective-permute-start | bytes 123128 | tf_op jit(solution)/shard_map/ppermute | solution.py:109

commit v5 on v4

--- a/solution.py
+++ b/solution.py
@@ -97,22 +97,27 @@
     )(*operands)
 
 
+SCAN_ROUNDS = {'gz': ((1,), (2, 4, 6)), 'tf': ((1, 2, 3),)}
+
+
+def scan_axis(group, axis, rounds):
+    me = lax.axis_index(axis)
+    count = lax.axis_size(axis)
+    before = jnp.zeros_like(group)
+    for masks in rounds:
+        bits = functools.reduce(lambda x, y: x | y, masks)
+        got = [lax.ppermute(group, axis, [(i, i ^ m) for i in range(count)]) for m in masks]
+        for m, part in zip(masks, got):
+            lower = ((me ^ m) & bits) < (me & bits)
+            before = before + jnp.where(lower, part, 0.0)
+        group = group + functools.reduce(lambda x, y: x + y, got)
+    return before, group
+
+
 def exclusive_prefix(totals):
-    before = jnp.zeros_like(totals)
-    group = totals
-    for axis in ("gz", "tf"):
-        count = lax.axis_size(axis)
-        me = lax.axis_index(axis)
-        mask = 1
-        while mask < count:
-            pairs = [(i, i ^ mask) for i in range(count)]
-            got = lax.ppermute(group, axis, pairs)
-            before = before + jnp.where((me & mask) != 0, got, 0.0)
-            group = group + got
-            mask *= 2
-        if axis == "gz":
-            before_row, before, group = before, jnp.zeros_like(totals), group
-    return before_row + before
+    before_row, row_sum = scan_axis(totals, "gz", SCAN_ROUNDS["gz"])
+    before_col, _ = scan_axis(row_sum, "tf", SCAN_ROUNDS["tf"])
+    return before_row + before_col
 
 
 def per_device(residuals, weights, fraction, voxels, kernel_reach):

time: 77.9 us -> 74.2 us (0.953)
  waiting for transfers between devices: 15.5 us -> 11.9 us
    ppermute x5 -> x7, waiting for transfers between devices: 12.1 us -> 8.45 us  [scan_axis(): lax.ppermute(group, axis, [(i, i ^ m) for i in range(count)])]
    ppermute x5 -> x7, starting transfers between devices: 15.6 us -> 15.5 us  [scan_axis(): lax.ppermute(group, axis, [(i, i ^ m) for i in range(count)])]
  transfers between devices with their start and end apart: 8 -> 10, of which waited for: 6 -> 5; matrix products, arithmetic and copies ran while one was open for 11% -> 11% of each run, Pallas kernels for 7% -> 7%
where the time goes in v5:
time: 74.2 us; the launch traced here: 73.9 us
  starting transfers between devices  25.4 us (34%)
  Pallas kernels  19.1 us (26%)
  waiting for transfers between devices  11.9 us (16%)
  matrix products  8.21 us (11%)
  local copies, waits for them, and re-layouts  5.9 us (8%)
  other arithmetic  3.14 us (4%)
    pallas_call x2, Pallas kernels, build_histogram(): pl.pallas_call(functools.partial(hist_kernel, cell_rows, first), out_shap...  19.1 us
    ppermute x7, starting transfers between devices, scan_axis(): lax.ppermute(group, axis, [(i, i ^ m) for i in range(count)])  15.5 us
    ppermute x7, waiting for transfers between devices, scan_axis(): lax.ppermute(group, axis, [(i, i ^ m) for i in range(count)])  8.45 us
    unnamed x3, matrix products  4.7 us
    all_to_all x1, starting transfers between devices, per_device(): incoming = lax.all_to_all(outgoing, 'tf', 0, 0, tiled=True)  4.29 us
    ppermute x1, starting transfers between devices, finish(): high = lax.ppermute(bottom, 'sec', backward)  3.64 us
    dot_general x1, matrix products, pad_smooth(): jnp.einsum('...rq,rpq->...rp', field, kernels, precision=lax.Precision.HI...  3.51 us
    all_to_all x1, waiting for transfers between devices, per_device(): incoming = lax.all_to_all(outgoing, 'tf', 0, 0, tiled=True)  3.42 us
  transfers between devices with their start and end apart: 10, of which 5 were waited for; matrix products, arithmetic and copies ran while one was open for 11% of the time, Pallas kernels for 7%

profile of v5, /device:TPU:8, one launch (start us, length us, event | category | flops | bytes accessed | tf_op | source)
XLA Modules:
  0.0 73.9 jit_solution(10092193587052405880)
XLA Ops:
  0.0 1.1 %fusion.32 = (bf16[4,1,8192]{2,0,1:T(4,128)(2,1)S(1)}, s32[1,1,1,1,4,8192]{5,4,3,2,1,0:T(4,128)S(1)}, s32[1,1,1,1,4,8192]{5,4,3,2,1,0:T(4,128)S(1)}) fusion(s32[3,1,1,1,4,8192]{5,4,3,2,1,0:T(4,128)} %param.8, s32[]{:T(128)S(6)} %mul.58), kind=kLoop, calls=%fused_computation.56 | loop fusion | flops 65536 | bytes 720900 | tf_op jit(solution)/shard_map/convert_element_type | solution.py:137
  2.0 2.0 %concatenate.21.rows_ref = bf16[4,7,8192]{2,1,0:T(8,128)(2,1)} concatenate(bf16[4,1,8192]{2,1,0:T(2,128)(2,1)S(1)} %fusion.20, bf16[4,1,8192]{2,1,0:T(2,128)(2,1)S(1)} %copy.34, bf16[4,3,8192]{2,1,0:T(4,128)(2,1)S(1)} %bitcast.66, bf16[4,1,8192]{2,1,0:T(2,128)(2,1)S(1)} %copy.35, bf16[4,1,8192]{2,1,0:T(2,128)(2,1)S(1)} %copy.36), dimensions={1} | concatenate | bytes 917504 | tf_op jit(solution)/shard_map/concatenate | solution.py:134
  4.0 4.3 %all-to-all-start = ((bf16[4,7,8192]{2,1,0:T(8,128)(2,1)}), bf16[4,7,8192]{2,1,0:T(8,128)(2,1)S(1)}, u32[]{:S(2)}, u32[]{:S(2)}) async-start(bf16[4,7,8192]{2,1,0:T(8,128)(2,1)} %concatenate.21.rows_ref), calls=%async_computation | async-start | bytes 1048576 | tf_op jit(solution)/shard_map/all_to_all | solution.py:144
  8.3 5.5 %shard_map.55.rest_0_ = f32[768,160]{1,0:T(8,128)} custom-call(s32[1]{0:T(128)} %bitcast.7.order_ref, bf16[4,7,8192]{2,1,0:T(8,128)(2,1)} %concatenate.21.rows_ref), custom_call_target="tpu_custom_call" | custom-call | flops 2013265920 | bytes 1097728 | tf_op jit(solution)/shard_map/pallas_call | solution.py:81
  14.3 3.4 %all-to-all-done.rows_ref = bf16[4,7,8192]{2,1,0:T(8,128)(2,1)S(1)} async-done(((bf16[4,7,8192]{2,1,0:T(8,128)(2,1)}), bf16[4,7,8192]{2,1,0:T(8,128)(2,1)S(1)}, u32[]{:S(2)}, u32[]{:S(2)}) %all-to-all-start) | async-done | bytes 458784 | tf_op jit(solution)/shard_map/all_to_all | solution.py:144
  17.8 0.8 %copy-done = bf16[4,7,8192]{2,1,0:T(8,128)(2,1)} copy-done((bf16[4,7,8192]{2,1,0:T(8,128)(2,1)}, bf16[4,7,8192]{2,1,0:T(8,128)(2,1)S(1)}, u32[]{:S(2)}) %copy-start) | copy-done | bytes 458776
  18.6 13.7 %shard_map.56 = f32[768,160]{1,0:T(8,128)} custom-call(s32[3]{0:T(128)} %and_select_fusion.order_ref, bf16[4,7,8192]{2,1,0:T(8,128)(2,1)} %copy-done, f32[768,160]{1,0:T(8,128)} %shard_map.55.rest_0_), custom_call_target="tpu_custom_call", output_to_operand_aliasing={{}: (2, {})} | custom-call | flops 6039797760 | bytes 1327104 | tf_op jit(solution)/shard_map/pallas_call | solution.py:81
  32.2 1.2 %slice.85 = f32[152,4,180]{0,2,1:T(8,128)S(1)} slice(f32[160,4,192]{0,2,1:T(8,128)} %bitcast.67), slice={[0:152], [0:4], [0:180]} | slice | bytes 875520 | tf_op jit(solution)/shard_map/slice | solution.py:150
  34.9 0.5 fusion.7
  35.4 1.9 %collective-permute-start = (f32[3,8,2,180]{3,1,0,2:T(8,128)S(1)}, f32[3,8,2,180]{3,1,0,2:T(8,128)S(1)}, u32[]{:S(2)}, u32[]{:S(2)}) collective-permute-start(f32[3,8,2,180]{3,1,0,2:T(8,128)S(1)} %fusion.6), channel_id=1, source_target_pairs={{0,1},{1,2},{2,3},{3,4},{4,5},{5,6},{6,7},{8,9},{9,10},{10,11},{11... | collective-permute-start | bytes 103688 | tf_op jit(solution)/shard_map/ppermute | solution.py:174
  37.3 3.6 %collective-permute-start.1 = (f32[3,8,2,180]{3,1,0,2:T(8,128)S(1)}, f32[3,8,2,180]{3,1,0,2:T(8,128)S(1)}, u32[]{:S(2)}, u32[]{:S(2)}) collective-permute-start(f32[3,8,2,180]{3,1,0,2:T(8,128)S(1)} %fusion.7), channel_id=1, source_target_pairs={{1,0},{2,1},{3,2},{4,3},{5,4},{6,5},{7,6},{9,8},{10,9},{11,10},{12... | collective-permute-start | bytes 103688 | tf_op jit(solution)/shard_map/ppermute | solution.py:175
  41.0 3.5 %fusion.5 = f32[3,19,180]{2,0,1:T(4,128)S(1)} fusion(f32[3,19,180]{2,0,1:T(4,128)S(1)} %get-tuple-element.5, f32[19]{0:T(128)S(1)} %get-tuple-element.11, f32[180,180]{1,0:T(8,128)S(1)} %abs_convert_fusion, f32[19]{0:T(128)S(1)} %get-tuple-element.10), kind=kOutput, calls=%fused_computation.6 | convolution fusion | flops 24008400 | bytes 211832 | tf_op jit(solution)/shard_map/...rq,rpq->...rp/dot_general | solution.py:158
  44.7 2.0 %collective-permute-start.2 = (f32[3,19,180]{2,0,1:T(4,128)S(1)}, f32[3,19,180]{2,0,1:T(4,128)S(1)}, u32[]{:S(2)}, u32[]{:S(2)}) collective-permute-start(f32[3,19,180]{2,0,1:T(4,128)S(1)} %fusion.27), channel_id=1, source_target_pairs={{0,8},{8,0},{16,24},{24,16},{32,40},{40,32},{48,56},{56,48},{1,9},... | collective-permute-start | bytes 123128 | tf_op jit(solution)/shard_map/ppermute | solution.py:109
  46.7 2.5 %collective-permute-done.2 = f32[3,19,180]{2,0,1:T(4,128)S(1)} collective-permute-done((f32[3,19,180]{2,0,1:T(4,128)S(1)}, f32[3,19,180]{2,0,1:T(4,128)S(1)}, u32[]{:S(2)}, u32[]{:S(2)}) %collective-permute-start.2) | collective-permute-done | bytes 41072 | tf_op jit(solution)/shard_map/ppermute | solution.py:109
  49.2 3.4 %collective-permute-start.3 = (f32[3,19,180]{2,0,1:T(4,128)S(1)}, f32[3,19,180]{2,0,1:T(4,128)S(1)}, u32[]{:S(2)}, u32[]{:S(2)}) collective-permute-start(f32[3,19,180]{2,0,1:T(4,128)S(1)} %add.121), channel_id=1, source_target_pairs={{0,16},{8,24},{16,0},{24,8},{32,48},{40,56},{48,32},{56,40},{1,17}... | collective-permute-start | bytes 123128 | tf_op jit(solution)/shard_map/ppermute | solution.py:109
  52.5 5.4 %collective-permute-start.4 = (f32[3,19,180]{2,0,1:T(4,128)S(1)}, f32[3,19,180]{2,0,1:T(4,128)S(1)}, u32[]{:S(2)}, u32[]{:S(2)}) collective-permute-start(f32[3,19,180]{2,0,1:T(4,128)S(1)} %add.121), channel_id=1, source_target_pairs={{0,32},{8,40},{16,48},{24,56},{32,0},{40,8},{48,16},{56,24},{1,33}... | collective-permute-start | bytes 123128 | tf_op jit(solution)/shard_map/ppermute | solution.py:109
  57.9 3.6 %fusion.4 = f32[3,8,19,180]{3,1,0,2:T(8,128)S(1)} fusion(f32[19]{0:T(128)S(1)} %get-tuple-element.11, f32[180,180]{1,0:T(8,128)S(1)} %abs_convert_fusion, f32[19]{0:T(128)S(1)} %get-tuple-element.10, f32[8,19,3,180]{3,2,1,0:T(4,128)S(1)} %slice.86, f32[8,19,180]{2,0,1:T(8,128)S(1)} %fusion.18), kind=kOutput, calls=%fused_computation.5 | convolution fusion | flops 179221680 | bytes 895832
  61.6 3.0 %collective-permute-done.5 = f32[3,19,180]{2,0,1:T(4,128)S(1)} collective-permute-done((f32[3,19,180]{2,0,1:T(4,128)S(1)}, f32[3,19,180]{2,0,1:T(4,128)S(1)}, u32[]{:S(2)}, u32[]{:S(2)}) %collective-permute-start.5) | collective-permute-done | bytes 41072 | tf_op jit(solution)/shard_map/ppermute | solution.py:109
  64.6 0.7 collective-permute-start.6
  65.2 2.1 %collective-permute-start.7 = (f32[3,19,180]{2,0,1:T(4,128)S(1)}, f32[3,19,180]{2,0,1:T(4,128)S(1)}, u32[]{:S(2)}, u32[]{:S(2)}) collective-permute-start(f32[3,19,180]{2,0,1:T(4,128)S(1)} %add_add_fusion.1), channel_id=1, source_target_pairs={{0,128},{64,192},{128,0},{192,64},{1,129},{65,193},{129,1},{193,65... | collective-permute-start | bytes 123128 | tf_op jit(solution)/shard_map/ppermute | solution.py:109
  67.3 2.1 %collective-permute-start.8 = (f32[3,19,180]{2,0,1:T(4,128)S(1)}, f32[3,19,180]{2,0,1:T(4,128)S(1)}, u32[]{:S(2)}, u32[]{:S(2)}) collective-permute-start(f32[3,19,180]{2,0,1:T(4,128)S(1)} %add_add_fusion.1), channel_id=1, source_target_pairs={{0,192},{64,128},{128,64},{192,0},{1,193},{65,129},{129,65},{193,1... | collective-permute-start | bytes 123128 | tf_op jit(solution)/shard_map/ppermute | solution.py:109
  69.9 1.2 %collective-permute-done.7 = f32[3,19,180]{2,0,1:T(4,128)S(1)} collective-permute-done((f32[3,19,180]{2,0,1:T(4,128)S(1)}, f32[3,19,180]{2,0,1:T(4,128)S(1)}, u32[]{:S(2)}, u32[]{:S(2)}) %collective-permute-start.7) | collective-permute-done | bytes 41072 | tf_op jit(solution)/shard_map/ppermute | solution.py:109
  71.1 1.8 %collective-permute-done.8 = f32[3,19,180]{2,0,1:T(4,128)S(1)} collective-permute-done((f32[3,19,180]{2,0,1:T(4,128)S(1)}, f32[3,19,180]{2,0,1:T(4,128)S(1)}, u32[]{:S(2)}, u32[]{:S(2)}) %collective-permute-start.8) | collective-permute-done | bytes 41072 | tf_op jit(solution)/shard_map/ppermute | solution.py:109
  73.1 0.8 %copy.40 = f32[3,8,19,180]{3,1,2,0:T(8,128)} copy(f32[3,8,19,180]{3,1,0,2:T(8,128)S(1)} %broadcast_add_fusion) | data formatting | bytes 656640 | tf_op jit(solution)/shard_map/add | solution.py:181
  (39 shorter events, 3.7 us)
Async XLA Ops:
  0.0 1.3 %copy-start.1 = (bf16[3,1,1,1,4,8192]{5,4,3,2,1,0:T(4,128)(2,1)S(1)}, bf16[3,1,1,1,4,8192]{5,4,3,2,1,0:T(4,128)(2,1)}, u32[]{:S(2)}) copy-start(bf16[3,1,1,1,4,8192]{5,4,3,2,1,0:T(4,128)(2,1)} %param.5) | copy-start | bytes 589828
  0.0 1.5 %copy-start.2 = (bf16[1,1,1,4,8192]{4,3,2,1,0:T(4,128)(2,1)S(1)}, bf16[1,1,1,4,8192]{4,3,2,1,0:T(4,128)(2,1)}, u32[]{:S(2)}) copy-start(bf16[1,1,1,4,8192]{4,3,2,1,0:T(4,128)(2,1)} %param.6) | copy-start | bytes 196612
  0.0 1.6 %copy-start.3 = (bf16[1,1,1,4,8192]{4,3,2,1,0:T(4,128)(2,1)S(1)}, bf16[1,1,1,4,8192]{4,3,2,1,0:T(4,128)(2,1)}, u32[]{:S(2)}) copy-start(bf16[1,1,1,4,8192]{4,3,2,1,0:T(4,128)(2,1)} %param.7) | copy-start | bytes 196612
  4.0 13.8 %all-to-all-start = ((bf16[4,7,8192]{2,1,0:T(8,128)(2,1)}), bf16[4,7,8192]{2,1,0:T(8,128)(2,1)S(1)}, u32[]{:S(2)}, u32[]{:S(2)}) async-start(bf16[4,7,8192]{2,1,0:T(8,128)(2,1)} %concatenate.21.rows_ref), calls=%async_computation | async-start | bytes 1048576 | tf_op jit(solution)/shard_map/all_to_all | solution.py:144
  8.3 6.0 %copy-start.4 = (s32[19]{0:T(128)S(1)}, s32[19]{0:T(128)}, u32[]{:S(2)}) copy-start(s32[19]{0:T(128)} %param.9) | copy-start | bytes 232
  17.8 0.8 %copy-start = (bf16[4,7,8192]{2,1,0:T(8,128)(2,1)}, bf16[4,7,8192]{2,1,0:T(8,128)(2,1)S(1)}, u32[]{:S(2)}) copy-start(bf16[4,7,8192]{2,1,0:T(8,128)(2,1)S(1)} %all-to-all-done.rows_ref) | copy-start | bytes 1376260
  35.4 9.1 %collective-permute-start = (f32[3,8,2,180]{3,1,0,2:T(8,128)S(1)}, f32[3,8,2,180]{3,1,0,2:T(8,128)S(1)}, u32[]{:S(2)}, u32[]{:S(2)}) collective-permute-start(f32[3,8,2,180]{3,1,0,2:T(8,128)S(1)} %fusion.6), channel_id=1, source_target_pairs={{0,1},{1,2},{2,3},{3,4},{4,5},{5,6},{6,7},{8,9},{9,10},{10,11},{11... | collective-permute-start | bytes 103688 | tf_op jit(solution)/shard_map/ppermute | solution.py:174
  37.3 7.2 %collective-permute-start.1 = (f32[3,8,2,180]{3,1,0,2:T(8,128)S(1)}, f32[3,8,2,180]{3,1,0,2:T(8,128)S(1)}, u32[]{:S(2)}, u32[]{:S(2)}) collective-permute-start(f32[3,8,2,180]{3,1,0,2:T(8,128)S(1)} %fusion.7), channel_id=1, source_target_pairs={{1,0},{2,1},{3,2},{4,3},{5,4},{6,5},{7,6},{9,8},{10,9},{11,10},{12... | collective-permute-start | bytes 103688 | tf_op jit(solution)/shard_map/ppermute | solution.py:175
  44.7 4.5 %collective-permute-start.2 = (f32[3,19,180]{2,0,1:T(4,128)S(1)}, f32[3,19,180]{2,0,1:T(4,128)S(1)}, u32[]{:S(2)}, u32[]{:S(2)}) collective-permute-start(f32[3,19,180]{2,0,1:T(4,128)S(1)} %fusion.27), channel_id=1, source_target_pairs={{0,8},{8,0},{16,24},{24,16},{32,40},{40,32},{48,56},{56,48},{1,9},... | collective-permute-start | bytes 123128 | tf_op jit(solution)/shard_map/ppermute | solution.py:109
  49.2 12.4 %collective-permute-start.3 = (f32[3,19,180]{2,0,1:T(4,128)S(1)}, f32[3,19,180]{2,0,1:T(4,128)S(1)}, u32[]{:S(2)}, u32[]{:S(2)}) collective-permute-start(f32[3,19,180]{2,0,1:T(4,128)S(1)} %add.121), channel_id=1, source_target_pairs={{0,16},{8,24},{16,0},{24,8},{32,48},{40,56},{48,32},{56,40},{1,17}... | collective-permute-start | bytes 123128 | tf_op jit(solution)/shard_map/ppermute | solution.py:109
  52.5 9.0 %collective-permute-start.4 = (f32[3,19,180]{2,0,1:T(4,128)S(1)}, f32[3,19,180]{2,0,1:T(4,128)S(1)}, u32[]{:S(2)}, u32[]{:S(2)}) collective-permute-start(f32[3,19,180]{2,0,1:T(4,128)S(1)} %add.121), channel_id=1, source_target_pairs={{0,32},{8,40},{16,48},{24,56},{32,0},{40,8},{48,16},{56,24},{1,33}... | collective-permute-start | bytes 123128 | tf_op jit(solution)/shard_map/ppermute | solution.py:109
  57.9 6.6 %collective-permute-start.5 = (f32[3,19,180]{2,0,1:T(4,128)S(1)}, f32[3,19,180]{2,0,1:T(4,128)S(1)}, u32[]{:S(2)}, u32[]{:S(2)}) collective-permute-start(f32[3,19,180]{2,0,1:T(4,128)S(1)} %add.121), channel_id=1, source_target_pairs={{0,48},{8,56},{16,32},{24,40},{32,16},{40,24},{48,0},{56,8},{1,49}... | collective-permute-start | bytes 123128 | tf_op jit(solution)/shard_map/ppermute | solution.py:109
  64.6 5.3 %collective-permute-start.6 = (f32[3,19,180]{2,0,1:T(4,128)S(1)}, f32[3,19,180]{2,0,1:T(4,128)S(1)}, u32[]{:S(2)}, u32[]{:S(2)}) collective-permute-start(f32[3,19,180]{2,0,1:T(4,128)S(1)} %add_add_fusion.1), channel_id=1, source_target_pairs={{0,64},{64,0},{128,192},{192,128},{1,65},{65,1},{129,193},{193,129... | collective-permute-start | bytes 123128 | tf_op jit(solution)/shard_map/ppermute | solution.py:109
  65.2 5.9 %collective-permute-start.7 = (f32[3,19,180]{2,0,1:T(4,128)S(1)}, f32[3,19,180]{2,0,1:T(4,128)S(1)}, u32[]{:S(2)}, u32[]{:S(2)}) collective-permute-start(f32[3,19,180]{2,0,1:T(4,128)S(1)} %add_add_fusion.1), channel_id=1, source_target_pairs={{0,128},{64,192},{128,0},{192,64},{1,129},{65,193},{129,1},{193,65... | collective-permute-start | bytes 123128 | tf_op jit(solution)/shard_map/ppermute | solution.py:109
  67.3 5.6 %collective-permute-start.8 = (f32[3,19,180]{2,0,1:T(4,128)S(1)}, f32[3,19,180]{2,0,1:T(4,128)S(1)}, u32[]{:S(2)}, u32[]{:S(2)}) collective-permute-start(f32[3,19,180]{2,0,1:T(4,128)S(1)} %add_add_fusion.1), channel_id=1, source_target_pairs={{0,192},{64,128},{128,64},{192,0},{1,193},{65,129},{129,65},{193,1... | collective-permute-start | bytes 123128 | tf_op jit(solution)/shard_map/ppermute | solution.py:109

commit v6 on v5

--- a/solution.py
+++ b/solution.py
@@ -11,14 +11,13 @@
 DRIFT = 256
 PAD_SLOT = 192
 CHUNK = 4096
-
-
-def row_kernels(kernel_reach):
-    spread = kernel_reach.astype(jnp.float32)[:, None, None]
-    places = lax.broadcasted_iota(jnp.int32, (PAD, PAD), 0)
-    others = lax.broadcasted_iota(jnp.int32, (PAD, PAD), 1)
-    distance = jnp.abs(places - others).astype(jnp.float32)[None]
-    return jnp.maximum(spread + 1.0 - distance, 0.0) / ((spread + 1.0) * (spread + 1.0))
+MAX_REACH = 4
+
+
+def row_taps(kernel_reach):
+    spread = kernel_reach.astype(jnp.float32)[:, None]
+    distance = jnp.abs(lax.broadcasted_iota(jnp.int32, (1, 2 * MAX_REACH + 1), 1) - MAX_REACH)
+    return jnp.maximum(spread + 1.0 - distance.astype(jnp.float32), 0.0) / ((spread + 1.0) * (spread + 1.0))
 
 
 def hist_kernel(cell_rows, first, order_ref, rows_ref, *rest):
@@ -154,8 +153,17 @@
     return finish(means, kernel_reach)
 
 
-def pad_smooth(field, kernels):
-    return jnp.einsum("...rq,rpq->...rp", field, kernels, precision=lax.Precision.HIGHEST)
+def pad_smooth(field, taps):
+    reach = taps.shape[-1] // 2
+    widths = [(0, 0)] * (field.ndim - 1) + [(reach, reach)]
+    padded = jnp.pad(field, widths)
+    total = field.shape[-1]
+    out = taps[:, reach : reach + 1] * field
+    for shift in range(-reach, reach + 1):
+        if shift != 0:
+            part = lax.slice_in_dim(padded, reach + shift, reach + shift + total, axis=field.ndim - 1)
+            out = out + taps[:, reach + shift : reach + shift + 1] * part
+    return out
 
 
 def row_smooth(rimmed, row_total, axis):
@@ -167,7 +175,7 @@
     count = lax.axis_size("sec")
     forward = [(i, i + 1) for i in range(count - 1)]
     backward = [(target, source) for source, target in forward]
-    kernels = row_kernels(kernel_reach)
+    kernels = row_taps(kernel_reach)
     row_total = kernels.shape[0]
     top = pad_smooth(means[:, :, row_total - 2 :], kernels[row_total - 2 :])
     bottom = pad_smooth(means[:, :, :2], kernels[:2])

time: 74.2 us -> 76.2 us (1.027)
  matrix products: 8.21 us -> 0 us
  other arithmetic: 3.14 us -> 7.81 us
  local copies, waits for them, and re-layouts: 5.9 us -> 8.83 us
  waiting for transfers between devices: 11.9 us -> 14.3 us
    unnamed x3 -> x0, matrix products: 4.7 us -> none
    add x2 -> x5, other arithmetic: 0.08 us -> 4.34 us  [the longest x4 4.34 us: pad_smooth(): out = out + taps[:, reach + shift:reach + shift + 1] * part]
    dot_general x1 -> x0, matrix products: 3.51 us -> none  [pad_smooth(): jnp.einsum('...rq,rpq->...rp', field, kernels, precision=lax.Precision.HI...]
    unnamed x12, local copies, waits for them, and re-layouts: 1.33 us -> 4.18 us
    ppermute x7, waiting for transfers between devices: 8.45 us -> 10.4 us  [scan_axis(): lax.ppermute(group, axis, [(i, i ^ m) for i in range(count)])]
    ppermute x1, waiting for transfers between devices: 0.01 us -> 1.27 us  [finish(): high = lax.ppermute(bottom, 'sec', backward)]
    all_to_all x1, waiting for transfers between devices: 3.42 us -> 2.62 us  [per_device(): incoming = lax.all_to_all(outgoing, 'tf', 0, 0, tiled=True)]
  transfers between devices with their start and end apart: 10 -> 10, of which waited for: 5 -> 6; matrix products, arithmetic and copies ran while one was open for 11% -> 6% of each run, Pallas kernels for 7% -> 7%
where the time goes in v6:
time: 76.2 us; the launch traced here: 75.7 us
  starting transfers between devices  25.5 us (33%)
  Pallas kernels  19.1 us (25%)
  waiting for transfers between devices  14.3 us (19%)
  local copies, waits for them, and re-layouts  8.83 us (12%)
  other arithmetic  7.81 us (10%)
    pallas_call x2, Pallas kernels, build_histogram(): pl.pallas_call(functools.partial(hist_kernel, cell_rows, first), out_shap...  19.1 us
    ppermute x7, starting transfers between devices, scan_axis(): lax.ppermute(group, axis, [(i, i ^ m) for i in range(count)])  15.6 us
    ppermute x7, waiting for transfers between devices, scan_axis(): lax.ppermute(group, axis, [(i, i ^ m) for i in range(count)])  10.4 us
    add x4, other arithmetic, pad_smooth(): out = out + taps[:, reach + shift:reach + shift + 1] * part  4.34 us
    all_to_all x1, starting transfers between devices, per_device(): incoming = lax.all_to_all(outgoing, 'tf', 0, 0, tiled=True)  4.29 us
    unnamed x12, local copies, waits for them, and re-layouts  4.18 us
    ppermute x1, starting transfers between devices, finish(): high = lax.ppermute(bottom, 'sec', backward)  3.64 us
    all_to_all x1, waiting for transfers between devices, per_device(): incoming = lax.all_to_all(outgoing, 'tf', 0, 0, tiled=True)  2.62 us
  transfers between devices with their start and end apart: 10, of which 6 were waited for; matrix products, arithmetic and copies ran while one was open for 6% of the time, Pallas kernels for 7%

profile of v6, /device:TPU:8, one launch (start us, length us, event | category | flops | bytes accessed | tf_op | source)
XLA Modules:
  0.0 75.7 jit_solution(1036453317446038352)
XLA Ops:
  0.0 1.1 %fusion.34 = (bf16[4,1,8192]{2,0,1:T(4,128)(2,1)S(1)}, s32[1,1,1,1,4,8192]{5,4,3,2,1,0:T(4,128)S(1)}, s32[1,1,1,1,4,8192]{5,4,3,2,1,0:T(4,128)S(1)}) fusion(s32[3,1,1,1,4,8192]{5,4,3,2,1,0:T(4,128)} %param.8, s32[]{:T(128)S(6)} %mul.402), kind=kLoop, calls=%fused_computation.55 | loop fusion | flops 65536 | bytes 720900 | tf_op jit(solution)/shard_map/convert_element_type | solution.py:136
  1.2 0.8 %copy-done.1 = bf16[3,1,1,1,4,8192]{5,4,3,2,1,0:T(4,128)(2,1)S(1)} copy-done((bf16[3,1,1,1,4,8192]{5,4,3,2,1,0:T(4,128)(2,1)S(1)}, bf16[3,1,1,1,4,8192]{5,4,3,2,1,0:T(4,128)(2,1)}, u32[]{:S(2)}) %copy-start.1) | copy-done | bytes 196632
  3.0 0.7 copy-done.3
  4.1 2.0 %concatenate.21.rows_ref = bf16[4,7,8192]{2,1,0:T(8,128)(2,1)} concatenate(bf16[4,1,8192]{2,1,0:T(2,128)(2,1)S(1)} %fusion.22, bf16[4,1,8192]{2,1,0:T(2,128)(2,1)S(1)} %copy.31, bf16[4,3,8192]{2,1,0:T(4,128)(2,1)S(1)} %bitcast.89, bf16[4,1,8192]{2,1,0:T(2,128)(2,1)S(1)} %copy.32, bf16[4,1,8192]{2,1,0:T(2,128)(2,1)S(1)} %copy.33), dimensions={1} | concatenate | bytes 917504 | tf_op jit(solution)/shard_map/concatenate | solution.py:133
  6.1 4.3 %all-to-all-start = ((bf16[4,7,8192]{2,1,0:T(8,128)(2,1)}), bf16[4,7,8192]{2,1,0:T(8,128)(2,1)S(1)}, u32[]{:S(2)}, u32[]{:S(2)}) async-start(bf16[4,7,8192]{2,1,0:T(8,128)(2,1)} %concatenate.21.rows_ref), calls=%async_computation | async-start | bytes 1048576 | tf_op jit(solution)/shard_map/all_to_all | solution.py:143
  11.2 5.4 %shard_map.55.rest_0_ = f32[768,160]{1,0:T(8,128)} custom-call(s32[1]{0:T(128)} %bitcast.8.order_ref, bf16[4,7,8192]{2,1,0:T(8,128)(2,1)} %concatenate.21.rows_ref), custom_call_target="tpu_custom_call" | custom-call | flops 2013265920 | bytes 1097728 | tf_op jit(solution)/shard_map/pallas_call | solution.py:80
  17.3 2.6 %all-to-all-done.rows_ref = bf16[4,7,8192]{2,1,0:T(8,128)(2,1)S(1)} async-done(((bf16[4,7,8192]{2,1,0:T(8,128)(2,1)}), bf16[4,7,8192]{2,1,0:T(8,128)(2,1)S(1)}, u32[]{:S(2)}, u32[]{:S(2)}) %all-to-all-start) | async-done | bytes 458784 | tf_op jit(solution)/shard_map/all_to_all | solution.py:143
  19.9 0.8 %copy-done = bf16[4,7,8192]{2,1,0:T(8,128)(2,1)} copy-done((bf16[4,7,8192]{2,1,0:T(8,128)(2,1)}, bf16[4,7,8192]{2,1,0:T(8,128)(2,1)S(1)}, u32[]{:S(2)}) %copy-start) | copy-done | bytes 458776
  20.7 13.7 %shard_map.56 = f32[768,160]{1,0:T(8,128)} custom-call(s32[3]{0:T(128)} %and_select_fusion.order_ref, bf16[4,7,8192]{2,1,0:T(8,128)(2,1)} %copy-done, f32[768,160]{1,0:T(8,128)} %shard_map.55.rest_0_), custom_call_target="tpu_custom_call", output_to_operand_aliasing={{}: (2, {})} | custom-call | flops 6039797760 | bytes 1327104 | tf_op jit(solution)/shard_map/pallas_call | solution.py:80
  34.4 1.2 %slice.343 = f32[152,4,180]{0,2,1:T(8,128)S(1)} slice(f32[160,4,192]{0,2,1:T(8,128)} %bitcast.90), slice={[0:152], [0:4], [0:180]} | slice | bytes 875520 | tf_op jit(solution)/shard_map/slice | solution.py:149
  36.8 1.9 %collective-permute-start = (f32[3,8,2,180]{3,0,2,1:T(4,128)S(1)}, f32[3,8,2,180]{3,0,2,1:T(4,128)S(1)}, u32[]{:S(2)}, u32[]{:S(2)}) collective-permute-start(f32[3,8,2,180]{3,0,2,1:T(4,128)S(1)} %multiply_add_fusion.3), channel_id=1, source_target_pairs={{0,1},{1,2},{2,3},{3,4},{4,5},{5,6},{6,7},{8,9},{9,10},{10,11},{11... | collective-permute-start | bytes 103688 | tf_op jit(solution)/shard_map/ppermute | solution.py:182
  39.1 3.6 %collective-permute-start.1 = (f32[3,8,2,180]{3,0,2,1:T(4,128)S(1)}, f32[3,8,2,180]{3,0,2,1:T(4,128)S(1)}, u32[]{:S(2)}, u32[]{:S(2)}) collective-permute-start(f32[3,8,2,180]{3,0,2,1:T(4,128)S(1)} %multiply_add_fusion.2), channel_id=1, source_target_pairs={{1,0},{2,1},{3,2},{4,3},{5,4},{6,5},{7,6},{9,8},{10,9},{11,10},{12... | collective-permute-start | bytes 103688 | tf_op jit(solution)/shard_map/ppermute | solution.py:183
  43.4 1.3 %collective-permute-done.1 = f32[3,8,2,180]{3,0,2,1:T(4,128)S(1)} collective-permute-done((f32[3,8,2,180]{3,0,2,1:T(4,128)S(1)}, f32[3,8,2,180]{3,0,2,1:T(4,128)S(1)}, u32[]{:S(2)}, u32[]{:S(2)}) %collective-permute-start.1) | collective-permute-done | bytes 34592 | tf_op jit(solution)/shard_map/ppermute | solution.py:183
  44.7 2.0 %collective-permute-start.2 = (f32[3,19,180]{2,0,1:T(4,128)S(1)}, f32[3,19,180]{2,0,1:T(4,128)S(1)}, u32[]{:S(2)}, u32[]{:S(2)}) collective-permute-start(f32[3,19,180]{2,0,1:T(4,128)S(1)} %fusion.29), channel_id=1, source_target_pairs={{0,8},{8,0},{16,24},{24,16},{32,40},{40,32},{48,56},{56,48},{1,9},... | collective-permute-start | bytes 123128 | tf_op jit(solution)/shard_map/ppermute | solution.py:108
  46.7 2.5 %collective-permute-done.2 = f32[3,19,180]{2,0,1:T(4,128)S(1)} collective-permute-done((f32[3,19,180]{2,0,1:T(4,128)S(1)}, f32[3,19,180]{2,0,1:T(4,128)S(1)}, u32[]{:S(2)}, u32[]{:S(2)}) %collective-permute-start.2) | collective-permute-done | bytes 41072 | tf_op jit(solution)/shard_map/ppermute | solution.py:108
  49.2 3.4 %collective-permute-start.3 = (f32[3,19,180]{2,0,1:T(4,128)S(1)}, f32[3,19,180]{2,0,1:T(4,128)S(1)}, u32[]{:S(2)}, u32[]{:S(2)}) collective-permute-start(f32[3,19,180]{2,0,1:T(4,128)S(1)} %add.255), channel_id=1, source_target_pairs={{0,16},{8,24},{16,0},{24,8},{32,48},{40,56},{48,32},{56,40},{1,17}... | collective-permute-start | bytes 123128 | tf_op jit(solution)/shard_map/ppermute | solution.py:108
  52.6 5.5 %collective-permute-start.4 = (f32[3,19,180]{2,0,1:T(4,128)S(1)}, f32[3,19,180]{2,0,1:T(4,128)S(1)}, u32[]{:S(2)}, u32[]{:S(2)}) collective-permute-start(f32[3,19,180]{2,0,1:T(4,128)S(1)} %add.255), channel_id=1, source_target_pairs={{0,32},{8,40},{16,48},{24,56},{32,0},{40,8},{48,16},{56,24},{1,33}... | collective-permute-start | bytes 123128 | tf_op jit(solution)/shard_map/ppermute | solution.py:108
  58.0 4.6 %collective-permute-done.4 = f32[3,19,180]{2,0,1:T(4,128)S(1)} collective-permute-done((f32[3,19,180]{2,0,1:T(4,128)S(1)}, f32[3,19,180]{2,0,1:T(4,128)S(1)}, u32[]{:S(2)}, u32[]{:S(2)}) %collective-permute-start.4) | collective-permute-done | bytes 41072 | tf_op jit(solution)/shard_map/ppermute | solution.py:108
  62.7 2.8 %collective-permute-done.5 = f32[3,19,180]{2,0,1:T(4,128)S(1)} collective-permute-done((f32[3,19,180]{2,0,1:T(4,128)S(1)}, f32[3,19,180]{2,0,1:T(4,128)S(1)}, u32[]{:S(2)}, u32[]{:S(2)}) %collective-permute-start.5) | collective-permute-done | bytes 41072 | tf_op jit(solution)/shard_map/ppermute | solution.py:108
  66.1 2.1 %collective-permute-start.7 = (f32[3,19,180]{2,0,1:T(4,128)S(1)}, f32[3,19,180]{2,0,1:T(4,128)S(1)}, u32[]{:S(2)}, u32[]{:S(2)}) collective-permute-start(f32[3,19,180]{2,0,1:T(4,128)S(1)} %add_add_fusion.1), channel_id=1, source_target_pairs={{0,128},{64,192},{128,0},{192,64},{1,129},{65,193},{129,1},{193,65... | collective-permute-start | bytes 123128 | tf_op jit(solution)/shard_map/ppermute | solution.py:108
  68.2 2.1 %collective-permute-start.8 = (f32[3,19,180]{2,0,1:T(4,128)S(1)}, f32[3,19,180]{2,0,1:T(4,128)S(1)}, u32[]{:S(2)}, u32[]{:S(2)}) collective-permute-start(f32[3,19,180]{2,0,1:T(4,128)S(1)} %add_add_fusion.1), channel_id=1, source_target_pairs={{0,192},{64,128},{128,64},{192,0},{1,193},{65,129},{129,65},{193,1... | collective-permute-start | bytes 123128 | tf_op jit(solution)/shard_map/ppermute | solution.py:108
  70.2 3.1 %multiply_add_fusion = f32[3,8,19,180]{3,0,2,1:T(4,128)S(1)} fusion(f32[3,8,19,180]{3,0,2,1:T(4,128)S(1)} %get-tuple-element.6, f32[19]{0:T(128)S(1)} %get-tuple-element.31, f32[19]{0:T(128)S(1)} %get-tuple-element.32, f32[19]{0:T(128)S(1)} %get-tuple-element.33, f32[19]{0:T(128)S(1)} %get-tuple-element.34, f32[19]{0:T(128)S(1)} %get-tuple-element.35, ...), kind=kLoop, calls=%fused_computation.21 | loop fusion | flops 1395360 | bytes 657324 | tf_op jit(solution)/shard_map/add | solution.py:165
  74.0 0.9 %broadcast_add_fusion = f32[3,8,19,180]{3,0,2,1:T(4,128)S(1)} fusion(f32[3,19,180]{2,0,1:T(4,128)S(1)} %add_add_fusion, f32[3,8,19,180]{3,0,2,1:T(4,128)S(1)} %multiply_add_fusion, f32[3,8,2,180]{3,0,2,1:T(4,128)S(1)} %collective-permute-done.1, f32[3,8,2,180]{3,0,2,1:T(4,128)S(1)} %collective-permute-done), kind=kOutput, calls=%fused_computation.25 | output fusion | flops 1641600 | bytes 766800 | tf_op jit(solution)/shard_map/jit(cumsum)/reduce_window_sum | solution.py:189
  74.9 0.9 %copy.37 = f32[3,8,19,180]{3,1,2,0:T(8,128)} copy(f32[3,8,19,180]{3,0,2,1:T(4,128)S(1)} %broadcast_add_fusion) | data formatting | bytes 656640 | tf_op jit(solution)/shard_map/add | solution.py:189
  (41 shorter events, 6.4 us)
Async XLA Ops:
  1.1 0.9 %copy-start.1 = (bf16[3,1,1,1,4,8192]{5,4,3,2,1,0:T(4,128)(2,1)S(1)}, bf16[3,1,1,1,4,8192]{5,4,3,2,1,0:T(4,128)(2,1)}, u32[]{:S(2)}) copy-start(bf16[3,1,1,1,4,8192]{5,4,3,2,1,0:T(4,128)(2,1)} %param.5) | copy-start | bytes 589828
  2.0 0.8 %copy-start.2 = (bf16[1,1,1,4,8192]{4,3,2,1,0:T(4,128)(2,1)S(1)}, bf16[1,1,1,4,8192]{4,3,2,1,0:T(4,128)(2,1)}, u32[]{:S(2)}) copy-start(bf16[1,1,1,4,8192]{4,3,2,1,0:T(4,128)(2,1)} %param.6) | copy-start | bytes 196612
  2.9 0.8 %copy-start.3 = (bf16[1,1,1,4,8192]{4,3,2,1,0:T(4,128)(2,1)S(1)}, bf16[1,1,1,4,8192]{4,3,2,1,0:T(4,128)(2,1)}, u32[]{:S(2)}) copy-start(bf16[1,1,1,4,8192]{4,3,2,1,0:T(4,128)(2,1)} %param.7) | copy-start | bytes 196612
  6.1 13.8 %all-to-all-start = ((bf16[4,7,8192]{2,1,0:T(8,128)(2,1)}), bf16[4,7,8192]{2,1,0:T(8,128)(2,1)S(1)}, u32[]{:S(2)}, u32[]{:S(2)}) async-start(bf16[4,7,8192]{2,1,0:T(8,128)(2,1)} %concatenate.21.rows_ref), calls=%async_computation | async-start | bytes 1048576 | tf_op jit(solution)/shard_map/all_to_all | solution.py:143
  10.4 0.7 copy-start.4
  19.9 0.8 %copy-start = (bf16[4,7,8192]{2,1,0:T(8,128)(2,1)}, bf16[4,7,8192]{2,1,0:T(8,128)(2,1)S(1)}, u32[]{:S(2)}) copy-start(bf16[4,7,8192]{2,1,0:T(8,128)(2,1)S(1)} %all-to-all-done.rows_ref) | copy-start | bytes 1376260
  36.8 6.5 %collective-permute-start = (f32[3,8,2,180]{3,0,2,1:T(4,128)S(1)}, f32[3,8,2,180]{3,0,2,1:T(4,128)S(1)}, u32[]{:S(2)}, u32[]{:S(2)}) collective-permute-start(f32[3,8,2,180]{3,0,2,1:T(4,128)S(1)} %multiply_add_fusion.3), channel_id=1, source_target_pairs={{0,1},{1,2},{2,3},{3,4},{4,5},{5,6},{6,7},{8,9},{9,10},{10,11},{11... | collective-permute-start | bytes 103688 | tf_op jit(solution)/shard_map/ppermute | solution.py:182
  39.1 5.5 %collective-permute-start.1 = (f32[3,8,2,180]{3,0,2,1:T(4,128)S(1)}, f32[3,8,2,180]{3,0,2,1:T(4,128)S(1)}, u32[]{:S(2)}, u32[]{:S(2)}) collective-permute-start(f32[3,8,2,180]{3,0,2,1:T(4,128)S(1)} %multiply_add_fusion.2), channel_id=1, source_target_pairs={{1,0},{2,1},{3,2},{4,3},{5,4},{6,5},{7,6},{9,8},{10,9},{11,10},{12... | collective-permute-start | bytes 103688 | tf_op jit(solution)/shard_map/ppermute | solution.py:183
  44.7 4.5 %collective-permute-start.2 = (f32[3,19,180]{2,0,1:T(4,128)S(1)}, f32[3,19,180]{2,0,1:T(4,128)S(1)}, u32[]{:S(2)}, u32[]{:S(2)}) collective-permute-start(f32[3,19,180]{2,0,1:T(4,128)S(1)} %fusion.29), channel_id=1, source_target_pairs={{0,8},{8,0},{16,24},{24,16},{32,40},{40,32},{48,56},{56,48},{1,9},... | collective-permute-start | bytes 123128 | tf_op jit(solution)/shard_map/ppermute | solution.py:108
  49.2 8.8 %collective-permute-start.3 = (f32[3,19,180]{2,0,1:T(4,128)S(1)}, f32[3,19,180]{2,0,1:T(4,128)S(1)}, u32[]{:S(2)}, u32[]{:S(2)}) collective-permute-start(f32[3,19,180]{2,0,1:T(4,128)S(1)} %add.255), channel_id=1, source_target_pairs={{0,16},{8,24},{16,0},{24,8},{32,48},{40,56},{48,32},{56,40},{1,17}... | collective-permute-start | bytes 123128 | tf_op jit(solution)/shard_map/ppermute | solution.py:108
  52.6 10.1 %collective-permute-start.4 = (f32[3,19,180]{2,0,1:T(4,128)S(1)}, f32[3,19,180]{2,0,1:T(4,128)S(1)}, u32[]{:S(2)}, u32[]{:S(2)}) collective-permute-start(f32[3,19,180]{2,0,1:T(4,128)S(1)} %add.255), channel_id=1, source_target_pairs={{0,32},{8,40},{16,48},{24,56},{32,0},{40,8},{48,16},{56,24},{1,33}... | collective-permute-start | bytes 123128 | tf_op jit(solution)/shard_map/ppermute | solution.py:108
  58.0 7.4 %collective-permute-start.5 = (f32[3,19,180]{2,0,1:T(4,128)S(1)}, f32[3,19,180]{2,0,1:T(4,128)S(1)}, u32[]{:S(2)}, u32[]{:S(2)}) collective-permute-start(f32[3,19,180]{2,0,1:T(4,128)S(1)} %add.255), channel_id=1, source_target_pairs={{0,48},{8,56},{16,32},{24,40},{32,16},{40,24},{48,0},{56,8},{1,49}... | collective-permute-start | bytes 123128 | tf_op jit(solution)/shard_map/ppermute | solution.py:108
  65.5 7.8 %collective-permute-start.6 = (f32[3,19,180]{2,0,1:T(4,128)S(1)}, f32[3,19,180]{2,0,1:T(4,128)S(1)}, u32[]{:S(2)}, u32[]{:S(2)}) collective-permute-start(f32[3,19,180]{2,0,1:T(4,128)S(1)} %add_add_fusion.1), channel_id=1, source_target_pairs={{0,64},{64,0},{128,192},{192,128},{1,65},{65,1},{129,193},{193,129... | collective-permute-start | bytes 123128 | tf_op jit(solution)/shard_map/ppermute | solution.py:108
  66.1 7.2 %collective-permute-start.7 = (f32[3,19,180]{2,0,1:T(4,128)S(1)}, f32[3,19,180]{2,0,1:T(4,128)S(1)}, u32[]{:S(2)}, u32[]{:S(2)}) collective-permute-start(f32[3,19,180]{2,0,1:T(4,128)S(1)} %add_add_fusion.1), channel_id=1, source_target_pairs={{0,128},{64,192},{128,0},{192,64},{1,129},{65,193},{129,1},{193,65... | collective-permute-start | bytes 123128 | tf_op jit(solution)/shard_map/ppermute | solution.py:108
  68.2 5.7 %collective-permute-start.8 = (f32[3,19,180]{2,0,1:T(4,128)S(1)}, f32[3,19,180]{2,0,1:T(4,128)S(1)}, u32[]{:S(2)}, u32[]{:S(2)}) collective-permute-start(f32[3,19,180]{2,0,1:T(4,128)S(1)} %add_add_fusion.1), channel_id=1, source_target_pairs={{0,192},{64,128},{128,64},{192,0},{1,193},{65,129},{129,65},{193,1... | collective-permute-start | bytes 123128 | tf_op jit(solution)/shard_map/ppermute | solution.py:108
